TPU v7x, 32 devices: a whole 2x2x4 slice. The times are simulated.
32 devices in a mesh: groups: 2 (over x), tile: 16 (over z, y, core).
Axes of the slice: x: 2, y: 2, z: 4, core: 2. Of those that a mesh axis runs over, the one named last changes fastest.
Arguments:
- hidden_in: bfloat16 [2048, 4096], P('groups', 'tile'), parts along dimension 0, may hold values from -6 to 6
- w_up: bfloat16 [16, 1024, 4096], P('tile'), may hold values from -0.09375 to 0.09375
- w_down: bfloat16 [16, 4096, 1024], P('tile'), may hold values from -0.046875 to 0.046875
- out_grad: bfloat16 [2048, 4096], P('groups', 'tile'), parts along dimension 0, may hold values from -6 to 6
Outputs:
- block_out: bfloat16 [2048, 4096], P('groups', 'tile'), parts along dimension 0
- input_grad: bfloat16 [2048, 4096], P('groups', 'tile'), parts along dimension 0
- grad_up: bfloat16 [16, 2048, 4096], P('tile', 'groups'), parts along dimension 1
- grad_down: bfloat16 [16, 8192, 1024], P('tile', 'groups'), parts along dimension 1
There are 2 independent parts, one for each index of `groups`. A program takes and returns all parts, laid end to end along the dimension named above; an argument that names none is the same for every part. Nothing has to cross between parts.
All inputs are finite; a program needn't handle non-finite values.
Results may differ from a plain program's by a relative error of at most 0.0062.
Values may be sent and summed in bfloat16 or wider, within the bound.
No kernel may reach another device: no remote copies, remote signals or barrier semaphores. Data moves between devices by JAX's collectives and lax.ppermute only.
A program may use at most 256 MiB of HBM per device.

v0:
```python
import jax
import jax.numpy as jnp
import numpy as np
from jax import lax
from jax.sharding import Mesh
from jax.sharding import PartitionSpec as P


root_half = 0.7071067811865476
inv_root_tau = 0.3989422804014327


def gelu_value(values):
    return 0.5 * values * (1.0 + lax.erf(values * root_half))


def gelu_slope(values):
    return (
        0.5 * (1.0 + lax.erf(values * root_half))
        + values * jnp.exp(-0.5 * values * values) * inv_root_tau
    )


class LineReduce:
    def __init__(self, terms):
        self.count = lax.axis_size("r")
        self.pos = lax.axis_index("r")
        rows = terms.shape[0] // self.count
        self.shares = terms.reshape(self.count, rows, terms.shape[1])
        self.up_in = jnp.zeros((rows, terms.shape[1]), jnp.float32)
        self.down_in = jnp.zeros((rows, terms.shape[1]), jnp.float32)

    def senders(self, step):
        return (0, step), (self.count - 1 - step, self.count - 1)

    def payload(self, step):
        last = self.count - 1
        up_block = jnp.clip(last - step + self.pos, 0, last)
        down_block = jnp.clip(self.pos + step - last, 0, last)
        up = self.up_in + lax.dynamic_index_in_dim(self.shares, up_block, 0, keepdims=False)
        down = self.down_in + lax.dynamic_index_in_dim(self.shares, down_block, 0, keepdims=False)
        return up.astype(jnp.bfloat16), down.astype(jnp.bfloat16)

    def receive(self, step, up, down):
        self.up_in = up.astype(jnp.float32)
        self.down_in = down.astype(jnp.float32)

    def result(self):
        own = lax.dynamic_index_in_dim(self.shares, self.pos, 0, keepdims=False)
        return self.up_in + own.astype(jnp.float32) + self.down_in


class LineGather:
    def __init__(self, block):
        self.count = lax.axis_size("r")
        self.pos = lax.axis_index("r")
        self.block = block
        self.up_cur = self.down_cur = block
        self.ups, self.downs = [], []

    def senders(self, step):
        return (step, self.count - 2), (1, self.count - 1 - step)

    def payload(self, step):
        return self.up_cur, self.down_cur

    def receive(self, step, up, down):
        self.up_cur, self.down_cur = up, down
        self.ups.append(up)
        self.downs.append(down)

    def result(self):
        count = self.count
        pieces = [self.block]
        for m in range(1, count):
            pieces.append(self.downs[m - 1] + self.ups[count - 1 - m])
        return jnp.concatenate(pieces, axis=0)


def rotate_rows(values, shift):
    doubled = jnp.concatenate([values, values], axis=0)
    return lax.dynamic_slice_in_dim(doubled, shift, values.shape[0], axis=0)


def run_slot(entries):
    pos = lax.axis_index("r")
    loads = [entry.payload(step) for entry, step in entries]
    ranges = [entry.senders(step) for entry, step in entries]
    received = []
    for direction, shift in ((0, 1), (1, -1)):
        combined = None
        pairs = []
        for load, rng in zip(loads, ranges):
            lo, hi = rng[direction]
            if lo > hi:
                continue
            pairs += [(i, i + shift) for i in range(lo, hi + 1)]
            mine = (pos >= lo) & (pos <= hi)
            combined = load[direction] if combined is None else jnp.where(mine, load[direction], combined)
        if combined is None:
            received.append(None)
            continue
        received.append(lax.ppermute(combined, "r", pairs))
    for (entry, step), load, rng in zip(entries, loads, ranges):
        parts = []
        for direction, shift in ((0, 1), (1, -1)):
            lo, hi = rng[direction]
            got = received[direction]
            if got is None or lo > hi:
                parts.append(jnp.zeros_like(load[direction]))
                continue
            mine = (pos >= lo + shift) & (pos <= hi + shift)
            parts.append(jnp.where(mine, got, jnp.zeros_like(got)))
        entry.receive(step, *parts)


def on_device(hidden_in, w_up, w_down, out_grad):
    up_tile = w_up[0]
    down_tile = w_down[0]
    count = lax.axis_size("r")
    x_rows = lax.all_gather(hidden_in, "p", axis=1, tiled=True)
    up_terms = jnp.dot(x_rows, up_tile, preferred_element_type=jnp.float32).astype(jnp.bfloat16)
    grad_rows = lax.all_gather(out_grad, "p", axis=1, tiled=True)
    grad_terms = lax.dot_general(
        grad_rows, down_tile, (((1,), (1,)), ((), ())), preferred_element_type=jnp.float32
    ).astype(jnp.bfloat16)

    up_sum = LineReduce(up_terms)
    if count > 1:
        run_slot([(up_sum, 0)])
        up_sum.up_in, up_sum.down_in, grad_terms = lax.optimization_barrier(
            (up_sum.up_in, up_sum.down_in, grad_terms)
        )
    grad_sum = LineReduce(grad_terms)
    for step in range(1, count - 1):
        run_slot([(up_sum, step)])
    preact = up_sum.result()
    act_gather = LineGather(gelu_value(preact).astype(jnp.bfloat16))
    if count > 1:
        run_slot([(act_gather, 0)])
    for step in range(1, count - 1):
        run_slot([(act_gather, step), (grad_sum, step - 1)])
    tokens = x_rows.shape[0]
    turn = lax.axis_index("r") * (tokens // count)
    grad_turned = rotate_rows(grad_rows, turn)
    activation = act_gather.result()
    out_part = jnp.dot(activation, down_tile, preferred_element_type=jnp.float32)
    out_sum = lax.psum_scatter(out_part, "p", scatter_dimension=1, tiled=True)
    grad_down = lax.dot_general(
        activation, grad_turned, (((0,), (0,)), ((), ())), preferred_element_type=jnp.float32
    ).astype(jnp.bfloat16)
    if count > 1:
        run_slot([(grad_sum, count - 2)])
    act_grad = grad_sum.result()
    pre_gather = LineGather((act_grad * gelu_slope(preact)).astype(jnp.bfloat16))
    for step in range(count - 1):
        run_slot([(pre_gather, step)])
        if step == min(1, count - 2):
            pre_gather.up_cur, pre_gather.down_cur, out_sum, grad_down = lax.optimization_barrier(
                (pre_gather.up_cur, pre_gather.down_cur, out_sum, grad_down)
            )
            pre_gather.ups[-1], pre_gather.downs[-1] = pre_gather.up_cur, pre_gather.down_cur
    pre_grad = pre_gather.result()
    block_out = (
        hidden_in.astype(jnp.float32) + rotate_rows(out_sum, tokens - turn)
    ).astype(jnp.bfloat16)
    grad_up = lax.dot_general(
        rotate_rows(x_rows, turn), pre_grad, (((0,), (0,)), ((), ())), preferred_element_type=jnp.float32
    ).astype(jnp.bfloat16)
    pos = lax.axis_index("r")
    pieces = [(pre_gather.block, pos)]
    for step in range(count - 1):
        up_piece, down_piece = pre_gather.ups[step], pre_gather.downs[step]
        up_at, down_at = pos - 1 - step, pos + 1 + step
        if 2 * step + 3 <= count:
            pieces += [(up_piece, up_at), (down_piece, down_at)]
        else:
            pieces.append((up_piece + down_piece, jnp.where(up_at >= 0, up_at, down_at)))
    sums = []
    for piece, at in pieces:
        back_rows = lax.dot_general(
            piece, up_tile, (((1,), (1,)), ((), ())), preferred_element_type=jnp.float32
        )
        sums.append((lax.psum_scatter(back_rows, "p", scatter_dimension=1, tiled=True), at))
    rows = pre_gather.block.shape[0]
    grad_blocks = out_grad.reshape(count, rows, out_grad.shape[1]).astype(jnp.float32)
    input_rows = []
    for k in range(count):
        total = grad_blocks[k]
        for value, at in sums:
            total = total + jnp.where(at == k, value, jnp.zeros_like(value))
        input_rows.append(total)
    input_grad = jnp.concatenate(input_rows, axis=0).astype(jnp.bfloat16)
    return (block_out, input_grad, grad_up[None], grad_down[None])


def solution(mesh):
    groups = mesh.shape["groups"]
    tile = mesh.shape["tile"]

    def run(hidden_in, w_up, w_down, out_grad):
        width_blocks = hidden_in.shape[1] // w_up.shape[1]
        grid = Mesh(
            np.asarray(mesh.devices).reshape(groups, width_blocks, tile // width_blocks),
            ("groups", "r", "p"),
        )
        cells = ("r", "p")
        return jax.shard_map(
            on_device,
            mesh=grid,
            in_specs=(
                P("groups", cells),
                P(cells, None, None),
                P(cells, None, None),
                P("groups", cells),
            ),
            out_specs=(
                P("groups", cells),
                P("groups", cells),
                P(cells, "groups", None),
                P(cells, "groups", None),
            ),
            check_vma=False,
        )(hidden_in, w_up, w_down, out_grad)

    return run
```

profile of v0, /device:TPU:0, one launch (start us, length us, event | category | flops | bytes accessed | tf_op | source)
XLA Modules:
  0.0 633.4 jit_solution(13595988755970181108)
XLA Ops:
  8.7 26.4 %all-gather.3.cloned.1.call-done = bf16[1024,1024]{1,0:T(8,128)(2,1)} async-done(((bf16[1024,256]{1,0:T(8,128)(2,1)}), bf16[1024,1024]{1,0:T(8,128)(2,1)}) %all-gather.3.cloned.1.call-update) | async-done | bytes 2097168 | tf_op jit(solution)/shard_map/all_gather | solution.py:121
  35.1 12.8 %fusion.24 = bf16[1024,4096]{1,0:T(8,128)(2,1)S(1)} fusion(bf16[1024,1024]{1,0:T(8,128)(2,1)} %all-gather.3.cloned.1.call-done, bf16[1,1024,4096]{2,1,0:T(8,128)(2,1)} %param.5), kind=kOutput, calls=%fused_computation.26 | convolution fusion | flops 8594128896 | bytes 18874368 | tf_op jit(solution)/shard_map/dot_general | solution.py:122
  49.9 2.0 copy-done
  53.9 4.7 collective-permute-start
  59.6 14.8 %fusion.27 = bf16[1024,4096]{1,0:T(8,128)(2,1)} fusion(bf16[1024,1024]{1,0:T(8,128)(2,1)} %all-gather.5.cloned.1.call-done, bf16[1,4096,1024]{2,1,0:T(8,128)(2,1)} %param.6), kind=kOutput, calls=%fused_computation.27 | convolution fusion | flops 8594128896 | bytes 18874368 | tf_op jit(solution)/shard_map/dot_general | solution.py:124
  74.7 27.9 %collective-permute-done = bf16[256,4096]{1,0:T(8,128)(2,1)} collective-permute-done((bf16[256,4096]{1,0:T(8,128)(2,1)S(1)}, bf16[256,4096]{1,0:T(8,128)(2,1)}, u32[]{:S(2)}, u32[]{:S(2)}) %collective-permute-start) | collective-permute-done | bytes 2097184 | tf_op jit(solution)/shard_map/ppermute | solution.py:103
  102.9 3.6 fusion.47
  106.4 6.2 collective-permute-start.2
  112.7 2.0 collective-permute-start.4
  114.7 42.6 %collective-permute-done.2 = bf16[256,4096]{1,0:T(8,128)(2,1)S(1)} collective-permute-done((bf16[256,4096]{1,0:T(8,128)(2,1)}, bf16[256,4096]{1,0:T(8,128)(2,1)S(1)}, u32[]{:S(2)}, u32[]{:S(2)}) %collective-permute-start.2) | collective-permute-done | bytes 2097184 | tf_op jit(solution)/shard_map/ppermute | solution.py:103
  157.3 6.0 fusion.46
  163.3 9.1 %collective-permute-start.3 = (bf16[256,4096]{1,0:T(8,128)(2,1)}, bf16[256,4096]{1,0:T(8,128)(2,1)S(1)}, u32[]{:S(2)}, u32[]{:S(2)}) collective-permute-start(bf16[256,4096]{1,0:T(8,128)(2,1)} %get-tuple-element.24), channel_id=1, source_target_pairs={{0,4},{4,8},{8,12},{1,5},{5,9},{9,13},{2,6},{6,10},{10,14},{3,7},{... | collective-permute-start | bytes 6291464 | tf_op jit(solution)/shard_map/ppermute | solution.py:103
  173.8 42.2 %collective-permute-done.3 = bf16[256,4096]{1,0:T(8,128)(2,1)S(1)} collective-permute-done((bf16[256,4096]{1,0:T(8,128)(2,1)}, bf16[256,4096]{1,0:T(8,128)(2,1)S(1)}, u32[]{:S(2)}, u32[]{:S(2)}) %collective-permute-start.3) | collective-permute-done | bytes 2097184 | tf_op jit(solution)/shard_map/ppermute | solution.py:103
  215.9 4.2 collective-permute-done.5
  220.2 4.3 multiply_convert_fusion
  225.8 4.7 collective-permute-start.6
  230.5 40.8 %collective-permute-done.10 = bf16[256,4096]{1,0:T(8,128)(2,1)} collective-permute-done((bf16[256,4096]{1,0:T(8,128)(2,1)}, bf16[256,4096]{1,0:T(8,128)(2,1)}, u32[]{:S(2)}, u32[]{:S(2)}) %collective-permute-start.10) | collective-permute-done | bytes 2097184 | tf_op jit(solution)/shard_map/ppermute | solution.py:103
  272.4 6.1 bitcast_select_fusion.1
  278.6 4.4 collective-permute-start.7
  284.3 39.9 %collective-permute-done.7 = bf16[256,4096]{1,0:T(8,128)(2,1)S(1)} collective-permute-done((bf16[256,4096]{1,0:T(8,128)(2,1)}, bf16[256,4096]{1,0:T(8,128)(2,1)S(1)}, u32[]{:S(2)}, u32[]{:S(2)}) %collective-permute-start.7) | collective-permute-done | bytes 2097184 | tf_op jit(solution)/shard_map/ppermute | solution.py:103
  324.1 4.2 collective-permute-done.11
  328.4 4.1 fusion.48
  332.5 2.6 collective-permute-start.8
  336.6 38.5 %collective-permute-done.8 = bf16[256,4096]{1,0:T(8,128)(2,1)S(1)} collective-permute-done((bf16[256,4096]{1,0:T(8,128)(2,1)S(1)}, bf16[256,4096]{1,0:T(8,128)(2,1)S(1)}, u32[]{:S(2)}, u32[]{:S(2)}) %collective-permute-start.8) | collective-permute-done | bytes 2097184 | tf_op jit(solution)/shard_map/ppermute | solution.py:103
  376.9 2.5 collective-permute-done.12
  382.1 14.8 %fusion.8 = f32[1024,1024]{1,0:T(8,128)} fusion(bf16[1,4096,1024]{2,1,0:T(8,128)(2,1)} %param.6, bf16[256,4096]{1,0:T(8,128)(2,1)S(1)} %select_add_fusion, bf16[256,4096]{1,0:T(8,128)(2,1)S(1)} %get-tuple-element.30, bf16[256,4096]{1,0:T(8,128)(2,1)S(1)} %select_add_fusion.1, bf16[256,4096]{1,0:T(8,128)(2,1)} %multiply_convert_fusion), kind=kOutput, calls=%fused_computation.9 | convolution fusion | flops 8623489024 | bytes 20971520 | tf_op jit(solution)/shard_map/dot_general | solution.py:147
  397.2 4.1 fusion.41
  401.3 3.8 collective-permute-start.9
  406.4 37.6 %collective-permute-done.9 = bf16[256,4096]{1,0:T(8,128)(2,1)S(1)} collective-permute-done((bf16[256,4096]{1,0:T(8,128)(2,1)S(1)}, bf16[256,4096]{1,0:T(8,128)(2,1)S(1)}, u32[]{:S(2)}, u32[]{:S(2)}) %collective-permute-start.9) | collective-permute-done | bytes 2097184 | tf_op jit(solution)/shard_map/ppermute | solution.py:103
  444.0 4.2 collective-permute-done.13
  448.3 6.4 %fusion.37 = bf16[256,4096]{1,0:T(8,128)(2,1)} fusion(bf16[256,4096]{1,0:T(8,128)(2,1)S(1)} %collective-permute-done.13, bf16[4,256,4096]{2,1,0:T(8,128)(2,1)} %bitcast.89, s32[]{:T(128)S(6)} %select_n.296, bf16[256,4096]{1,0:T(8,128)(2,1)S(1)} %collective-permute-done.9, pred[]{:T(512)S(6)} %and.26, pred[]{:T(512)S(6)} %and.20, ...), kind=kLoop, calls=%fused_computation.35 | loop fusion | flops 25165824 | bytes 14680070 | tf_op jit(solution)/shard_map/convert_element_type | solution.py:155
  456.0 4.7 collective-permute-start.14
  460.7 7.4 %fusion.20 = f32[256,1024]{1,0:T(8,128)} fusion(bf16[256,4096]{1,0:T(8,128)(2,1)} %fusion.37, bf16[1,1024,4096]{2,1,0:T(8,128)(2,1)} %param.5), kind=kOutput, calls=%fused_computation.21 | convolution fusion | flops 2147483648 | bytes 11534336 | tf_op jit(solution)/shard_map/dot_general | solution.py:181
  468.1 29.3 %collective-permute-done.16 = bf16[256,4096]{1,0:T(8,128)(2,1)} collective-permute-done((bf16[256,4096]{1,0:T(8,128)(2,1)}, bf16[256,4096]{1,0:T(8,128)(2,1)}, u32[]{:S(2)}, u32[]{:S(2)}) %collective-permute-start.16) | collective-permute-done | bytes 2097184 | tf_op jit(solution)/shard_map/ppermute | solution.py:103
  497.4 3.0 broadcast_select_fusion.1
  503.8 2.1 collective-permute-start.15
  505.8 7.5 %fusion.16 = f32[256,1024]{1,0:T(8,128)} fusion(bf16[256,4096]{1,0:T(8,128)(2,1)} %broadcast_select_fusion.1, bf16[1,1024,4096]{2,1,0:T(8,128)(2,1)} %param.5), kind=kOutput, calls=%fused_computation.17 | convolution fusion | flops 2147483648 | bytes 11534336 | tf_op jit(solution)/shard_map/dot_general | solution.py:181
  513.6 14.0 %convolution_convert_fusion = bf16[4096,1024]{1,0:T(8,128)(2,1)} fusion(s32[]{:T(128)S(6)} %select_n.321, bf16[1024,1024]{1,0:T(8,128)(2,1)} %all-gather.5.cloned.1.call-done, bf16[256,4096]{1,0:T(8,128)(2,1)} %copy-done.13, bf16[256,4096]{1,0:T(8,128)(2,1)} %copy-done.14, bf16[256,4096]{1,0:T(8,128)(2,1)S(1)} %copy-done.12, ...), kind=kOutput, calls=%fused_computation.28 | convolution fusion | flops 8631877632 | bytes 18874372 | tf_op jit(solution)/shard_map/dot_general | solution.py:149
  527.6 7.4 %fusion.18 = f32[256,1024]{1,0:T(8,128)} fusion(bf16[256,4096]{1,0:T(8,128)(2,1)} %broadcast_select_fusion.6, bf16[1,1024,4096]{2,1,0:T(8,128)(2,1)} %param.5), kind=kOutput, calls=%fused_computation.19 | convolution fusion | flops 2147483648 | bytes 11534336 | tf_op jit(solution)/shard_map/dot_general | solution.py:181
  535.0 7.1 %collective-permute-done.17 = bf16[256,4096]{1,0:T(8,128)(2,1)} collective-permute-done((bf16[256,4096]{1,0:T(8,128)(2,1)}, bf16[256,4096]{1,0:T(8,128)(2,1)}, u32[]{:S(2)}, u32[]{:S(2)}) %collective-permute-start.17) | collective-permute-done | bytes 2097184 | tf_op jit(solution)/shard_map/ppermute | solution.py:103
  545.4 2.0 collective-permute-start.18
  548.7 2.4 add.231
  552.5 6.7 %fusion.14 = f32[256,1024]{1,0:T(8,128)} fusion(bf16[256,4096]{1,0:T(8,128)(2,1)S(1)} %add.231, bf16[1,1024,4096]{2,1,0:T(8,128)(2,1)} %param.5), kind=kOutput, calls=%fused_computation.15 | convolution fusion | flops 2147483648 | bytes 11534336 | tf_op jit(solution)/shard_map/dot_general | solution.py:181
  560.7 2.5 fusion.60
  563.2 26.0 %collective-permute-done.19 = bf16[256,4096]{1,0:T(8,128)(2,1)} collective-permute-done((bf16[256,4096]{1,0:T(8,128)(2,1)S(1)}, bf16[256,4096]{1,0:T(8,128)(2,1)}, u32[]{:S(2)}, u32[]{:S(2)}) %collective-permute-start.19) | collective-permute-done | bytes 2097184 | tf_op jit(solution)/shard_map/ppermute | solution.py:103
  589.2 7.4 %fusion.12 = f32[256,1024]{1,0:T(8,128)} fusion(bf16[1,1024,4096]{2,1,0:T(8,128)(2,1)} %param.5, bf16[256,4096]{1,0:T(8,128)(2,1)} %collective-permute-done.19, pred[]{:T(512)S(6)} %and.24, bf16[256,4096]{1,0:T(8,128)(2,1)} %collective-permute-done.18, pred[]{:T(512)S(6)} %and.27), kind=kOutput, calls=%fused_computation.13 | convolution fusion | flops 2150629376 | bytes 13631490 | tf_op jit(solution)/shard_map/dot_general | solution.py:181
  601.1 14.1 %convert_bitcast_fusion = bf16[1,1024,4096]{2,1,0:T(8,128)(2,1)} fusion(bf16[256,4096]{1,0:T(8,128)(2,1)S(1)} %fusion.56, bf16[256,4096]{1,0:T(8,128)(2,1)S(1)} %copy-done.10, bf16[256,4096]{1,0:T(8,128)(2,1)S(1)} %fusion.57, bf16[256,4096]{1,0:T(8,128)(2,1)} %fusion.37, s32[]{:T(128)S(6)} %select_n.321, bf16[1024,1024]{1,0:T(8,128)(2,1)} %all-gather.3.cloned.1.call-done), kind=kOutput, calls=%fused_computation.25 | convolution fusion | flops 8631877632 | bytes 18874372 | tf_op jit(solution)/shard_map/dot_general | solution.py:167
  615.3 8.2 %reduce-scatter.17.cloned.1.call-done = f32[256,256]{1,0:T(8,128)} async-done(((f32[256,1024]{1,0:T(8,128)}), f32[256,256]{1,0:T(8,128)}) %reduce-scatter.17.cloned.1.call-update) | async-done | bytes 262160 | tf_op jit(solution)/shard_map/reduce_scatter | solution.py:184
  (90 shorter events, 38.7 us)
Async XLA Ops:
  7.2 28.0 %all-gather.3.cloned.1.call-start = ((), (), s32[]{:S(2)}) async-start(), calls=%async_computation.6 | async-start | bytes 2621440 | tf_op jit(solution)/shard_map/all_gather | solution.py:121
  7.9 51.7 %all-gather.5.cloned.1.call-start = ((), (), s32[]{:S(2)}) async-start(), calls=%async_computation.7 | async-start | bytes 2621440 | tf_op jit(solution)/shard_map/all_gather | solution.py:123
  8.6 536.7 %reduce-scatter.7.cloned.1.call-start = ((), (), s32[]{:S(2)}) async-start(), calls=%async_computation.8 | async-start | bytes 5242880 | tf_op jit(solution)/shard_map/reduce_scatter | solution.py:148
  47.9 4.0 copy-start
  51.9 22.5 %collective-permute-start.1 = (bf16[256,4096]{1,0:T(8,128)(2,1)}, bf16[256,4096]{1,0:T(8,128)(2,1)}, u32[]{:S(2)}, u32[]{:S(2)}) collective-permute-start(bf16[256,4096]{1,0:T(8,128)(2,1)} %get-tuple-element.28), channel_id=1, source_target_pairs={{12,8},{13,9},{14,10},{15,11},{28,24},{29,25},{30,26},{31,27}} | collective-permute-start | bytes 6291464 | tf_op jit(solution)/shard_map/ppermute | solution.py:103
  53.9 48.7 %collective-permute-start = (bf16[256,4096]{1,0:T(8,128)(2,1)S(1)}, bf16[256,4096]{1,0:T(8,128)(2,1)}, u32[]{:S(2)}, u32[]{:S(2)}) collective-permute-start(bf16[256,4096]{1,0:T(8,128)(2,1)S(1)} %get-tuple-element.29), channel_id=1, source_target_pairs={{0,4},{1,5},{2,6},{3,7},{16,20},{17,21},{18,22},{19,23}} | collective-permute-start | bytes 6291464 | tf_op jit(solution)/shard_map/ppermute | solution.py:103
  74.4 28.5 %copy-start.1 = (bf16[1024,4096]{1,0:T(8,128)(2,1)S(1)}, bf16[1024,4096]{1,0:T(8,128)(2,1)}, u32[]{:S(2)}) copy-start(bf16[1024,4096]{1,0:T(8,128)(2,1)} %copy-done) | copy-start | bytes 25165828
  106.4 50.9 %collective-permute-start.2 = (bf16[256,4096]{1,0:T(8,128)(2,1)}, bf16[256,4096]{1,0:T(8,128)(2,1)S(1)}, u32[]{:S(2)}, u32[]{:S(2)}) collective-permute-start(bf16[256,4096]{1,0:T(8,128)(2,1)} %get-tuple-element.26), channel_id=1, source_target_pairs={{0,4},{4,8},{1,5},{5,9},{2,6},{6,10},{3,7},{7,11},{16,20},{20,24},... | collective-permute-start | bytes 6291464 | tf_op jit(solution)/shard_map/ppermute | solution.py:103
  112.7 44.7 %collective-permute-start.4 = (bf16[256,4096]{1,0:T(8,128)(2,1)}, bf16[256,4096]{1,0:T(8,128)(2,1)}, u32[]{:S(2)}, u32[]{:S(2)}) collective-permute-start(bf16[256,4096]{1,0:T(8,128)(2,1)} %get-tuple-element.27), channel_id=1, source_target_pairs={{8,4},{12,8},{9,5},{13,9},{10,6},{14,10},{11,7},{15,11},{24,20},{2... | collective-permute-start | bytes 6291464 | tf_op jit(solution)/shard_map/ppermute | solution.py:103
  163.3 52.6 %collective-permute-start.3 = (bf16[256,4096]{1,0:T(8,128)(2,1)}, bf16[256,4096]{1,0:T(8,128)(2,1)S(1)}, u32[]{:S(2)}, u32[]{:S(2)}) collective-permute-start(bf16[256,4096]{1,0:T(8,128)(2,1)} %get-tuple-element.24), channel_id=1, source_target_pairs={{0,4},{4,8},{8,12},{1,5},{5,9},{9,13},{2,6},{6,10},{10,14},{3,7},{... | collective-permute-start | bytes 6291464 | tf_op jit(solution)/shard_map/ppermute | solution.py:103
  172.4 47.7 %collective-permute-start.5 = (bf16[256,4096]{1,0:T(8,128)(2,1)}, bf16[256,4096]{1,0:T(8,128)(2,1)}, u32[]{:S(2)}, u32[]{:S(2)}) collective-permute-start(bf16[256,4096]{1,0:T(8,128)(2,1)} %get-tuple-element.25), channel_id=1, source_target_pairs={{4,0},{8,4},{12,8},{5,1},{9,5},{13,9},{6,2},{10,6},{14,10},{7,3},{... | collective-permute-start | bytes 6291464 | tf_op jit(solution)/shard_map/ppermute | solution.py:103
  215.9 8.6 %copy-start.5 = (bf16[256,4096]{1,0:T(8,128)(2,1)}, bf16[256,4096]{1,0:T(8,128)(2,1)S(1)}, u32[]{:S(2)}) copy-start(bf16[256,4096]{1,0:T(8,128)(2,1)S(1)} %collective-permute-done.3) | copy-start | bytes 6291460
  224.5 46.8 %collective-permute-start.10 = (bf16[256,4096]{1,0:T(8,128)(2,1)}, bf16[256,4096]{1,0:T(8,128)(2,1)}, u32[]{:S(2)}, u32[]{:S(2)}) collective-permute-start(bf16[256,4096]{1,0:T(8,128)(2,1)} %multiply_convert_fusion), channel_id=1, source_target_pairs={{4,0},{8,4},{12,8},{5,1},{9,5},{13,9},{6,2},{10,6},{14,10},{7,3},{... | collective-permute-start | bytes 6291464 | tf_op jit(solution)/shard_map/ppermute | solution.py:103
  225.8 46.7 %collective-permute-start.6 = (bf16[256,4096]{1,0:T(8,128)(2,1)}, bf16[256,4096]{1,0:T(8,128)(2,1)S(1)}, u32[]{:S(2)}, u32[]{:S(2)}) collective-permute-start(bf16[256,4096]{1,0:T(8,128)(2,1)} %multiply_convert_fusion), channel_id=1, source_target_pairs={{0,4},{4,8},{8,12},{1,5},{5,9},{9,13},{2,6},{6,10},{10,14},{3,7},{... | collective-permute-start | bytes 6291464 | tf_op jit(solution)/shard_map/ppermute | solution.py:103
  272.4 6.1 copy-start.7
  278.6 45.6 %collective-permute-start.7 = (bf16[256,4096]{1,0:T(8,128)(2,1)}, bf16[256,4096]{1,0:T(8,128)(2,1)S(1)}, u32[]{:S(2)}, u32[]{:S(2)}) collective-permute-start(bf16[256,4096]{1,0:T(8,128)(2,1)} %get-tuple-element.22), channel_id=1, source_target_pairs={{4,8},{8,12},{0,4},{5,9},{9,13},{1,5},{6,10},{10,14},{2,6},{7,11},... | collective-permute-start | bytes 6291464 | tf_op jit(solution)/shard_map/ppermute | solution.py:103
  283.0 45.4 %collective-permute-start.11 = (bf16[256,4096]{1,0:T(8,128)(2,1)}, bf16[256,4096]{1,0:T(8,128)(2,1)}, u32[]{:S(2)}, u32[]{:S(2)}) collective-permute-start(bf16[256,4096]{1,0:T(8,128)(2,1)} %get-tuple-element.23), channel_id=1, source_target_pairs={{4,0},{8,4},{12,8},{5,1},{9,5},{13,9},{6,2},{10,6},{14,10},{7,3},{... | collective-permute-start | bytes 6291464 | tf_op jit(solution)/shard_map/ppermute | solution.py:103
  332.5 48.3 %copy-start.14 = (bf16[256,4096]{1,0:T(8,128)(2,1)}, bf16[256,4096]{1,0:T(8,128)(2,1)S(1)}, u32[]{:S(2)}) copy-start(bf16[256,4096]{1,0:T(8,128)(2,1)S(1)} %get-tuple-element.30) | copy-start | bytes 6291460
  332.5 42.6 %collective-permute-start.8 = (bf16[256,4096]{1,0:T(8,128)(2,1)S(1)}, bf16[256,4096]{1,0:T(8,128)(2,1)S(1)}, u32[]{:S(2)}, u32[]{:S(2)}) collective-permute-start(bf16[256,4096]{1,0:T(8,128)(2,1)S(1)} %get-tuple-element.20), channel_id=1, source_target_pairs={{8,12},{0,4},{4,8},{9,13},{1,5},{5,9},{10,14},{2,6},{6,10},{11,15}... | collective-permute-start | bytes 6291464 | tf_op jit(solution)/shard_map/ppermute | solution.py:103
  335.1 44.3 %copy-start.8 = (bf16[256,4096]{1,0:T(8,128)(2,1)S(1)}, bf16[256,4096]{1,0:T(8,128)(2,1)}, u32[]{:S(2)}) copy-start(bf16[256,4096]{1,0:T(8,128)(2,1)} %copy-done.7) | copy-start | bytes 6291460
  335.2 44.3 %collective-permute-start.12 = (bf16[256,4096]{1,0:T(8,128)(2,1)S(1)}, bf16[256,4096]{1,0:T(8,128)(2,1)S(1)}, u32[]{:S(2)}, u32[]{:S(2)}) collective-permute-start(bf16[256,4096]{1,0:T(8,128)(2,1)S(1)} %get-tuple-element.21), channel_id=1, source_target_pairs={{4,0},{8,4},{12,8},{5,1},{9,5},{13,9},{6,2},{10,6},{14,10},{7,3},{... | collective-permute-start | bytes 6291464 | tf_op jit(solution)/shard_map/ppermute | solution.py:103
  376.9 3.9 copy-start.11
  379.5 1.3 copy-start.2
  380.8 1.4 copy-start.13
  397.0 218.2 %reduce-scatter.9.cloned.1.call-start = ((), (), s32[]{:S(2)}) async-start(), calls=%async_computation.9 | async-start | bytes 1310720 | tf_op jit(solution)/shard_map/reduce_scatter | solution.py:184
  397.2 51.1 %copy-start.6 = (bf16[256,4096]{1,0:T(8,128)(2,1)S(1)}, bf16[256,4096]{1,0:T(8,128)(2,1)}, u32[]{:S(2)}) copy-start(bf16[256,4096]{1,0:T(8,128)(2,1)} %copy-done.5) | copy-start | bytes 6291460
  401.3 42.7 %collective-permute-start.9 = (bf16[256,4096]{1,0:T(8,128)(2,1)S(1)}, bf16[256,4096]{1,0:T(8,128)(2,1)S(1)}, u32[]{:S(2)}, u32[]{:S(2)}) collective-permute-start(bf16[256,4096]{1,0:T(8,128)(2,1)S(1)} %get-tuple-element.18), channel_id=1, source_target_pairs={{0,4},{4,8},{8,12},{1,5},{5,9},{9,13},{2,6},{6,10},{10,14},{3,7},{... | collective-permute-start | bytes 6291464 | tf_op jit(solution)/shard_map/ppermute | solution.py:103
  405.1 43.1 %collective-permute-start.13 = (bf16[256,4096]{1,0:T(8,128)(2,1)S(1)}, bf16[256,4096]{1,0:T(8,128)(2,1)S(1)}, u32[]{:S(2)}, u32[]{:S(2)}) collective-permute-start(bf16[256,4096]{1,0:T(8,128)(2,1)S(1)} %get-tuple-element.19), channel_id=1, source_target_pairs={{4,0},{8,4},{12,8},{5,1},{9,5},{13,9},{6,2},{10,6},{14,10},{7,3},{... | collective-permute-start | bytes 6291464 | tf_op jit(solution)/shard_map/ppermute | solution.py:103
  454.7 42.7 %collective-permute-start.16 = (bf16[256,4096]{1,0:T(8,128)(2,1)}, bf16[256,4096]{1,0:T(8,128)(2,1)}, u32[]{:S(2)}, u32[]{:S(2)}) collective-permute-start(bf16[256,4096]{1,0:T(8,128)(2,1)} %fusion.37), channel_id=1, source_target_pairs={{4,0},{8,4},{12,8},{5,1},{9,5},{13,9},{6,2},{10,6},{14,10},{7,3},{... | collective-permute-start | bytes 6291464 | tf_op jit(solution)/shard_map/ppermute | solution.py:103
  456.0 45.8 %collective-permute-start.14 = (bf16[256,4096]{1,0:T(8,128)(2,1)}, bf16[256,4096]{1,0:T(8,128)(2,1)S(1)}, u32[]{:S(2)}, u32[]{:S(2)}) collective-permute-start(bf16[256,4096]{1,0:T(8,128)(2,1)} %fusion.37), channel_id=1, source_target_pairs={{0,4},{4,8},{8,12},{1,5},{5,9},{9,13},{2,6},{6,10},{10,14},{3,7},{... | collective-permute-start | bytes 6291464 | tf_op jit(solution)/shard_map/ppermute | solution.py:103
  468.1 147.1 %reduce-scatter.13.cloned.1.call-start = ((), (), s32[]{:S(2)}) async-start(), calls=%async_computation.11 | async-start | bytes 1310720 | tf_op jit(solution)/shard_map/reduce_scatter | solution.py:184
  500.5 41.7 %collective-permute-start.17 = (bf16[256,4096]{1,0:T(8,128)(2,1)}, bf16[256,4096]{1,0:T(8,128)(2,1)}, u32[]{:S(2)}, u32[]{:S(2)}) collective-permute-start(bf16[256,4096]{1,0:T(8,128)(2,1)} %broadcast_select_fusion.1), channel_id=1, source_target_pairs={{4,0},{8,4},{5,1},{9,5},{6,2},{10,6},{7,3},{11,7},{20,16},{24,20},... | collective-permute-start | bytes 6291464 | tf_op jit(solution)/shard_map/ppermute | solution.py:103
  501.8 2.0 copy-start.3
  503.8 40.1 %collective-permute-start.15 = (bf16[256,4096]{1,0:T(8,128)(2,1)}, bf16[256,4096]{1,0:T(8,128)(2,1)}, u32[]{:S(2)}, u32[]{:S(2)}) collective-permute-start(bf16[256,4096]{1,0:T(8,128)(2,1)} %broadcast_select_fusion.6), channel_id=1, source_target_pairs={{4,8},{8,12},{5,9},{9,13},{6,10},{10,14},{7,11},{11,15},{20,24},{2... | collective-permute-start | bytes 6291464 | tf_op jit(solution)/shard_map/ppermute | solution.py:103
  505.8 7.8 %copy-start.12 = (bf16[256,4096]{1,0:T(8,128)(2,1)S(1)}, bf16[256,4096]{1,0:T(8,128)(2,1)}, u32[]{:S(2)}) copy-start(bf16[256,4096]{1,0:T(8,128)(2,1)} %copy-done.11) | copy-start | bytes 6291460
  513.4 101.9 %reduce-scatter.11.cloned.1.call-start = ((), (), s32[]{:S(2)}) async-start(), calls=%async_computation.10 | async-start | bytes 1310720 | tf_op jit(solution)/shard_map/reduce_scatter | solution.py:184
  535.0 80.3 %reduce-scatter.15.cloned.1.call-start = ((), (), s32[]{:S(2)}) async-start(), calls=%async_computation.12 | async-start | bytes 1310720 | tf_op jit(solution)/shard_map/reduce_scatter | solution.py:184
  545.4 17.8 %collective-permute-start.18 = (bf16[256,4096]{1,0:T(8,128)(2,1)}, bf16[256,4096]{1,0:T(8,128)(2,1)}, u32[]{:S(2)}, u32[]{:S(2)}) collective-permute-start(bf16[256,4096]{1,0:T(8,128)(2,1)} %broadcast_select_fusion.8), channel_id=1, source_target_pairs={{8,12},{9,13},{10,14},{11,15},{24,28},{25,29},{26,30},{27,31}} | collective-permute-start | bytes 6291464 | tf_op jit(solution)/shard_map/ppermute | solution.py:103
  547.4 41.8 %collective-permute-start.19 = (bf16[256,4096]{1,0:T(8,128)(2,1)S(1)}, bf16[256,4096]{1,0:T(8,128)(2,1)}, u32[]{:S(2)}, u32[]{:S(2)}) collective-permute-start(bf16[256,4096]{1,0:T(8,128)(2,1)S(1)} %broadcast_select_fusion.4), channel_id=1, source_target_pairs={{4,0},{5,1},{6,2},{7,3},{20,16},{21,17},{22,18},{23,19}} | collective-permute-start | bytes 6291464 | tf_op jit(solution)/shard_map/ppermute | solution.py:103
  551.1 1.4 copy-start.9
  559.2 64.3 %reduce-scatter.17.cloned.1.call-start = ((), (), s32[]{:S(2)}) async-start(), calls=%async_computation.13 | async-start | bytes 1310720 | tf_op jit(solution)/shard_map/reduce_scatter | solution.py:184
  596.7 2.2 copy-start.4
  598.9 2.2 copy-start.10
  615.2 9.8 %copy-start.15 = (f32[256,256]{1,0:T(8,128)S(1)}, f32[256,256]{1,0:T(8,128)}, u32[]{:S(2)}) copy-start(f32[256,256]{1,0:T(8,128)} %reduce-scatter.9.cloned.1.call-done) | copy-start | bytes 786436
  615.2 9.8 %copy-start.16 = (f32[256,256]{1,0:T(8,128)S(1)}, f32[256,256]{1,0:T(8,128)}, u32[]{:S(2)}) copy-start(f32[256,256]{1,0:T(8,128)} %reduce-scatter.13.cloned.1.call-done) | copy-start | bytes 786436
  615.2 9.8 %copy-start.17 = (f32[256,256]{1,0:T(8,128)S(1)}, f32[256,256]{1,0:T(8,128)}, u32[]{:S(2)}) copy-start(f32[256,256]{1,0:T(8,128)} %reduce-scatter.11.cloned.1.call-done) | copy-start | bytes 786436
  615.3 9.8 %copy-start.18 = (f32[256,256]{1,0:T(8,128)S(1)}, f32[256,256]{1,0:T(8,128)}, u32[]{:S(2)}) copy-start(f32[256,256]{1,0:T(8,128)} %reduce-scatter.15.cloned.1.call-done) | copy-start | bytes 786436
  623.5 1.5 copy-start.19
Sparse Core Ops, SparseCore 0:
  9.6 25.5 all-gather.2
  36.7 22.8 all-gather.4
  397.1 42.3 reduce-scatter.6
  468.2 23.0 reduce-scatter.8
  513.5 27.5 reduce-scatter.12
  543.6 24.8 reduce-scatter.10
  571.0 24.8 reduce-scatter.14
  598.6 24.8 reduce-scatter.16
where the time goes:
time: 642 us; the launch traced here: 633 us
  waiting for transfers between devices  385 us (60%)
  matrix products  107 us (17%)
  starting transfers between devices  59.7 us (9%)
  other arithmetic  57.7 us (9%)
  between operations  15.1 us (2%)
  local copies, waits for them, and re-layouts  8.72 us (1%)
    ppermute x20, waiting for transfers between devices, run_slot(): received.append(lax.ppermute(combined, 'r', pairs))  348 us
    ppermute x20, starting transfers between devices, run_slot(): received.append(lax.ppermute(combined, 'r', pairs))  58.7 us
    dot_general x5, matrix products, on_device(): lax.dot_general(piece, up_tile, (((1,), (1,)), ((), ())), preferred_eleme...  36.3 us
    all_gather x1, waiting for transfers between devices, on_device(): x_rows = lax.all_gather(hidden_in, 'p', axis=1, tiled=True)  26.4 us
    dot_general x1, matrix products, on_device(): lax.dot_general(grad_rows, down_tile, (((1,), (1,)), ((), ())), preferred...  14.8 us
    dot_general x1, matrix products, on_device(): jnp.dot(activation, down_tile, preferred_element_type=jnp.float32)  14.8 us
    dot_general x1, matrix products, on_device(): lax.dot_general(rotate_rows(x_rows, turn), pre_grad, (((0,), (0,)), ((),...  14.1 us
    dot_general x1, matrix products, on_device(): lax.dot_general(activation, grad_turned, (((0,), (0,)), ((), ())), prefer...  14 us
  transfers between devices with their start and end apart: 28, of which 18 were waited for; matrix products, arithmetic and copies ran while one was open for 20% of the time, Pallas kernels for 0%

commit v1 on v0

--- a/solution.py
+++ b/solution.py
@@ -29,11 +29,14 @@
         self.shares = terms.reshape(self.count, rows, terms.shape[1])
         self.up_in = jnp.zeros((rows, terms.shape[1]), jnp.float32)
         self.down_in = jnp.zeros((rows, terms.shape[1]), jnp.float32)
+        self.first = None
 
     def senders(self, step):
         return (0, step), (self.count - 1 - step, self.count - 1)
 
     def payload(self, step):
+        if step == 0 and self.first is not None:
+            return self.first
         last = self.count - 1
         up_block = jnp.clip(last - step + self.pos, 0, last)
         down_block = jnp.clip(self.pos + step - last, 0, last)
@@ -127,9 +130,18 @@
 
     up_sum = LineReduce(up_terms)
     if count > 1:
+        rows = x_rows.shape[0] // count
+        last = count - 1
+        pos = lax.axis_index("r")
+
+        def block_terms(block):
+            x_block = lax.dynamic_slice_in_dim(x_rows, block * rows, rows, axis=0)
+            return jnp.dot(x_block, up_tile, preferred_element_type=jnp.float32).astype(jnp.bfloat16)
+
+        up_sum.first = (block_terms(jnp.clip(last + pos, 0, last)), block_terms(jnp.clip(pos - last, 0, last)))
         run_slot([(up_sum, 0)])
-        up_sum.up_in, up_sum.down_in, grad_terms = lax.optimization_barrier(
-            (up_sum.up_in, up_sum.down_in, grad_terms)
+        up_sum.up_in, up_sum.down_in, up_sum.shares, grad_terms = lax.optimization_barrier(
+            (up_sum.up_in, up_sum.down_in, up_sum.shares, grad_terms)
         )
     grad_sum = LineReduce(grad_terms)
     for step in range(1, count - 1):

time: 642 us -> 635 us (0.989)
  waiting for transfers between devices: 385 us -> 366 us
  matrix products: 107 us -> 119 us
    ppermute x20, waiting for transfers between devices: 348 us -> 330 us  [run_slot(): received.append(lax.ppermute(combined, 'r', pairs))]
    dot_general x0 -> x2, matrix products: none -> 14.5 us  [block_terms(): jnp.dot(x_block, up_tile, preferred_element_type=jnp.float32)]
  transfers between devices with their start and end apart: 28 -> 28, of which waited for: 18 -> 17; matrix products, arithmetic and copies ran while one was open for 20% -> 21% of each run, Pallas kernels for 0% -> 0%
where the time goes in v1:
time: 635 us; the launch traced here: 630 us
  waiting for transfers between devices  366 us (58%)
  matrix products  119 us (19%)
  starting transfers between devices  64.1 us (10%)
  other arithmetic  57.7 us (9%)
  between operations  14.9 us (2%)
  local copies, waits for them, and re-layouts  7.45 us (1%)
    ppermute x20, waiting for transfers between devices, run_slot(): received.append(lax.ppermute(combined, 'r', pairs))  330 us
    ppermute x20, starting transfers between devices, run_slot(): received.append(lax.ppermute(combined, 'r', pairs))  63.2 us
    dot_general x5, matrix products, on_device(): lax.dot_general(piece, up_tile, (((1,), (1,)), ((), ())), preferred_eleme...  36.4 us
    all_gather x1, waiting for transfers between devices, on_device(): x_rows = lax.all_gather(hidden_in, 'p', axis=1, tiled=True)  26.4 us
    dot_general x1, matrix products, on_device(): lax.dot_general(grad_rows, down_tile, (((1,), (1,)), ((), ())), preferred...  14.8 us
    dot_general x1, matrix products, on_device(): jnp.dot(activation, down_tile, preferred_element_type=jnp.float32)  14.8 us
    dot_general x2, matrix products, block_terms(): jnp.dot(x_block, up_tile, preferred_element_type=jnp.float32)  14.5 us
    dot_general x1, matrix products, on_device(): lax.dot_general(rotate_rows(x_rows, turn), pre_grad, (((0,), (0,)), ((),...  14.1 us
  transfers between devices with their start and end apart: 28, of which 17 were waited for; matrix products, arithmetic and copies ran while one was open for 21% of the time, Pallas kernels for 0%

profile of v1, /device:TPU:0, one launch (start us, length us, event | category | flops | bytes accessed | tf_op | source)
XLA Modules:
  0.0 630.0 jit_solution(16077709888512194625)
XLA Ops:
  8.7 26.4 %all-gather.3.cloned.1.call-done = bf16[1024,1024]{1,0:T(8,128)(2,1)} async-done(((bf16[1024,256]{1,0:T(8,128)(2,1)}), bf16[1024,1024]{1,0:T(8,128)(2,1)}) %all-gather.3.cloned.1.call-update) | async-done | bytes 2097168 | tf_op jit(solution)/shard_map/all_gather | solution.py:124
  35.1 7.4 %fusion.36 = bf16[256,4096]{1,0:T(8,128)(2,1)} fusion(bf16[1,1024,4096]{2,1,0:T(8,128)(2,1)} %param.5, bf16[1024,1024]{1,0:T(8,128)(2,1)} %all-gather.3.cloned.1.call-done, s32[]{:T(128)S(6)} %select_n.295), kind=kOutput, calls=%fused_computation.34 | convolution fusion | flops 2148532224 | bytes 11010052 | tf_op jit(solution)/shard_map/dot_general | solution.py:139
  42.5 3.8 collective-permute-start
  46.3 7.1 %fusion.39 = bf16[256,4096]{1,0:T(8,128)(2,1)} fusion(bf16[1,1024,4096]{2,1,0:T(8,128)(2,1)} %param.5, bf16[1024,1024]{1,0:T(8,128)(2,1)S(1)} %copy-done.19, s32[]{:T(128)S(6)} %select_n.298), kind=kOutput, calls=%fused_computation.35 | convolution fusion | flops 2148532224 | bytes 11010052 | tf_op jit(solution)/shard_map/dot_general | solution.py:139
  53.4 2.4 collective-permute-start.1
  55.9 10.8 %fusion.28 = bf16[1024,4096]{1,0:T(8,128)(2,1)} fusion(bf16[1024,1024]{1,0:T(8,128)(2,1)S(1)} %copy-done.19, bf16[1,1024,4096]{2,1,0:T(8,128)(2,1)S(1)} %bitcast.94), kind=kOutput, calls=%fused_computation.30 | convolution fusion | flops 8594128896 | bytes 18874368 | tf_op jit(solution)/shard_map/dot_general | solution.py:125
  66.7 14.8 %fusion.31 = bf16[1024,4096]{1,0:T(8,128)(2,1)} fusion(bf16[1024,1024]{1,0:T(8,128)(2,1)} %all-gather.5.cloned.1.call-done, bf16[1,4096,1024]{2,1,0:T(8,128)(2,1)} %param.6), kind=kOutput, calls=%fused_computation.31 | convolution fusion | flops 8594128896 | bytes 18874368 | tf_op jit(solution)/shard_map/dot_general | solution.py:127
  81.5 10.2 %collective-permute-done = bf16[256,4096]{1,0:T(8,128)(2,1)S(1)} collective-permute-done((bf16[256,4096]{1,0:T(8,128)(2,1)}, bf16[256,4096]{1,0:T(8,128)(2,1)S(1)}, u32[]{:S(2)}, u32[]{:S(2)}) %collective-permute-start) | collective-permute-done | bytes 2097184 | tf_op jit(solution)/shard_map/ppermute | solution.py:106
  92.3 2.8 copy-done
  95.1 3.6 fusion.57
  98.7 4.4 collective-permute-start.2
  105.1 42.6 %collective-permute-done.2 = bf16[256,4096]{1,0:T(8,128)(2,1)S(1)} collective-permute-done((bf16[256,4096]{1,0:T(8,128)(2,1)}, bf16[256,4096]{1,0:T(8,128)(2,1)S(1)}, u32[]{:S(2)}, u32[]{:S(2)}) %collective-permute-start.2) | collective-permute-done | bytes 2097184 | tf_op jit(solution)/shard_map/ppermute | solution.py:106
  147.8 6.0 fusion.56
  153.8 15.5 %collective-permute-start.3 = (bf16[256,4096]{1,0:T(8,128)(2,1)}, bf16[256,4096]{1,0:T(8,128)(2,1)S(1)}, u32[]{:S(2)}, u32[]{:S(2)}) collective-permute-start(bf16[256,4096]{1,0:T(8,128)(2,1)} %get-tuple-element.26), channel_id=1, source_target_pairs={{0,4},{4,8},{8,12},{1,5},{5,9},{9,13},{2,6},{6,10},{10,14},{3,7},{... | collective-permute-start | bytes 6291464 | tf_op jit(solution)/shard_map/ppermute | solution.py:106
  170.7 42.1 %collective-permute-done.3 = bf16[256,4096]{1,0:T(8,128)(2,1)S(1)} collective-permute-done((bf16[256,4096]{1,0:T(8,128)(2,1)}, bf16[256,4096]{1,0:T(8,128)(2,1)S(1)}, u32[]{:S(2)}, u32[]{:S(2)}) %collective-permute-start.3) | collective-permute-done | bytes 2097184 | tf_op jit(solution)/shard_map/ppermute | solution.py:106
  212.8 4.2 collective-permute-done.5
  217.1 4.3 multiply_convert_fusion
  222.7 4.9 collective-permute-start.6
  227.5 40.6 %collective-permute-done.10 = bf16[256,4096]{1,0:T(8,128)(2,1)} collective-permute-done((bf16[256,4096]{1,0:T(8,128)(2,1)}, bf16[256,4096]{1,0:T(8,128)(2,1)}, u32[]{:S(2)}, u32[]{:S(2)}) %collective-permute-start.10) | collective-permute-done | bytes 2097184 | tf_op jit(solution)/shard_map/ppermute | solution.py:106
  269.3 6.1 bitcast_select_fusion.1
  275.4 4.4 collective-permute-start.7
  281.2 39.8 %collective-permute-done.7 = bf16[256,4096]{1,0:T(8,128)(2,1)S(1)} collective-permute-done((bf16[256,4096]{1,0:T(8,128)(2,1)}, bf16[256,4096]{1,0:T(8,128)(2,1)S(1)}, u32[]{:S(2)}, u32[]{:S(2)}) %collective-permute-start.7) | collective-permute-done | bytes 2097184 | tf_op jit(solution)/shard_map/ppermute | solution.py:106
  321.0 4.2 collective-permute-done.11
  325.3 4.1 fusion.58
  329.4 2.6 collective-permute-start.8
  333.5 38.5 %collective-permute-done.8 = bf16[256,4096]{1,0:T(8,128)(2,1)S(1)} collective-permute-done((bf16[256,4096]{1,0:T(8,128)(2,1)S(1)}, bf16[256,4096]{1,0:T(8,128)(2,1)S(1)}, u32[]{:S(2)}, u32[]{:S(2)}) %collective-permute-start.8) | collective-permute-done | bytes 2097184 | tf_op jit(solution)/shard_map/ppermute | solution.py:106
  373.8 2.5 collective-permute-done.12
  379.0 14.8 %fusion.8 = f32[1024,1024]{1,0:T(8,128)} fusion(bf16[1,4096,1024]{2,1,0:T(8,128)(2,1)} %param.6, bf16[256,4096]{1,0:T(8,128)(2,1)S(1)} %select_add_fusion, bf16[256,4096]{1,0:T(8,128)(2,1)S(1)} %get-tuple-element.30, bf16[256,4096]{1,0:T(8,128)(2,1)S(1)} %select_add_fusion.1, bf16[256,4096]{1,0:T(8,128)(2,1)} %multiply_convert_fusion), kind=kOutput, calls=%fused_computation.9 | convolution fusion | flops 8623489024 | bytes 20971520 | tf_op jit(solution)/shard_map/dot_general | solution.py:159
  393.9 4.1 fusion.51
  398.0 3.8 collective-permute-start.9
  403.3 37.4 %collective-permute-done.9 = bf16[256,4096]{1,0:T(8,128)(2,1)S(1)} collective-permute-done((bf16[256,4096]{1,0:T(8,128)(2,1)S(1)}, bf16[256,4096]{1,0:T(8,128)(2,1)S(1)}, u32[]{:S(2)}, u32[]{:S(2)}) %collective-permute-start.9) | collective-permute-done | bytes 2097184 | tf_op jit(solution)/shard_map/ppermute | solution.py:106
  440.7 4.2 collective-permute-done.13
  444.9 6.4 %fusion.47 = bf16[256,4096]{1,0:T(8,128)(2,1)} fusion(bf16[256,4096]{1,0:T(8,128)(2,1)S(1)} %collective-permute-done.13, bf16[4,256,4096]{2,1,0:T(8,128)(2,1)} %bitcast.88, s32[]{:T(128)S(6)} %select_n.302, bf16[256,4096]{1,0:T(8,128)(2,1)S(1)} %collective-permute-done.9, pred[]{:T(512)S(6)} %and.26, pred[]{:T(512)S(6)} %and.20, ...), kind=kLoop, calls=%fused_computation.41 | loop fusion | flops 25165824 | bytes 14680070 | tf_op jit(solution)/shard_map/convert_element_type | solution.py:167
  452.7 4.7 collective-permute-start.14
  457.4 7.4 %fusion.20 = f32[256,1024]{1,0:T(8,128)} fusion(bf16[256,4096]{1,0:T(8,128)(2,1)} %fusion.47, bf16[1,1024,4096]{2,1,0:T(8,128)(2,1)} %param.5), kind=kOutput, calls=%fused_computation.21 | convolution fusion | flops 2147483648 | bytes 11534336 | tf_op jit(solution)/shard_map/dot_general | solution.py:193
  464.8 29.3 %collective-permute-done.16 = bf16[256,4096]{1,0:T(8,128)(2,1)} collective-permute-done((bf16[256,4096]{1,0:T(8,128)(2,1)}, bf16[256,4096]{1,0:T(8,128)(2,1)}, u32[]{:S(2)}, u32[]{:S(2)}) %collective-permute-start.16) | collective-permute-done | bytes 2097184 | tf_op jit(solution)/shard_map/ppermute | solution.py:106
  494.1 3.0 broadcast_select_fusion.1
  502.5 7.5 %fusion.16 = f32[256,1024]{1,0:T(8,128)} fusion(bf16[256,4096]{1,0:T(8,128)(2,1)} %broadcast_select_fusion.1, bf16[1,1024,4096]{2,1,0:T(8,128)(2,1)} %param.5), kind=kOutput, calls=%fused_computation.17 | convolution fusion | flops 2147483648 | bytes 11534336 | tf_op jit(solution)/shard_map/dot_general | solution.py:193
  510.5 13.9 %convolution_convert_fusion = bf16[4096,1024]{1,0:T(8,128)(2,1)} fusion(s32[]{:T(128)S(6)} %select_n.327, bf16[1024,1024]{1,0:T(8,128)(2,1)} %all-gather.5.cloned.1.call-done, bf16[256,4096]{1,0:T(8,128)(2,1)} %copy-done.12, bf16[256,4096]{1,0:T(8,128)(2,1)} %copy-done.13, bf16[256,4096]{1,0:T(8,128)(2,1)S(1)} %copy-done.11, ...), kind=kOutput, calls=%fused_computation.32 | convolution fusion | flops 8631877632 | bytes 18874372 | tf_op jit(solution)/shard_map/dot_general | solution.py:161
  524.4 7.4 %fusion.18 = f32[256,1024]{1,0:T(8,128)} fusion(bf16[256,4096]{1,0:T(8,128)(2,1)} %broadcast_select_fusion.6, bf16[1,1024,4096]{2,1,0:T(8,128)(2,1)} %param.5), kind=kOutput, calls=%fused_computation.19 | convolution fusion | flops 2147483648 | bytes 11534336 | tf_op jit(solution)/shard_map/dot_general | solution.py:193
  531.9 6.9 %collective-permute-done.17 = bf16[256,4096]{1,0:T(8,128)(2,1)} collective-permute-done((bf16[256,4096]{1,0:T(8,128)(2,1)}, bf16[256,4096]{1,0:T(8,128)(2,1)}, u32[]{:S(2)}, u32[]{:S(2)}) %collective-permute-start.17) | collective-permute-done | bytes 2097184 | tf_op jit(solution)/shard_map/ppermute | solution.py:106
  545.4 2.4 add.237
  549.2 6.7 %fusion.14 = f32[256,1024]{1,0:T(8,128)} fusion(bf16[256,4096]{1,0:T(8,128)(2,1)S(1)} %add.237, bf16[1,1024,4096]{2,1,0:T(8,128)(2,1)} %param.5), kind=kOutput, calls=%fused_computation.15 | convolution fusion | flops 2147483648 | bytes 11534336 | tf_op jit(solution)/shard_map/dot_general | solution.py:193
  557.4 2.5 fusion.70
  559.9 26.0 %collective-permute-done.19 = bf16[256,4096]{1,0:T(8,128)(2,1)} collective-permute-done((bf16[256,4096]{1,0:T(8,128)(2,1)S(1)}, bf16[256,4096]{1,0:T(8,128)(2,1)}, u32[]{:S(2)}, u32[]{:S(2)}) %collective-permute-start.19) | collective-permute-done | bytes 2097184 | tf_op jit(solution)/shard_map/ppermute | solution.py:106
  585.9 7.4 %fusion.12 = f32[256,1024]{1,0:T(8,128)} fusion(bf16[1,1024,4096]{2,1,0:T(8,128)(2,1)} %param.5, bf16[256,4096]{1,0:T(8,128)(2,1)} %collective-permute-done.19, pred[]{:T(512)S(6)} %and.24, bf16[256,4096]{1,0:T(8,128)(2,1)} %collective-permute-done.18, pred[]{:T(512)S(6)} %and.27), kind=kOutput, calls=%fused_computation.13 | convolution fusion | flops 2150629376 | bytes 13631490 | tf_op jit(solution)/shard_map/dot_general | solution.py:193
  597.7 14.1 %convert_bitcast_fusion = bf16[1,1024,4096]{2,1,0:T(8,128)(2,1)} fusion(bf16[256,4096]{1,0:T(8,128)(2,1)S(1)} %fusion.66, bf16[256,4096]{1,0:T(8,128)(2,1)S(1)} %copy-done.9, bf16[256,4096]{1,0:T(8,128)(2,1)S(1)} %fusion.67, bf16[256,4096]{1,0:T(8,128)(2,1)} %fusion.47, s32[]{:T(128)S(6)} %select_n.327, bf16[1024,1024]{1,0:T(8,128)(2,1)} %all-gather.3.cloned.1.call-done), kind=kOutput, calls=%fused_computation.29 | convolution fusion | flops 8631877632 | bytes 18874372 | tf_op jit(solution)/shard_map/dot_general | solution.py:179
  611.9 8.5 %reduce-scatter.17.cloned.1.call-done = f32[256,256]{1,0:T(8,128)} async-done(((f32[256,1024]{1,0:T(8,128)}), f32[256,256]{1,0:T(8,128)}) %reduce-scatter.17.cloned.1.call-update) | async-done | bytes 262160 | tf_op jit(solution)/shard_map/reduce_scatter | solution.py:196
  (96 shorter events, 40.1 us)
Async XLA Ops:
  7.2 28.0 %all-gather.3.cloned.1.call-start = ((), (), s32[]{:S(2)}) async-start(), calls=%async_computation.6 | async-start | bytes 2621440 | tf_op jit(solution)/shard_map/all_gather | solution.py:124
  7.9 58.8 %all-gather.5.cloned.1.call-start = ((), (), s32[]{:S(2)}) async-start(), calls=%async_computation.7 | async-start | bytes 2621440 | tf_op jit(solution)/shard_map/all_gather | solution.py:126
  8.6 533.4 %reduce-scatter.7.cloned.1.call-start = ((), (), s32[]{:S(2)}) async-start(), calls=%async_computation.8 | async-start | bytes 5242880 | tf_op jit(solution)/shard_map/reduce_scatter | solution.py:160
  35.1 11.2 %copy-start.19 = (bf16[1024,1024]{1,0:T(8,128)(2,1)S(1)}, bf16[1024,1024]{1,0:T(8,128)(2,1)}, u32[]{:S(2)}) copy-start(bf16[1024,1024]{1,0:T(8,128)(2,1)} %all-gather.3.cloned.1.call-done) | copy-start | bytes 6291460
  35.1 20.7 %slice-start = ((s8[8388608]{0:T(1024)(128)(4,1)}), s8[4194304]{0:T(1024)(128)(4,1)S(1)}, s32[]{:S(2)}) async-start(s8[8388608]{0:T(1024)(128)(4,1)} %bitcast.93), calls=%async_computation.14 | async-start | bytes 8388608
  42.5 13.3 %slice-start.1 = ((s8[8388608]{0:T(1024)(128)(4,1)}), s8[4194304]{0:T(1024)(128)(4,1)S(1)}, s32[]{:S(2)}) async-start(s8[8388608]{0:T(1024)(128)(4,1)} %bitcast.93), calls=%async_computation.15 | async-start | bytes 8388608
  42.5 49.3 %collective-permute-start = (bf16[256,4096]{1,0:T(8,128)(2,1)}, bf16[256,4096]{1,0:T(8,128)(2,1)S(1)}, u32[]{:S(2)}, u32[]{:S(2)}) collective-permute-start(bf16[256,4096]{1,0:T(8,128)(2,1)} %fusion.36), channel_id=1, source_target_pairs={{0,4},{1,5},{2,6},{3,7},{16,20},{17,21},{18,22},{19,23}} | collective-permute-start | bytes 6291464 | tf_op jit(solution)/shard_map/ppermute | solution.py:106
  53.4 38.6 %collective-permute-start.1 = (bf16[256,4096]{1,0:T(8,128)(2,1)}, bf16[256,4096]{1,0:T(8,128)(2,1)}, u32[]{:S(2)}, u32[]{:S(2)}) collective-permute-start(bf16[256,4096]{1,0:T(8,128)(2,1)} %fusion.39), channel_id=1, source_target_pairs={{12,8},{13,9},{14,10},{15,11},{28,24},{29,25},{30,26},{31,27}} | collective-permute-start | bytes 6291464 | tf_op jit(solution)/shard_map/ppermute | solution.py:106
  91.8 3.4 copy-start
  98.7 49.1 %collective-permute-start.2 = (bf16[256,4096]{1,0:T(8,128)(2,1)}, bf16[256,4096]{1,0:T(8,128)(2,1)S(1)}, u32[]{:S(2)}, u32[]{:S(2)}) collective-permute-start(bf16[256,4096]{1,0:T(8,128)(2,1)} %get-tuple-element.28), channel_id=1, source_target_pairs={{0,4},{4,8},{1,5},{5,9},{2,6},{6,10},{3,7},{7,11},{16,20},{20,24},... | collective-permute-start | bytes 6291464 | tf_op jit(solution)/shard_map/ppermute | solution.py:106
  103.1 44.7 %collective-permute-start.4 = (bf16[256,4096]{1,0:T(8,128)(2,1)}, bf16[256,4096]{1,0:T(8,128)(2,1)}, u32[]{:S(2)}, u32[]{:S(2)}) collective-permute-start(bf16[256,4096]{1,0:T(8,128)(2,1)} %get-tuple-element.29), channel_id=1, source_target_pairs={{8,4},{12,8},{9,5},{13,9},{10,6},{14,10},{11,7},{15,11},{24,20},{2... | collective-permute-start | bytes 6291464 | tf_op jit(solution)/shard_map/ppermute | solution.py:106
  153.8 59.0 %collective-permute-start.3 = (bf16[256,4096]{1,0:T(8,128)(2,1)}, bf16[256,4096]{1,0:T(8,128)(2,1)S(1)}, u32[]{:S(2)}, u32[]{:S(2)}) collective-permute-start(bf16[256,4096]{1,0:T(8,128)(2,1)} %get-tuple-element.26), channel_id=1, source_target_pairs={{0,4},{4,8},{8,12},{1,5},{5,9},{9,13},{2,6},{6,10},{10,14},{3,7},{... | collective-permute-start | bytes 6291464 | tf_op jit(solution)/shard_map/ppermute | solution.py:106
  169.4 47.7 %collective-permute-start.5 = (bf16[256,4096]{1,0:T(8,128)(2,1)}, bf16[256,4096]{1,0:T(8,128)(2,1)}, u32[]{:S(2)}, u32[]{:S(2)}) collective-permute-start(bf16[256,4096]{1,0:T(8,128)(2,1)} %get-tuple-element.27), channel_id=1, source_target_pairs={{4,0},{8,4},{12,8},{5,1},{9,5},{13,9},{6,2},{10,6},{14,10},{7,3},{... | collective-permute-start | bytes 6291464 | tf_op jit(solution)/shard_map/ppermute | solution.py:106
  212.8 8.6 %copy-start.4 = (bf16[256,4096]{1,0:T(8,128)(2,1)}, bf16[256,4096]{1,0:T(8,128)(2,1)S(1)}, u32[]{:S(2)}) copy-start(bf16[256,4096]{1,0:T(8,128)(2,1)S(1)} %collective-permute-done.3) | copy-start | bytes 6291460
  221.4 46.8 %collective-permute-start.10 = (bf16[256,4096]{1,0:T(8,128)(2,1)}, bf16[256,4096]{1,0:T(8,128)(2,1)}, u32[]{:S(2)}, u32[]{:S(2)}) collective-permute-start(bf16[256,4096]{1,0:T(8,128)(2,1)} %multiply_convert_fusion), channel_id=1, source_target_pairs={{4,0},{8,4},{12,8},{5,1},{9,5},{13,9},{6,2},{10,6},{14,10},{7,3},{... | collective-permute-start | bytes 6291464 | tf_op jit(solution)/shard_map/ppermute | solution.py:106
  222.7 46.7 %collective-permute-start.6 = (bf16[256,4096]{1,0:T(8,128)(2,1)}, bf16[256,4096]{1,0:T(8,128)(2,1)S(1)}, u32[]{:S(2)}, u32[]{:S(2)}) collective-permute-start(bf16[256,4096]{1,0:T(8,128)(2,1)} %multiply_convert_fusion), channel_id=1, source_target_pairs={{0,4},{4,8},{8,12},{1,5},{5,9},{9,13},{2,6},{6,10},{10,14},{3,7},{... | collective-permute-start | bytes 6291464 | tf_op jit(solution)/shard_map/ppermute | solution.py:106
  269.3 6.1 copy-start.6
  275.4 45.6 %collective-permute-start.7 = (bf16[256,4096]{1,0:T(8,128)(2,1)}, bf16[256,4096]{1,0:T(8,128)(2,1)S(1)}, u32[]{:S(2)}, u32[]{:S(2)}) collective-permute-start(bf16[256,4096]{1,0:T(8,128)(2,1)} %get-tuple-element.24), channel_id=1, source_target_pairs={{4,8},{8,12},{0,4},{5,9},{9,13},{1,5},{6,10},{10,14},{2,6},{7,11},... | collective-permute-start | bytes 6291464 | tf_op jit(solution)/shard_map/ppermute | solution.py:106
  279.9 45.4 %collective-permute-start.11 = (bf16[256,4096]{1,0:T(8,128)(2,1)}, bf16[256,4096]{1,0:T(8,128)(2,1)}, u32[]{:S(2)}, u32[]{:S(2)}) collective-permute-start(bf16[256,4096]{1,0:T(8,128)(2,1)} %get-tuple-element.25), channel_id=1, source_target_pairs={{4,0},{8,4},{12,8},{5,1},{9,5},{13,9},{6,2},{10,6},{14,10},{7,3},{... | collective-permute-start | bytes 6291464 | tf_op jit(solution)/shard_map/ppermute | solution.py:106
  329.4 48.3 %copy-start.13 = (bf16[256,4096]{1,0:T(8,128)(2,1)}, bf16[256,4096]{1,0:T(8,128)(2,1)S(1)}, u32[]{:S(2)}) copy-start(bf16[256,4096]{1,0:T(8,128)(2,1)S(1)} %get-tuple-element.30) | copy-start | bytes 6291460
  329.4 42.6 %collective-permute-start.8 = (bf16[256,4096]{1,0:T(8,128)(2,1)S(1)}, bf16[256,4096]{1,0:T(8,128)(2,1)S(1)}, u32[]{:S(2)}, u32[]{:S(2)}) collective-permute-start(bf16[256,4096]{1,0:T(8,128)(2,1)S(1)} %get-tuple-element.22), channel_id=1, source_target_pairs={{8,12},{0,4},{4,8},{9,13},{1,5},{5,9},{10,14},{2,6},{6,10},{11,15}... | collective-permute-start | bytes 6291464 | tf_op jit(solution)/shard_map/ppermute | solution.py:106
  332.0 44.3 %copy-start.7 = (bf16[256,4096]{1,0:T(8,128)(2,1)S(1)}, bf16[256,4096]{1,0:T(8,128)(2,1)}, u32[]{:S(2)}) copy-start(bf16[256,4096]{1,0:T(8,128)(2,1)} %copy-done.6) | copy-start | bytes 6291460
  332.0 44.3 %collective-permute-start.12 = (bf16[256,4096]{1,0:T(8,128)(2,1)S(1)}, bf16[256,4096]{1,0:T(8,128)(2,1)S(1)}, u32[]{:S(2)}, u32[]{:S(2)}) collective-permute-start(bf16[256,4096]{1,0:T(8,128)(2,1)S(1)} %get-tuple-element.23), channel_id=1, source_target_pairs={{4,0},{8,4},{12,8},{5,1},{9,5},{13,9},{6,2},{10,6},{14,10},{7,3},{... | collective-permute-start | bytes 6291464 | tf_op jit(solution)/shard_map/ppermute | solution.py:106
  373.8 3.9 copy-start.10
  393.8 218.0 %reduce-scatter.9.cloned.1.call-start = ((), (), s32[]{:S(2)}) async-start(), calls=%async_computation.9 | async-start | bytes 1310720 | tf_op jit(solution)/shard_map/reduce_scatter | solution.py:196
  393.9 51.1 %copy-start.5 = (bf16[256,4096]{1,0:T(8,128)(2,1)S(1)}, bf16[256,4096]{1,0:T(8,128)(2,1)}, u32[]{:S(2)}) copy-start(bf16[256,4096]{1,0:T(8,128)(2,1)} %copy-done.4) | copy-start | bytes 6291460
  398.0 42.7 %collective-permute-start.9 = (bf16[256,4096]{1,0:T(8,128)(2,1)S(1)}, bf16[256,4096]{1,0:T(8,128)(2,1)S(1)}, u32[]{:S(2)}, u32[]{:S(2)}) collective-permute-start(bf16[256,4096]{1,0:T(8,128)(2,1)S(1)} %get-tuple-element.20), channel_id=1, source_target_pairs={{0,4},{4,8},{8,12},{1,5},{5,9},{9,13},{2,6},{6,10},{10,14},{3,7},{... | collective-permute-start | bytes 6291464 | tf_op jit(solution)/shard_map/ppermute | solution.py:106
  401.8 43.1 %collective-permute-start.13 = (bf16[256,4096]{1,0:T(8,128)(2,1)S(1)}, bf16[256,4096]{1,0:T(8,128)(2,1)S(1)}, u32[]{:S(2)}, u32[]{:S(2)}) collective-permute-start(bf16[256,4096]{1,0:T(8,128)(2,1)S(1)} %get-tuple-element.21), channel_id=1, source_target_pairs={{4,0},{8,4},{12,8},{5,1},{9,5},{13,9},{6,2},{10,6},{14,10},{7,3},{... | collective-permute-start | bytes 6291464 | tf_op jit(solution)/shard_map/ppermute | solution.py:106
  451.4 42.7 %collective-permute-start.16 = (bf16[256,4096]{1,0:T(8,128)(2,1)}, bf16[256,4096]{1,0:T(8,128)(2,1)}, u32[]{:S(2)}, u32[]{:S(2)}) collective-permute-start(bf16[256,4096]{1,0:T(8,128)(2,1)} %fusion.47), channel_id=1, source_target_pairs={{4,0},{8,4},{12,8},{5,1},{9,5},{13,9},{6,2},{10,6},{14,10},{7,3},{... | collective-permute-start | bytes 6291464 | tf_op jit(solution)/shard_map/ppermute | solution.py:106
  452.7 45.8 %collective-permute-start.14 = (bf16[256,4096]{1,0:T(8,128)(2,1)}, bf16[256,4096]{1,0:T(8,128)(2,1)S(1)}, u32[]{:S(2)}, u32[]{:S(2)}) collective-permute-start(bf16[256,4096]{1,0:T(8,128)(2,1)} %fusion.47), channel_id=1, source_target_pairs={{0,4},{4,8},{8,12},{1,5},{5,9},{9,13},{2,6},{6,10},{10,14},{3,7},{... | collective-permute-start | bytes 6291464 | tf_op jit(solution)/shard_map/ppermute | solution.py:106
  464.7 147.1 %reduce-scatter.13.cloned.1.call-start = ((), (), s32[]{:S(2)}) async-start(), calls=%async_computation.11 | async-start | bytes 1310720 | tf_op jit(solution)/shard_map/reduce_scatter | solution.py:196
  497.1 41.7 %collective-permute-start.17 = (bf16[256,4096]{1,0:T(8,128)(2,1)}, bf16[256,4096]{1,0:T(8,128)(2,1)}, u32[]{:S(2)}, u32[]{:S(2)}) collective-permute-start(bf16[256,4096]{1,0:T(8,128)(2,1)} %broadcast_select_fusion.1), channel_id=1, source_target_pairs={{4,0},{8,4},{5,1},{9,5},{6,2},{10,6},{7,3},{11,7},{20,16},{24,20},... | collective-permute-start | bytes 6291464 | tf_op jit(solution)/shard_map/ppermute | solution.py:106
  498.4 2.0 copy-start.2
  500.4 40.2 %collective-permute-start.15 = (bf16[256,4096]{1,0:T(8,128)(2,1)}, bf16[256,4096]{1,0:T(8,128)(2,1)}, u32[]{:S(2)}, u32[]{:S(2)}) collective-permute-start(bf16[256,4096]{1,0:T(8,128)(2,1)} %broadcast_select_fusion.6), channel_id=1, source_target_pairs={{4,8},{8,12},{5,9},{9,13},{6,10},{10,14},{7,11},{11,15},{20,24},{2... | collective-permute-start | bytes 6291464 | tf_op jit(solution)/shard_map/ppermute | solution.py:106
  502.5 8.0 %copy-start.11 = (bf16[256,4096]{1,0:T(8,128)(2,1)S(1)}, bf16[256,4096]{1,0:T(8,128)(2,1)}, u32[]{:S(2)}) copy-start(bf16[256,4096]{1,0:T(8,128)(2,1)} %copy-done.10) | copy-start | bytes 6291460
  510.0 101.8 %reduce-scatter.11.cloned.1.call-start = ((), (), s32[]{:S(2)}) async-start(), calls=%async_computation.10 | async-start | bytes 1310720 | tf_op jit(solution)/shard_map/reduce_scatter | solution.py:196
  531.9 80.0 %reduce-scatter.15.cloned.1.call-start = ((), (), s32[]{:S(2)}) async-start(), calls=%async_computation.12 | async-start | bytes 1310720 | tf_op jit(solution)/shard_map/reduce_scatter | solution.py:196
  542.1 17.8 %collective-permute-start.18 = (bf16[256,4096]{1,0:T(8,128)(2,1)}, bf16[256,4096]{1,0:T(8,128)(2,1)}, u32[]{:S(2)}, u32[]{:S(2)}) collective-permute-start(bf16[256,4096]{1,0:T(8,128)(2,1)} %broadcast_select_fusion.8), channel_id=1, source_target_pairs={{8,12},{9,13},{10,14},{11,15},{24,28},{25,29},{26,30},{27,31}} | collective-permute-start | bytes 6291464 | tf_op jit(solution)/shard_map/ppermute | solution.py:106
  544.1 41.8 %collective-permute-start.19 = (bf16[256,4096]{1,0:T(8,128)(2,1)S(1)}, bf16[256,4096]{1,0:T(8,128)(2,1)}, u32[]{:S(2)}, u32[]{:S(2)}) collective-permute-start(bf16[256,4096]{1,0:T(8,128)(2,1)S(1)} %broadcast_select_fusion.4), channel_id=1, source_target_pairs={{4,0},{5,1},{6,2},{7,3},{20,16},{21,17},{22,18},{23,19}} | collective-permute-start | bytes 6291464 | tf_op jit(solution)/shard_map/ppermute | solution.py:106
  547.8 1.4 copy-start.8
  555.9 64.4 %reduce-scatter.17.cloned.1.call-start = ((), (), s32[]{:S(2)}) async-start(), calls=%async_computation.13 | async-start | bytes 1310720 | tf_op jit(solution)/shard_map/reduce_scatter | solution.py:196
  593.3 2.2 copy-start.3
  595.5 2.2 copy-start.9
  611.8 10.1 %copy-start.14 = (f32[256,256]{1,0:T(8,128)S(1)}, f32[256,256]{1,0:T(8,128)}, u32[]{:S(2)}) copy-start(f32[256,256]{1,0:T(8,128)} %reduce-scatter.9.cloned.1.call-done) | copy-start | bytes 786436
  611.8 10.0 %copy-start.15 = (f32[256,256]{1,0:T(8,128)S(1)}, f32[256,256]{1,0:T(8,128)}, u32[]{:S(2)}) copy-start(f32[256,256]{1,0:T(8,128)} %reduce-scatter.13.cloned.1.call-done) | copy-start | bytes 786436
  611.9 10.0 %copy-start.16 = (f32[256,256]{1,0:T(8,128)S(1)}, f32[256,256]{1,0:T(8,128)}, u32[]{:S(2)}) copy-start(f32[256,256]{1,0:T(8,128)} %reduce-scatter.11.cloned.1.call-done) | copy-start | bytes 786436
  611.9 10.0 %copy-start.17 = (f32[256,256]{1,0:T(8,128)S(1)}, f32[256,256]{1,0:T(8,128)}, u32[]{:S(2)}) copy-start(f32[256,256]{1,0:T(8,128)} %reduce-scatter.15.cloned.1.call-done) | copy-start | bytes 786436
  620.4 1.5 copy-start.18
  (2 other events, 2.7 us)
Sparse Core Ops, SparseCore 0:
  9.6 25.5 all-gather.2
  36.7 22.8 all-gather.4
  394.0 42.4 reduce-scatter.6
  464.9 23.1 reduce-scatter.8
  510.1 27.6 reduce-scatter.12
  540.4 24.8 reduce-scatter.10
  567.8 24.8 reduce-scatter.14
  595.4 24.8 reduce-scatter.16

commit v2 on v1

--- a/solution.py
+++ b/solution.py
@@ -157,12 +157,15 @@
     grad_turned = rotate_rows(grad_rows, turn)
     activation = act_gather.result()
     out_part = jnp.dot(activation, down_tile, preferred_element_type=jnp.float32)
-    out_sum = lax.psum_scatter(out_part, "p", scatter_dimension=1, tiled=True)
     grad_down = lax.dot_general(
         activation, grad_turned, (((0,), (0,)), ((), ())), preferred_element_type=jnp.float32
     ).astype(jnp.bfloat16)
     if count > 1:
         run_slot([(grad_sum, count - 2)])
+        grad_sum.up_in, grad_sum.down_in, out_part = lax.optimization_barrier(
+            (grad_sum.up_in, grad_sum.down_in, out_part)
+        )
+    out_sum = lax.psum_scatter(out_part, "p", scatter_dimension=1, tiled=True)
     act_grad = grad_sum.result()
     pre_gather = LineGather((act_grad * gelu_slope(preact)).astype(jnp.bfloat16))
     for step in range(count - 1):

time: 635 us -> 627 us (0.987)
  waiting for transfers between devices: 366 us -> 342 us
  starting transfers between devices: 64.1 us -> 75.1 us
    ppermute x20, waiting for transfers between devices: 330 us -> 305 us  [run_slot(): received.append(lax.ppermute(combined, 'r', pairs))]
    ppermute x20, starting transfers between devices: 63.2 us -> 74 us  [run_slot(): received.append(lax.ppermute(combined, 'r', pairs))]
  transfers between devices with their start and end apart: 28 -> 28, of which waited for: 17 -> 18; matrix products, arithmetic and copies ran while one was open for 21% -> 23% of each run, Pallas kernels for 0% -> 0%
where the time goes in v2:
time: 627 us; the launch traced here: 623 us
  waiting for transfers between devices  342 us (55%)
  matrix products  120 us (19%)
  starting transfers between devices  75.1 us (12%)
  other arithmetic  61.4 us (10%)
  between operations  14.8 us (2%)
  local copies, waits for them, and re-layouts  9.26 us (1%)
    ppermute x20, waiting for transfers between devices, run_slot(): received.append(lax.ppermute(combined, 'r', pairs))  305 us
    ppermute x20, starting transfers between devices, run_slot(): received.append(lax.ppermute(combined, 'r', pairs))  74 us
    dot_general x5, matrix products, on_device(): lax.dot_general(piece, up_tile, (((1,), (1,)), ((), ())), preferred_eleme...  37.4 us
    all_gather x1, waiting for transfers between devices, on_device(): x_rows = lax.all_gather(hidden_in, 'p', axis=1, tiled=True)  26.4 us
    convert_element_type x3, other arithmetic, payload(): return (up.astype(jnp.bfloat16), down.astype(jnp.bfloat16))  15.6 us
    dot_general x1, matrix products, on_device(): lax.dot_general(grad_rows, down_tile, (((1,), (1,)), ((), ())), preferred...  14.8 us
    dot_general x1, matrix products, on_device(): jnp.dot(activation, down_tile, preferred_element_type=jnp.float32)  14.8 us
    dot_general x2, matrix products, block_terms(): jnp.dot(x_block, up_tile, preferred_element_type=jnp.float32)  14.5 us
  transfers between devices with their start and end apart: 28, of which 18 were waited for; matrix products, arithmetic and copies ran while one was open for 23% of the time, Pallas kernels for 0%

profile of v2, /device:TPU:0, one launch (start us, length us, event | category | flops | bytes accessed | tf_op | source)
XLA Modules:
  0.0 622.9 jit_solution(10841979687824546355)
XLA Ops:
  8.7 26.4 %all-gather.3.cloned.1.call-done = bf16[1024,1024]{1,0:T(8,128)(2,1)} async-done(((bf16[1024,256]{1,0:T(8,128)(2,1)}), bf16[1024,1024]{1,0:T(8,128)(2,1)}) %all-gather.3.cloned.1.call-update) | async-done | bytes 2097168 | tf_op jit(solution)/shard_map/all_gather | solution.py:124
  35.1 7.4 %fusion.36 = bf16[256,4096]{1,0:T(8,128)(2,1)} fusion(bf16[1,1024,4096]{2,1,0:T(8,128)(2,1)} %param.5, bf16[1024,1024]{1,0:T(8,128)(2,1)} %all-gather.3.cloned.1.call-done, s32[]{:T(128)S(6)} %select_n.295), kind=kOutput, calls=%fused_computation.34 | convolution fusion | flops 2148532224 | bytes 11010052 | tf_op jit(solution)/shard_map/dot_general | solution.py:139
  42.5 3.8 collective-permute-start
  46.3 7.1 %fusion.39 = bf16[256,4096]{1,0:T(8,128)(2,1)} fusion(bf16[1,1024,4096]{2,1,0:T(8,128)(2,1)} %param.5, bf16[1024,1024]{1,0:T(8,128)(2,1)S(1)} %copy-done.16, s32[]{:T(128)S(6)} %select_n.298), kind=kOutput, calls=%fused_computation.35 | convolution fusion | flops 2148532224 | bytes 11010052 | tf_op jit(solution)/shard_map/dot_general | solution.py:139
  53.4 2.5 collective-permute-start.1
  55.9 10.8 %fusion.28 = bf16[1024,4096]{1,0:T(8,128)(2,1)} fusion(bf16[1024,1024]{1,0:T(8,128)(2,1)S(1)} %copy-done.16, bf16[1,1024,4096]{2,1,0:T(8,128)(2,1)S(1)} %bitcast.94), kind=kOutput, calls=%fused_computation.30 | convolution fusion | flops 8594128896 | bytes 18874368 | tf_op jit(solution)/shard_map/dot_general | solution.py:125
  66.7 14.8 %fusion.31 = bf16[1024,4096]{1,0:T(8,128)(2,1)} fusion(bf16[1024,1024]{1,0:T(8,128)(2,1)} %all-gather.5.cloned.1.call-done, bf16[1,4096,1024]{2,1,0:T(8,128)(2,1)} %param.6), kind=kOutput, calls=%fused_computation.31 | convolution fusion | flops 8594128896 | bytes 18874368 | tf_op jit(solution)/shard_map/dot_general | solution.py:127
  81.5 10.2 %collective-permute-done = bf16[256,4096]{1,0:T(8,128)(2,1)S(1)} collective-permute-done((bf16[256,4096]{1,0:T(8,128)(2,1)}, bf16[256,4096]{1,0:T(8,128)(2,1)S(1)}, u32[]{:S(2)}, u32[]{:S(2)}) %collective-permute-start) | collective-permute-done | bytes 2097184 | tf_op jit(solution)/shard_map/ppermute | solution.py:106
  92.3 2.8 copy-done
  95.1 3.5 fusion.57
  98.6 4.4 collective-permute-start.2
  105.1 42.6 %collective-permute-done.2 = bf16[256,4096]{1,0:T(8,128)(2,1)S(1)} collective-permute-done((bf16[256,4096]{1,0:T(8,128)(2,1)}, bf16[256,4096]{1,0:T(8,128)(2,1)S(1)}, u32[]{:S(2)}, u32[]{:S(2)}) %collective-permute-start.2) | collective-permute-done | bytes 2097184 | tf_op jit(solution)/shard_map/ppermute | solution.py:106
  147.7 5.9 fusion.56
  154.9 17.4 %collective-permute-start.3 = (bf16[256,4096]{1,0:T(8,128)(2,1)}, bf16[256,4096]{1,0:T(8,128)(2,1)}, u32[]{:S(2)}, u32[]{:S(2)}) collective-permute-start(bf16[256,4096]{1,0:T(8,128)(2,1)} %get-tuple-element.32), channel_id=1, source_target_pairs={{0,4},{4,8},{8,12},{1,5},{5,9},{9,13},{2,6},{6,10},{10,14},{3,7},{... | collective-permute-start | bytes 6291464 | tf_op jit(solution)/shard_map/ppermute | solution.py:106
  172.4 40.9 %collective-permute-done.5 = bf16[256,4096]{1,0:T(8,128)(2,1)S(1)} collective-permute-done((bf16[256,4096]{1,0:T(8,128)(2,1)}, bf16[256,4096]{1,0:T(8,128)(2,1)S(1)}, u32[]{:S(2)}, u32[]{:S(2)}) %collective-permute-start.5) | collective-permute-done | bytes 2097184 | tf_op jit(solution)/shard_map/ppermute | solution.py:106
  214.7 3.9 multiply_convert_fusion
  219.9 6.8 %collective-permute-start.6 = (bf16[256,4096]{1,0:T(8,128)(2,1)}, bf16[256,4096]{1,0:T(8,128)(2,1)}, u32[]{:S(2)}, u32[]{:S(2)}) collective-permute-start(bf16[256,4096]{1,0:T(8,128)(2,1)} %multiply_convert_fusion), channel_id=1, source_target_pairs={{0,4},{4,8},{8,12},{1,5},{5,9},{9,13},{2,6},{6,10},{10,14},{3,7},{... | collective-permute-start | bytes 6291464 | tf_op jit(solution)/shard_map/ppermute | solution.py:106
  226.6 39.9 %collective-permute-done.10 = bf16[256,4096]{1,0:T(8,128)(2,1)S(1)} collective-permute-done((bf16[256,4096]{1,0:T(8,128)(2,1)}, bf16[256,4096]{1,0:T(8,128)(2,1)S(1)}, u32[]{:S(2)}, u32[]{:S(2)}) %collective-permute-start.10) | collective-permute-done | bytes 2097184 | tf_op jit(solution)/shard_map/ppermute | solution.py:106
  267.8 4.7 bitcast_select_fusion
  273.8 7.0 %collective-permute-start.7 = (bf16[256,4096]{1,0:T(8,128)(2,1)}, bf16[256,4096]{1,0:T(8,128)(2,1)}, u32[]{:S(2)}, u32[]{:S(2)}) collective-permute-start(bf16[256,4096]{1,0:T(8,128)(2,1)} %get-tuple-element.31), channel_id=1, source_target_pairs={{4,8},{8,12},{0,4},{5,9},{9,13},{1,5},{6,10},{10,14},{2,6},{7,11},... | collective-permute-start | bytes 6291464 | tf_op jit(solution)/shard_map/ppermute | solution.py:106
  280.9 39.2 %collective-permute-done.11 = bf16[256,4096]{1,0:T(8,128)(2,1)} collective-permute-done((bf16[256,4096]{1,0:T(8,128)(2,1)}, bf16[256,4096]{1,0:T(8,128)(2,1)}, u32[]{:S(2)}, u32[]{:S(2)}) %collective-permute-start.11) | collective-permute-done | bytes 2097184 | tf_op jit(solution)/shard_map/ppermute | solution.py:106
  321.2 4.5 fusion.59
  327.1 5.1 collective-permute-start.8
  332.2 39.2 %collective-permute-done.12 = bf16[256,4096]{1,0:T(8,128)(2,1)S(1)} collective-permute-done((bf16[256,4096]{1,0:T(8,128)(2,1)S(1)}, bf16[256,4096]{1,0:T(8,128)(2,1)S(1)}, u32[]{:S(2)}, u32[]{:S(2)}) %collective-permute-start.12) | collective-permute-done | bytes 2097184 | tf_op jit(solution)/shard_map/ppermute | solution.py:106
  372.6 6.2 fusion.49
  378.8 5.7 collective-permute-start.9
  388.0 14.8 %fusion.8 = f32[1024,1024]{1,0:T(8,128)} fusion(bf16[1,4096,1024]{2,1,0:T(8,128)(2,1)} %param.6, bf16[256,4096]{1,0:T(8,128)(2,1)S(1)} %select_add_fusion, bf16[256,4096]{1,0:T(8,128)(2,1)S(1)} %get-tuple-element.36, bf16[256,4096]{1,0:T(8,128)(2,1)S(1)} %select_add_fusion.1, bf16[256,4096]{1,0:T(8,128)(2,1)} %multiply_convert_fusion), kind=kOutput, calls=%fused_computation.9 | convolution fusion | flops 8623489024 | bytes 20971520 | tf_op jit(solution)/shard_map/dot_general | solution.py:159
  402.8 20.3 %collective-permute-done.9 = bf16[256,4096]{1,0:T(8,128)(2,1)} collective-permute-done((bf16[256,4096]{1,0:T(8,128)(2,1)}, bf16[256,4096]{1,0:T(8,128)(2,1)}, u32[]{:S(2)}, u32[]{:S(2)}) %collective-permute-start.9) | collective-permute-done | bytes 2097184 | tf_op jit(solution)/shard_map/ppermute | solution.py:106
  423.0 2.3 select_convert_fusion.1
  425.3 3.1 collective-permute-done.13
  428.4 3.9 select_convert_fusion
  434.0 8.2 %fusion.47 = bf16[256,4096]{1,0:T(8,128)(2,1)} fusion(f32[256,4096]{1,0:T(8,128)} %select_convert_fusion, f32[256,4096]{1,0:T(8,128)} %select_convert_fusion.1, bf16[4,256,4096]{2,1,0:T(8,128)(2,1)} %bitcast.88, s32[]{:T(128)S(6)} %select_n.302, bf16[256,4096]{1,0:T(8,128)(2,1)S(1)} %copy-done.4, pred[]{:T(512)S(6)} %and.26, ...), kind=kLoop, calls=%fused_computation.41 | loop fusion | flops 20971520 | bytes 18874374 | tf_op jit(solution)/shard_map/convert_element_type | solution.py:170
  442.1 5.0 collective-permute-start.14
  448.5 8.1 %fusion.20 = f32[256,1024]{1,0:T(8,128)} fusion(bf16[256,4096]{1,0:T(8,128)(2,1)} %fusion.47, bf16[1,1024,4096]{2,1,0:T(8,128)(2,1)} %param.5), kind=kOutput, calls=%fused_computation.21 | convolution fusion | flops 2147483648 | bytes 11534336 | tf_op jit(solution)/shard_map/dot_general | solution.py:196
  456.6 26.9 %collective-permute-done.14 = bf16[256,4096]{1,0:T(8,128)(2,1)} collective-permute-done((bf16[256,4096]{1,0:T(8,128)(2,1)}, bf16[256,4096]{1,0:T(8,128)(2,1)}, u32[]{:S(2)}, u32[]{:S(2)}) %collective-permute-start.14) | collective-permute-done | bytes 2097184 | tf_op jit(solution)/shard_map/ppermute | solution.py:106
  492.2 7.7 %fusion.16 = f32[256,1024]{1,0:T(8,128)} fusion(bf16[256,4096]{1,0:T(8,128)(2,1)} %broadcast_select_fusion.1, bf16[1,1024,4096]{2,1,0:T(8,128)(2,1)} %param.5), kind=kOutput, calls=%fused_computation.17 | convolution fusion | flops 2147483648 | bytes 11534336 | tf_op jit(solution)/shard_map/dot_general | solution.py:196
  500.3 14.0 %convolution_convert_fusion = bf16[4096,1024]{1,0:T(8,128)(2,1)} fusion(s32[]{:T(128)S(6)} %select_n.327, bf16[1024,1024]{1,0:T(8,128)(2,1)} %all-gather.5.cloned.1.call-done, bf16[256,4096]{1,0:T(8,128)(2,1)S(1)} %copy-done.8, bf16[256,4096]{1,0:T(8,128)(2,1)} %copy-done.10, bf16[256,4096]{1,0:T(8,128)(2,1)} %copy-done.9, ...), kind=kOutput, calls=%fused_computation.32 | convolution fusion | flops 8631877632 | bytes 18874372 | tf_op jit(solution)/shard_map/dot_general | solution.py:160
  514.3 7.4 %fusion.18 = f32[256,1024]{1,0:T(8,128)} fusion(bf16[256,4096]{1,0:T(8,128)(2,1)} %broadcast_select_fusion.6, bf16[1,1024,4096]{2,1,0:T(8,128)(2,1)} %param.5), kind=kOutput, calls=%fused_computation.19 | convolution fusion | flops 2147483648 | bytes 11534336 | tf_op jit(solution)/shard_map/dot_general | solution.py:196
  521.9 15.4 %collective-permute-done.17 = bf16[256,4096]{1,0:T(8,128)(2,1)} collective-permute-done((bf16[256,4096]{1,0:T(8,128)(2,1)}, bf16[256,4096]{1,0:T(8,128)(2,1)}, u32[]{:S(2)}, u32[]{:S(2)}) %collective-permute-start.17) | collective-permute-done | bytes 2097184 | tf_op jit(solution)/shard_map/ppermute | solution.py:106
  537.3 3.2 broadcast_select_fusion.4
  541.8 2.0 collective-permute-start.18
  543.8 2.4 add.237
  547.5 6.9 %fusion.14 = f32[256,1024]{1,0:T(8,128)} fusion(bf16[256,4096]{1,0:T(8,128)(2,1)S(1)} %add.237, bf16[1,1024,4096]{2,1,0:T(8,128)(2,1)} %param.5), kind=kOutput, calls=%fused_computation.15 | convolution fusion | flops 2147483648 | bytes 11534336 | tf_op jit(solution)/shard_map/dot_general | solution.py:196
  555.9 2.5 fusion.70
  558.4 20.9 %collective-permute-done.19 = bf16[256,4096]{1,0:T(8,128)(2,1)} collective-permute-done((bf16[256,4096]{1,0:T(8,128)(2,1)}, bf16[256,4096]{1,0:T(8,128)(2,1)}, u32[]{:S(2)}, u32[]{:S(2)}) %collective-permute-start.19) | collective-permute-done | bytes 2097184 | tf_op jit(solution)/shard_map/ppermute | solution.py:106
  579.3 7.4 %fusion.12 = f32[256,1024]{1,0:T(8,128)} fusion(bf16[1,1024,4096]{2,1,0:T(8,128)(2,1)} %param.5, bf16[256,4096]{1,0:T(8,128)(2,1)} %collective-permute-done.19, pred[]{:T(512)S(6)} %and.24, bf16[256,4096]{1,0:T(8,128)(2,1)} %collective-permute-done.18, pred[]{:T(512)S(6)} %and.27), kind=kOutput, calls=%fused_computation.13 | convolution fusion | flops 2150629376 | bytes 13631490 | tf_op jit(solution)/shard_map/dot_general | solution.py:196
  590.5 14.1 %convert_bitcast_fusion = bf16[1,1024,4096]{2,1,0:T(8,128)(2,1)} fusion(bf16[256,4096]{1,0:T(8,128)(2,1)S(1)} %fusion.66, bf16[256,4096]{1,0:T(8,128)(2,1)S(1)} %copy-done.6, bf16[256,4096]{1,0:T(8,128)(2,1)S(1)} %fusion.67, bf16[256,4096]{1,0:T(8,128)(2,1)} %fusion.47, s32[]{:T(128)S(6)} %select_n.327, bf16[1024,1024]{1,0:T(8,128)(2,1)} %all-gather.3.cloned.1.call-done), kind=kOutput, calls=%fused_computation.29 | convolution fusion | flops 8631877632 | bytes 18874372 | tf_op jit(solution)/shard_map/dot_general | solution.py:182
  604.7 8.6 %reduce-scatter.17.cloned.1.call-done = f32[256,256]{1,0:T(8,128)} async-done(((f32[256,1024]{1,0:T(8,128)}), f32[256,256]{1,0:T(8,128)}) %reduce-scatter.17.cloned.1.call-update) | async-done | bytes 262160 | tf_op jit(solution)/shard_map/reduce_scatter | solution.py:199
  (92 shorter events, 40.3 us)
Async XLA Ops:
  7.2 28.0 %all-gather.3.cloned.1.call-start = ((), (), s32[]{:S(2)}) async-start(), calls=%async_computation.6 | async-start | bytes 2621440 | tf_op jit(solution)/shard_map/all_gather | solution.py:124
  7.9 58.8 %all-gather.5.cloned.1.call-start = ((), (), s32[]{:S(2)}) async-start(), calls=%async_computation.7 | async-start | bytes 2621440 | tf_op jit(solution)/shard_map/all_gather | solution.py:126
  8.6 531.9 %reduce-scatter.7.cloned.1.call-start = ((), (), s32[]{:S(2)}) async-start(), calls=%async_computation.8 | async-start | bytes 5242880 | tf_op jit(solution)/shard_map/reduce_scatter | solution.py:168
  35.1 11.2 %copy-start.16 = (bf16[1024,1024]{1,0:T(8,128)(2,1)S(1)}, bf16[1024,1024]{1,0:T(8,128)(2,1)}, u32[]{:S(2)}) copy-start(bf16[1024,1024]{1,0:T(8,128)(2,1)} %all-gather.3.cloned.1.call-done) | copy-start | bytes 6291460
  35.1 20.7 %slice-start = ((s8[8388608]{0:T(1024)(128)(4,1)}), s8[4194304]{0:T(1024)(128)(4,1)S(1)}, s32[]{:S(2)}) async-start(s8[8388608]{0:T(1024)(128)(4,1)} %bitcast.93), calls=%async_computation.14 | async-start | bytes 8388608
  42.5 13.4 %slice-start.1 = ((s8[8388608]{0:T(1024)(128)(4,1)}), s8[4194304]{0:T(1024)(128)(4,1)S(1)}, s32[]{:S(2)}) async-start(s8[8388608]{0:T(1024)(128)(4,1)} %bitcast.93), calls=%async_computation.15 | async-start | bytes 8388608
  42.5 49.3 %collective-permute-start = (bf16[256,4096]{1,0:T(8,128)(2,1)}, bf16[256,4096]{1,0:T(8,128)(2,1)S(1)}, u32[]{:S(2)}, u32[]{:S(2)}) collective-permute-start(bf16[256,4096]{1,0:T(8,128)(2,1)} %fusion.36), channel_id=1, source_target_pairs={{0,4},{1,5},{2,6},{3,7},{16,20},{17,21},{18,22},{19,23}} | collective-permute-start | bytes 6291464 | tf_op jit(solution)/shard_map/ppermute | solution.py:106
  53.4 38.6 %collective-permute-start.1 = (bf16[256,4096]{1,0:T(8,128)(2,1)}, bf16[256,4096]{1,0:T(8,128)(2,1)}, u32[]{:S(2)}, u32[]{:S(2)}) collective-permute-start(bf16[256,4096]{1,0:T(8,128)(2,1)} %fusion.39), channel_id=1, source_target_pairs={{12,8},{13,9},{14,10},{15,11},{28,24},{29,25},{30,26},{31,27}} | collective-permute-start | bytes 6291464 | tf_op jit(solution)/shard_map/ppermute | solution.py:106
  91.8 3.4 copy-start
  98.6 49.1 %collective-permute-start.2 = (bf16[256,4096]{1,0:T(8,128)(2,1)}, bf16[256,4096]{1,0:T(8,128)(2,1)S(1)}, u32[]{:S(2)}, u32[]{:S(2)}) collective-permute-start(bf16[256,4096]{1,0:T(8,128)(2,1)} %get-tuple-element.34), channel_id=1, source_target_pairs={{0,4},{4,8},{1,5},{5,9},{2,6},{6,10},{3,7},{7,11},{16,20},{20,24},... | collective-permute-start | bytes 6291464 | tf_op jit(solution)/shard_map/ppermute | solution.py:106
  103.1 44.7 %collective-permute-start.4 = (bf16[256,4096]{1,0:T(8,128)(2,1)}, bf16[256,4096]{1,0:T(8,128)(2,1)}, u32[]{:S(2)}, u32[]{:S(2)}) collective-permute-start(bf16[256,4096]{1,0:T(8,128)(2,1)} %get-tuple-element.35), channel_id=1, source_target_pairs={{8,4},{12,8},{9,5},{13,9},{10,6},{14,10},{11,7},{15,11},{24,20},{2... | collective-permute-start | bytes 6291464 | tf_op jit(solution)/shard_map/ppermute | solution.py:106
  153.6 59.6 %collective-permute-start.5 = (bf16[256,4096]{1,0:T(8,128)(2,1)}, bf16[256,4096]{1,0:T(8,128)(2,1)S(1)}, u32[]{:S(2)}, u32[]{:S(2)}) collective-permute-start(bf16[256,4096]{1,0:T(8,128)(2,1)} %get-tuple-element.33), channel_id=1, source_target_pairs={{4,0},{8,4},{12,8},{5,1},{9,5},{13,9},{6,2},{10,6},{14,10},{7,3},{... | collective-permute-start | bytes 6291464 | tf_op jit(solution)/shard_map/ppermute | solution.py:106
  154.9 59.6 %collective-permute-start.3 = (bf16[256,4096]{1,0:T(8,128)(2,1)}, bf16[256,4096]{1,0:T(8,128)(2,1)}, u32[]{:S(2)}, u32[]{:S(2)}) collective-permute-start(bf16[256,4096]{1,0:T(8,128)(2,1)} %get-tuple-element.32), channel_id=1, source_target_pairs={{0,4},{4,8},{8,12},{1,5},{5,9},{9,13},{2,6},{6,10},{10,14},{3,7},{... | collective-permute-start | bytes 6291464 | tf_op jit(solution)/shard_map/ppermute | solution.py:106
  213.3 1.4 copy-start.3
  218.6 47.9 %collective-permute-start.10 = (bf16[256,4096]{1,0:T(8,128)(2,1)}, bf16[256,4096]{1,0:T(8,128)(2,1)S(1)}, u32[]{:S(2)}, u32[]{:S(2)}) collective-permute-start(bf16[256,4096]{1,0:T(8,128)(2,1)} %multiply_convert_fusion), channel_id=1, source_target_pairs={{4,0},{8,4},{12,8},{5,1},{9,5},{13,9},{6,2},{10,6},{14,10},{7,3},{... | collective-permute-start | bytes 6291464 | tf_op jit(solution)/shard_map/ppermute | solution.py:106
  219.9 47.9 %collective-permute-start.6 = (bf16[256,4096]{1,0:T(8,128)(2,1)}, bf16[256,4096]{1,0:T(8,128)(2,1)}, u32[]{:S(2)}, u32[]{:S(2)}) collective-permute-start(bf16[256,4096]{1,0:T(8,128)(2,1)} %multiply_convert_fusion), channel_id=1, source_target_pairs={{0,4},{4,8},{8,12},{1,5},{5,9},{9,13},{2,6},{6,10},{10,14},{3,7},{... | collective-permute-start | bytes 6291464 | tf_op jit(solution)/shard_map/ppermute | solution.py:106
  272.5 47.5 %collective-permute-start.11 = (bf16[256,4096]{1,0:T(8,128)(2,1)}, bf16[256,4096]{1,0:T(8,128)(2,1)}, u32[]{:S(2)}, u32[]{:S(2)}) collective-permute-start(bf16[256,4096]{1,0:T(8,128)(2,1)} %get-tuple-element.30), channel_id=1, source_target_pairs={{4,0},{8,4},{12,8},{5,1},{9,5},{13,9},{6,2},{10,6},{14,10},{7,3},{... | collective-permute-start | bytes 6291464 | tf_op jit(solution)/shard_map/ppermute | solution.py:106
  273.8 47.4 %collective-permute-start.7 = (bf16[256,4096]{1,0:T(8,128)(2,1)}, bf16[256,4096]{1,0:T(8,128)(2,1)}, u32[]{:S(2)}, u32[]{:S(2)}) collective-permute-start(bf16[256,4096]{1,0:T(8,128)(2,1)} %get-tuple-element.31), channel_id=1, source_target_pairs={{4,8},{8,12},{0,4},{5,9},{9,13},{1,5},{6,10},{10,14},{2,6},{7,11},... | collective-permute-start | bytes 6291464 | tf_op jit(solution)/shard_map/ppermute | solution.py:106
  325.8 60.5 %copy-start.10 = (bf16[256,4096]{1,0:T(8,128)(2,1)}, bf16[256,4096]{1,0:T(8,128)(2,1)S(1)}, u32[]{:S(2)}) copy-start(bf16[256,4096]{1,0:T(8,128)(2,1)S(1)} %get-tuple-element.36) | copy-start | bytes 6291460
  325.8 45.7 %collective-permute-start.12 = (bf16[256,4096]{1,0:T(8,128)(2,1)S(1)}, bf16[256,4096]{1,0:T(8,128)(2,1)S(1)}, u32[]{:S(2)}, u32[]{:S(2)}) collective-permute-start(bf16[256,4096]{1,0:T(8,128)(2,1)S(1)} %get-tuple-element.28), channel_id=1, source_target_pairs={{4,0},{8,4},{12,8},{5,1},{9,5},{13,9},{6,2},{10,6},{14,10},{7,3},{... | collective-permute-start | bytes 6291464 | tf_op jit(solution)/shard_map/ppermute | solution.py:106
  327.1 45.5 %collective-permute-start.8 = (bf16[256,4096]{1,0:T(8,128)(2,1)S(1)}, bf16[256,4096]{1,0:T(8,128)(2,1)S(1)}, u32[]{:S(2)}, u32[]{:S(2)}) collective-permute-start(bf16[256,4096]{1,0:T(8,128)(2,1)S(1)} %get-tuple-element.29), channel_id=1, source_target_pairs={{8,12},{0,4},{4,8},{9,13},{1,5},{5,9},{10,14},{2,6},{6,10},{11,15}... | collective-permute-start | bytes 6291464 | tf_op jit(solution)/shard_map/ppermute | solution.py:106
  378.8 44.3 %collective-permute-start.9 = (bf16[256,4096]{1,0:T(8,128)(2,1)}, bf16[256,4096]{1,0:T(8,128)(2,1)}, u32[]{:S(2)}, u32[]{:S(2)}) collective-permute-start(bf16[256,4096]{1,0:T(8,128)(2,1)} %get-tuple-element.27), channel_id=1, source_target_pairs={{0,4},{4,8},{8,12},{1,5},{5,9},{9,13},{2,6},{6,10},{10,14},{3,7},{... | collective-permute-start | bytes 6291464 | tf_op jit(solution)/shard_map/ppermute | solution.py:106
  384.4 44.0 %collective-permute-start.13 = (bf16[256,4096]{1,0:T(8,128)(2,1)}, bf16[256,4096]{1,0:T(8,128)(2,1)}, u32[]{:S(2)}, u32[]{:S(2)}) collective-permute-start(bf16[256,4096]{1,0:T(8,128)(2,1)} %get-tuple-element.26), channel_id=1, source_target_pairs={{4,0},{8,4},{12,8},{5,1},{9,5},{13,9},{6,2},{10,6},{14,10},{7,3},{... | collective-permute-start | bytes 6291464 | tf_op jit(solution)/shard_map/ppermute | solution.py:106
  386.0 1.4 copy-start.7
  386.3 1.7 copy-start.9
  432.4 1.6 copy-start.4
  432.4 172.1 %reduce-scatter.9.cloned.1.call-start = ((), (), s32[]{:S(2)}) async-start(), calls=%async_computation.9 | async-start | bytes 1310720 | tf_op jit(solution)/shard_map/reduce_scatter | solution.py:199
  442.1 41.4 %collective-permute-start.14 = (bf16[256,4096]{1,0:T(8,128)(2,1)}, bf16[256,4096]{1,0:T(8,128)(2,1)}, u32[]{:S(2)}, u32[]{:S(2)}) collective-permute-start(bf16[256,4096]{1,0:T(8,128)(2,1)} %fusion.47), channel_id=1, source_target_pairs={{0,4},{4,8},{8,12},{1,5},{5,9},{9,13},{2,6},{6,10},{10,14},{3,7},{... | collective-permute-start | bytes 6291464 | tf_op jit(solution)/shard_map/ppermute | solution.py:106
  447.2 41.7 %collective-permute-start.16 = (bf16[256,4096]{1,0:T(8,128)(2,1)}, bf16[256,4096]{1,0:T(8,128)(2,1)S(1)}, u32[]{:S(2)}, u32[]{:S(2)}) collective-permute-start(bf16[256,4096]{1,0:T(8,128)(2,1)} %fusion.47), channel_id=1, source_target_pairs={{4,0},{8,4},{12,8},{5,1},{9,5},{13,9},{6,2},{10,6},{14,10},{7,3},{... | collective-permute-start | bytes 6291464 | tf_op jit(solution)/shard_map/ppermute | solution.py:106
  456.5 148.0 %reduce-scatter.13.cloned.1.call-start = ((), (), s32[]{:S(2)}) async-start(), calls=%async_computation.11 | async-start | bytes 1310720 | tf_op jit(solution)/shard_map/reduce_scatter | solution.py:199
  485.0 36.8 %collective-permute-start.15 = (bf16[256,4096]{1,0:T(8,128)(2,1)}, bf16[256,4096]{1,0:T(8,128)(2,1)}, u32[]{:S(2)}, u32[]{:S(2)}) collective-permute-start(bf16[256,4096]{1,0:T(8,128)(2,1)} %broadcast_select_fusion.6), channel_id=1, source_target_pairs={{4,8},{8,12},{5,9},{9,13},{6,10},{10,14},{7,11},{11,15},{20,24},{2... | collective-permute-start | bytes 6291464 | tf_op jit(solution)/shard_map/ppermute | solution.py:106
  488.8 2.0 copy-start.1
  490.9 46.5 %collective-permute-start.17 = (bf16[256,4096]{1,0:T(8,128)(2,1)}, bf16[256,4096]{1,0:T(8,128)(2,1)}, u32[]{:S(2)}, u32[]{:S(2)}) collective-permute-start(bf16[256,4096]{1,0:T(8,128)(2,1)} %broadcast_select_fusion.1), channel_id=1, source_target_pairs={{4,0},{8,4},{5,1},{9,5},{6,2},{10,6},{7,3},{11,7},{20,16},{24,20},... | collective-permute-start | bytes 6291464 | tf_op jit(solution)/shard_map/ppermute | solution.py:106
  492.2 8.2 %copy-start.8 = (bf16[256,4096]{1,0:T(8,128)(2,1)S(1)}, bf16[256,4096]{1,0:T(8,128)(2,1)}, u32[]{:S(2)}) copy-start(bf16[256,4096]{1,0:T(8,128)(2,1)} %copy-done.7) | copy-start | bytes 6291460
  499.9 104.7 %reduce-scatter.11.cloned.1.call-start = ((), (), s32[]{:S(2)}) async-start(), calls=%async_computation.10 | async-start | bytes 1310720 | tf_op jit(solution)/shard_map/reduce_scatter | solution.py:199
  521.7 82.9 %reduce-scatter.15.cloned.1.call-start = ((), (), s32[]{:S(2)}) async-start(), calls=%async_computation.12 | async-start | bytes 1310720 | tf_op jit(solution)/shard_map/reduce_scatter | solution.py:199
  540.5 38.7 %collective-permute-start.19 = (bf16[256,4096]{1,0:T(8,128)(2,1)}, bf16[256,4096]{1,0:T(8,128)(2,1)}, u32[]{:S(2)}, u32[]{:S(2)}) collective-permute-start(bf16[256,4096]{1,0:T(8,128)(2,1)} %broadcast_select_fusion.4), channel_id=1, source_target_pairs={{4,0},{5,1},{6,2},{7,3},{20,16},{21,17},{22,18},{23,19}} | collective-permute-start | bytes 6291464 | tf_op jit(solution)/shard_map/ppermute | solution.py:106
  541.8 37.5 %collective-permute-start.18 = (bf16[256,4096]{1,0:T(8,128)(2,1)S(1)}, bf16[256,4096]{1,0:T(8,128)(2,1)}, u32[]{:S(2)}, u32[]{:S(2)}) collective-permute-start(bf16[256,4096]{1,0:T(8,128)(2,1)S(1)} %broadcast_select_fusion.8), channel_id=1, source_target_pairs={{8,12},{9,13},{10,14},{11,15},{24,28},{25,29},{26,30},{27,31}} | collective-permute-start | bytes 6291464 | tf_op jit(solution)/shard_map/ppermute | solution.py:106
  546.2 1.3 copy-start.5
  554.5 58.8 %reduce-scatter.17.cloned.1.call-start = ((), (), s32[]{:S(2)}) async-start(), calls=%async_computation.13 | async-start | bytes 1310720 | tf_op jit(solution)/shard_map/reduce_scatter | solution.py:199
  586.7 2.2 copy-start.2
  588.9 1.6 copy-start.6
  604.6 10.2 %copy-start.11 = (f32[256,256]{1,0:T(8,128)S(1)}, f32[256,256]{1,0:T(8,128)}, u32[]{:S(2)}) copy-start(f32[256,256]{1,0:T(8,128)} %reduce-scatter.9.cloned.1.call-done) | copy-start | bytes 786436
  604.6 10.2 %copy-start.12 = (f32[256,256]{1,0:T(8,128)S(1)}, f32[256,256]{1,0:T(8,128)}, u32[]{:S(2)}) copy-start(f32[256,256]{1,0:T(8,128)} %reduce-scatter.13.cloned.1.call-done) | copy-start | bytes 786436
  604.6 10.2 %copy-start.13 = (f32[256,256]{1,0:T(8,128)S(1)}, f32[256,256]{1,0:T(8,128)}, u32[]{:S(2)}) copy-start(f32[256,256]{1,0:T(8,128)} %reduce-scatter.11.cloned.1.call-done) | copy-start | bytes 786436
  604.6 10.1 %copy-start.14 = (f32[256,256]{1,0:T(8,128)S(1)}, f32[256,256]{1,0:T(8,128)}, u32[]{:S(2)}) copy-start(f32[256,256]{1,0:T(8,128)} %reduce-scatter.15.cloned.1.call-done) | copy-start | bytes 786436
  613.3 1.5 copy-start.15
Sparse Core Ops, SparseCore 0:
  9.6 25.5 all-gather.2
  36.7 22.8 all-gather.4
  432.5 43.0 reduce-scatter.6
  478.2 24.8 reduce-scatter.8
  505.5 25.1 reduce-scatter.12
  533.2 24.8 reduce-scatter.10
  560.7 24.9 reduce-scatter.14
  588.3 24.8 reduce-scatter.16

commit v3 on v2

--- a/solution.py
+++ b/solution.py
@@ -134,11 +134,15 @@
         last = count - 1
         pos = lax.axis_index("r")
 
-        def block_terms(block):
-            x_block = lax.dynamic_slice_in_dim(x_rows, block * rows, rows, axis=0)
-            return jnp.dot(x_block, up_tile, preferred_element_type=jnp.float32).astype(jnp.bfloat16)
-
-        up_sum.first = (block_terms(jnp.clip(last + pos, 0, last)), block_terms(jnp.clip(pos - last, 0, last)))
+        first_rows = jnp.concatenate(
+            [
+                lax.dynamic_slice_in_dim(x_rows, jnp.clip(last + pos, 0, last) * rows, rows, axis=0),
+                lax.dynamic_slice_in_dim(x_rows, jnp.clip(pos - last, 0, last) * rows, rows, axis=0),
+            ],
+            axis=0,
+        )
+        first = jnp.dot(first_rows, up_tile, preferred_element_type=jnp.float32).astype(jnp.bfloat16)
+        up_sum.first = (first[:rows], first[rows:])
         run_slot([(up_sum, 0)])
         up_sum.up_in, up_sum.down_in, up_sum.shares, grad_terms = lax.optimization_barrier(
             (up_sum.up_in, up_sum.down_in, up_sum.shares, grad_terms)
@@ -150,8 +154,13 @@
     act_gather = LineGather(gelu_value(preact).astype(jnp.bfloat16))
     if count > 1:
         run_slot([(act_gather, 0)])
+    slope = gelu_slope(preact)
     for step in range(1, count - 1):
         run_slot([(act_gather, step), (grad_sum, step - 1)])
+        if step == 1:
+            grad_sum.up_in, grad_sum.down_in, slope = lax.optimization_barrier(
+                (grad_sum.up_in, grad_sum.down_in, slope)
+            )
     tokens = x_rows.shape[0]
     turn = lax.axis_index("r") * (tokens // count)
     grad_turned = rotate_rows(grad_rows, turn)
@@ -167,7 +176,7 @@
         )
     out_sum = lax.psum_scatter(out_part, "p", scatter_dimension=1, tiled=True)
     act_grad = grad_sum.result()
-    pre_gather = LineGather((act_grad * gelu_slope(preact)).astype(jnp.bfloat16))
+    pre_gather = LineGather((act_grad * slope).astype(jnp.bfloat16))
     for step in range(count - 1):
         run_slot([(pre_gather, step)])
         if step == min(1, count - 2):

time: 627 us -> 630 us (level)
  starting transfers between devices: 75.1 us -> 62.6 us
  waiting for transfers between devices: 342 us -> 353 us
    ppermute x20, starting transfers between devices: 74 us -> 62.3 us  [run_slot(): received.append(lax.ppermute(combined, 'r', pairs))]
    ppermute x20, waiting for transfers between devices: 305 us -> 313 us  [run_slot(): received.append(lax.ppermute(combined, 'r', pairs))]
    dot_general x2 -> x1, matrix products: 14.5 us -> 8.71 us  [on_device(): jnp.dot(first_rows, up_tile, preferred_element_type=jnp.float32)]
  transfers between devices with their start and end apart: 28 -> 28, of which waited for: 18 -> 16; matrix products, arithmetic and copies ran while one was open for 23% -> 25% of each run, Pallas kernels for 0% -> 0%
where the time goes in v3:
time: 630 us; the launch traced here: 621 us
  waiting for transfers between devices  353 us (56%)
  matrix products  115 us (18%)
  other arithmetic  66.7 us (11%)
  starting transfers between devices  62.6 us (10%)
  between operations  15.2 us (2%)
  local copies, waits for them, and re-layouts  7.8 us (1%)
    ppermute x20, waiting for transfers between devices, run_slot(): received.append(lax.ppermute(combined, 'r', pairs))  313 us
    ppermute x20, starting transfers between devices, run_slot(): received.append(lax.ppermute(combined, 'r', pairs))  62.3 us
    dot_general x5, matrix products, on_device(): lax.dot_general(piece, up_tile, (((1,), (1,)), ((), ())), preferred_eleme...  37.8 us
    all_gather x1, waiting for transfers between devices, on_device(): x_rows = lax.all_gather(hidden_in, 'p', axis=1, tiled=True)  26.4 us
    dot_general x1, matrix products, on_device(): jnp.dot(activation, down_tile, preferred_element_type=jnp.float32)  14.8 us
    dot_general x1, matrix products, on_device(): lax.dot_general(grad_rows, down_tile, (((1,), (1,)), ((), ())), preferred...  14.8 us
    dot_general x1, matrix products, on_device(): lax.dot_general(rotate_rows(x_rows, turn), pre_grad, (((0,), (0,)), ((),...  14.1 us
    dot_general x1, matrix products, on_device(): lax.dot_general(activation, grad_turned, (((0,), (0,)), ((), ())), prefer...  14 us
  transfers between devices with their start and end apart: 28, of which 16 were waited for; matrix products, arithmetic and copies ran while one was open for 25% of the time, Pallas kernels for 0%

profile of v3, /device:TPU:0, one launch (start us, length us, event | category | flops | bytes accessed | tf_op | source)
XLA Modules:
  0.0 621.2 jit_solution(10017567144337324446)
XLA Ops:
  8.7 26.4 %all-gather.3.cloned.1.call-done = bf16[1024,1024]{1,0:T(8,128)(2,1)} async-done(((bf16[1024,256]{1,0:T(8,128)(2,1)}), bf16[1024,1024]{1,0:T(8,128)(2,1)}) %all-gather.3.cloned.1.call-update) | async-done | bytes 2097168 | tf_op jit(solution)/shard_map/all_gather | solution.py:124
  36.6 8.7 %fusion.34 = bf16[512,4096]{1,0:T(8,128)(2,1)S(1)} fusion(bf16[1,1024,4096]{2,1,0:T(8,128)(2,1)} %param.5, bf16[256,1024]{1,0:T(8,128)(2,1)S(1)} %get-tuple-element.52, bf16[256,1024]{1,0:T(8,128)(2,1)S(1)} %get-tuple-element.51), kind=kOutput, calls=%fused_computation.32 | convolution fusion | flops 4299161600 | bytes 13631488 | tf_op jit(solution)/shard_map/dot_general | solution.py:144
  45.3 2.5 fusion.97
  49.8 3.5 collective-permute-start
  53.4 11.2 %fusion.26 = bf16[1024,4096]{1,0:T(8,128)(2,1)} fusion(bf16[1024,1024]{1,0:T(8,128)(2,1)S(1)} %copy-done.16, bf16[1,1024,4096]{2,1,0:T(8,128)(2,1)S(1)} %bitcast.91), kind=kOutput, calls=%fused_computation.28 | convolution fusion | flops 8594128896 | bytes 18874368 | tf_op jit(solution)/shard_map/dot_general | solution.py:125
  64.6 14.8 %fusion.29 = bf16[1024,4096]{1,0:T(8,128)(2,1)} fusion(bf16[1024,1024]{1,0:T(8,128)(2,1)} %all-gather.5.cloned.1.call-done, bf16[1,4096,1024]{2,1,0:T(8,128)(2,1)} %param.6), kind=kOutput, calls=%fused_computation.29 | convolution fusion | flops 8594128896 | bytes 18874368 | tf_op jit(solution)/shard_map/dot_general | solution.py:127
  79.7 19.1 %collective-permute-done = bf16[256,4096]{1,0:T(8,128)(2,1)S(1)} collective-permute-done((bf16[256,4096]{1,0:T(8,128)(2,1)}, bf16[256,4096]{1,0:T(8,128)(2,1)S(1)}, u32[]{:S(2)}, u32[]{:S(2)}) %collective-permute-start) | collective-permute-done | bytes 2097184 | tf_op jit(solution)/shard_map/ppermute | solution.py:106
  99.1 3.5 fusion.52
  102.6 4.4 collective-permute-start.2
  107.0 2.5 collective-permute-start.4
  109.5 42.2 %collective-permute-done.2 = bf16[256,4096]{1,0:T(8,128)(2,1)S(1)} collective-permute-done((bf16[256,4096]{1,0:T(8,128)(2,1)}, bf16[256,4096]{1,0:T(8,128)(2,1)S(1)}, u32[]{:S(2)}, u32[]{:S(2)}) %collective-permute-start.2) | collective-permute-done | bytes 2097184 | tf_op jit(solution)/shard_map/ppermute | solution.py:106
  151.7 6.0 fusion.51
  157.7 10.1 %collective-permute-start.3 = (bf16[256,4096]{1,0:T(8,128)(2,1)}, bf16[256,4096]{1,0:T(8,128)(2,1)S(1)}, u32[]{:S(2)}, u32[]{:S(2)}) collective-permute-start(bf16[256,4096]{1,0:T(8,128)(2,1)} %get-tuple-element.40), channel_id=1, source_target_pairs={{0,4},{4,8},{8,12},{1,5},{5,9},{9,13},{2,6},{6,10},{10,14},{3,7},{... | collective-permute-start | bytes 6291464 | tf_op jit(solution)/shard_map/ppermute | solution.py:106
  169.1 42.2 %collective-permute-done.3 = bf16[256,4096]{1,0:T(8,128)(2,1)S(1)} collective-permute-done((bf16[256,4096]{1,0:T(8,128)(2,1)}, bf16[256,4096]{1,0:T(8,128)(2,1)S(1)}, u32[]{:S(2)}, u32[]{:S(2)}) %collective-permute-start.3) | collective-permute-done | bytes 2097184 | tf_op jit(solution)/shard_map/ppermute | solution.py:106
  211.2 4.2 collective-permute-done.5
  215.5 6.1 fusion.40
  221.6 2.2 collective-permute-start.6
  225.1 41.2 %collective-permute-done.6 = bf16[256,4096]{1,0:T(8,128)(2,1)S(1)} collective-permute-done((bf16[256,4096]{1,0:T(8,128)(2,1)}, bf16[256,4096]{1,0:T(8,128)(2,1)S(1)}, u32[]{:S(2)}, u32[]{:S(2)}) %collective-permute-start.6) | collective-permute-done | bytes 2097184 | tf_op jit(solution)/shard_map/ppermute | solution.py:106
  266.3 4.2 collective-permute-done.8
  270.5 5.4 bitcast_select_fusion
  277.2 5.9 collective-permute-start.7
  283.1 38.6 %collective-permute-done.9 = bf16[256,4096]{1,0:T(8,128)(2,1)S(1)} collective-permute-done((bf16[256,4096]{1,0:T(8,128)(2,1)}, bf16[256,4096]{1,0:T(8,128)(2,1)S(1)}, u32[]{:S(2)}, u32[]{:S(2)}) %collective-permute-start.9) | collective-permute-done | bytes 2097184 | tf_op jit(solution)/shard_map/ppermute | solution.py:106
  323.3 3.9 fusion.54
  327.2 6.1 collective-permute-start.10
  334.6 38.5 %collective-permute-done.10 = bf16[256,4096]{1,0:T(8,128)(2,1)S(1)} collective-permute-done((bf16[256,4096]{1,0:T(8,128)(2,1)S(1)}, bf16[256,4096]{1,0:T(8,128)(2,1)S(1)}, u32[]{:S(2)}, u32[]{:S(2)}) %collective-permute-start.10) | collective-permute-done | bytes 2097184 | tf_op jit(solution)/shard_map/ppermute | solution.py:106
  373.2 4.2 collective-permute-done.12
  377.4 3.1 fusion.44
  381.8 6.2 %collective-permute-start.11 = (bf16[256,4096]{1,0:T(8,128)(2,1)S(1)}, bf16[256,4096]{1,0:T(8,128)(2,1)}, u32[]{:S(2)}, u32[]{:S(2)}) collective-permute-start(bf16[256,4096]{1,0:T(8,128)(2,1)S(1)} %get-tuple-element.35), channel_id=1, source_target_pairs={{0,4},{4,8},{8,12},{1,5},{5,9},{9,13},{2,6},{6,10},{10,14},{3,7},{... | collective-permute-start | bytes 6291464 | tf_op jit(solution)/shard_map/ppermute | solution.py:106
  392.0 14.8 %fusion.8 = f32[1024,1024]{1,0:T(8,128)} fusion(bf16[1,4096,1024]{2,1,0:T(8,128)(2,1)} %param.6, bf16[256,4096]{1,0:T(8,128)(2,1)S(1)} %select_add_fusion, bf16[256,4096]{1,0:T(8,128)(2,1)S(1)} %get-tuple-element.44, bf16[256,4096]{1,0:T(8,128)(2,1)S(1)} %select_add_fusion.1, bf16[256,4096]{1,0:T(8,128)(2,1)} %get-tuple-element.33), kind=kOutput, calls=%fused_computation.9 | convolution fusion | flops 8623489024 | bytes 20971520 | tf_op jit(solution)/shard_map/dot_general | solution.py:168
  406.8 17.2 %collective-permute-done.13 = bf16[256,4096]{1,0:T(8,128)(2,1)} collective-permute-done((bf16[256,4096]{1,0:T(8,128)(2,1)}, bf16[256,4096]{1,0:T(8,128)(2,1)}, u32[]{:S(2)}, u32[]{:S(2)}) %collective-permute-start.13) | collective-permute-done | bytes 2097184 | tf_op jit(solution)/shard_map/ppermute | solution.py:106
  424.0 3.9 select_convert_fusion
  427.9 2.3 select_convert_fusion.1
  430.3 8.7 %fusion.43 = bf16[256,4096]{1,0:T(8,128)(2,1)} fusion(f32[256,4096]{1,0:T(8,128)} %get-tuple-element.26, f32[256,4096]{1,0:T(8,128)} %select_convert_fusion, f32[256,4096]{1,0:T(8,128)} %select_convert_fusion.1, bf16[4,256,4096]{2,1,0:T(8,128)(2,1)} %bitcast.83, s32[]{:T(128)S(6)} %select_n.302), kind=kLoop, calls=%fused_computation.44 | loop fusion | flops 5242880 | bytes 16777220 | tf_op jit(solution)/shard_map/convert_element_type | solution.py:179
  440.3 4.7 collective-permute-start.14
  445.0 8.1 %fusion.20 = f32[256,1024]{1,0:T(8,128)} fusion(bf16[256,4096]{1,0:T(8,128)(2,1)} %fusion.43, bf16[1,1024,4096]{2,1,0:T(8,128)(2,1)} %param.5), kind=kOutput, calls=%fused_computation.21 | convolution fusion | flops 2147483648 | bytes 11534336 | tf_op jit(solution)/shard_map/dot_general | solution.py:205
  453.2 28.5 %collective-permute-done.16 = bf16[256,4096]{1,0:T(8,128)(2,1)} collective-permute-done((bf16[256,4096]{1,0:T(8,128)(2,1)}, bf16[256,4096]{1,0:T(8,128)(2,1)}, u32[]{:S(2)}, u32[]{:S(2)}) %collective-permute-start.16) | collective-permute-done | bytes 2097184 | tf_op jit(solution)/shard_map/ppermute | solution.py:106
  481.7 3.1 broadcast_select_fusion.1
  490.2 7.7 %fusion.16 = f32[256,1024]{1,0:T(8,128)} fusion(bf16[256,4096]{1,0:T(8,128)(2,1)} %broadcast_select_fusion.1, bf16[1,1024,4096]{2,1,0:T(8,128)(2,1)} %param.5), kind=kOutput, calls=%fused_computation.17 | convolution fusion | flops 2147483648 | bytes 11534336 | tf_op jit(solution)/shard_map/dot_general | solution.py:205
  498.0 14.0 %convolution_convert_fusion = bf16[4096,1024]{1,0:T(8,128)(2,1)} fusion(s32[]{:T(128)S(6)} %select_n.327, bf16[1024,1024]{1,0:T(8,128)(2,1)} %all-gather.5.cloned.1.call-done, bf16[256,4096]{1,0:T(8,128)(2,1)} %copy-done.10, bf16[256,4096]{1,0:T(8,128)(2,1)S(1)} %copy-done.6, bf16[256,4096]{1,0:T(8,128)(2,1)} %copy-done.9, ...), kind=kOutput, calls=%fused_computation.30 | convolution fusion | flops 8631877632 | bytes 18874372 | tf_op jit(solution)/shard_map/dot_general | solution.py:169
  511.9 7.4 %fusion.18 = f32[256,1024]{1,0:T(8,128)} fusion(bf16[256,4096]{1,0:T(8,128)(2,1)} %broadcast_select_fusion.6, bf16[1,1024,4096]{2,1,0:T(8,128)(2,1)} %param.5), kind=kOutput, calls=%fused_computation.19 | convolution fusion | flops 2147483648 | bytes 11534336 | tf_op jit(solution)/shard_map/dot_general | solution.py:205
  519.4 7.0 %collective-permute-done.17 = bf16[256,4096]{1,0:T(8,128)(2,1)} collective-permute-done((bf16[256,4096]{1,0:T(8,128)(2,1)}, bf16[256,4096]{1,0:T(8,128)(2,1)}, u32[]{:S(2)}, u32[]{:S(2)}) %collective-permute-start.17) | collective-permute-done | bytes 2097184 | tf_op jit(solution)/shard_map/ppermute | solution.py:106
  533.2 2.4 add.237
  536.9 7.1 %fusion.14 = f32[256,1024]{1,0:T(8,128)} fusion(bf16[256,4096]{1,0:T(8,128)(2,1)S(1)} %add.237, bf16[1,1024,4096]{2,1,0:T(8,128)(2,1)} %param.5), kind=kOutput, calls=%fused_computation.15 | convolution fusion | flops 2147483648 | bytes 11534336 | tf_op jit(solution)/shard_map/dot_general | solution.py:205
  545.3 2.5 fusion.65
  547.8 24.7 %collective-permute-done.19 = bf16[256,4096]{1,0:T(8,128)(2,1)} collective-permute-done((bf16[256,4096]{1,0:T(8,128)(2,1)S(1)}, bf16[256,4096]{1,0:T(8,128)(2,1)}, u32[]{:S(2)}, u32[]{:S(2)}) %collective-permute-start.19) | collective-permute-done | bytes 2097184 | tf_op jit(solution)/shard_map/ppermute | solution.py:106
  572.5 7.6 %fusion.12 = f32[256,1024]{1,0:T(8,128)} fusion(bf16[1,1024,4096]{2,1,0:T(8,128)(2,1)} %param.5, bf16[256,4096]{1,0:T(8,128)(2,1)} %collective-permute-done.19, pred[]{:T(512)S(6)} %and.24, bf16[256,4096]{1,0:T(8,128)(2,1)} %collective-permute-done.18, pred[]{:T(512)S(6)} %and.27), kind=kOutput, calls=%fused_computation.13 | convolution fusion | flops 2150629376 | bytes 13631490 | tf_op jit(solution)/shard_map/dot_general | solution.py:205
  584.6 14.1 %convert_bitcast_fusion = bf16[1,1024,4096]{2,1,0:T(8,128)(2,1)} fusion(bf16[256,4096]{1,0:T(8,128)(2,1)S(1)} %fusion.61, bf16[256,4096]{1,0:T(8,128)(2,1)S(1)} %copy-done.8, bf16[256,4096]{1,0:T(8,128)(2,1)S(1)} %fusion.62, bf16[256,4096]{1,0:T(8,128)(2,1)} %fusion.43, s32[]{:T(128)S(6)} %select_n.327, bf16[1024,1024]{1,0:T(8,128)(2,1)} %all-gather.3.cloned.1.call-done), kind=kOutput, calls=%fused_computation.27 | convolution fusion | flops 8631877632 | bytes 18874372 | tf_op jit(solution)/shard_map/dot_general | solution.py:191
  598.8 12.5 %reduce-scatter.17.cloned.1.call-done = f32[256,256]{1,0:T(8,128)} async-done(((f32[256,1024]{1,0:T(8,128)}), f32[256,256]{1,0:T(8,128)}) %reduce-scatter.17.cloned.1.call-update) | async-done | bytes 262160 | tf_op jit(solution)/shard_map/reduce_scatter | solution.py:208
  (100 shorter events, 40.6 us)
Async XLA Ops:
  7.2 28.0 %all-gather.3.cloned.1.call-start = ((), (), s32[]{:S(2)}) async-start(), calls=%async_computation.6 | async-start | bytes 2621440 | tf_op jit(solution)/shard_map/all_gather | solution.py:124
  7.9 56.7 %all-gather.5.cloned.1.call-start = ((), (), s32[]{:S(2)}) async-start(), calls=%async_computation.7 | async-start | bytes 2621440 | tf_op jit(solution)/shard_map/all_gather | solution.py:126
  8.6 521.0 %reduce-scatter.7.cloned.1.call-start = ((), (), s32[]{:S(2)}) async-start(), calls=%async_computation.8 | async-start | bytes 5242880 | tf_op jit(solution)/shard_map/reduce_scatter | solution.py:177
  35.1 18.3 %slice-start.2 = ((s8[8388608]{0:T(1024)(128)(4,1)}), s8[4194304]{0:T(1024)(128)(4,1)S(1)}, s32[]{:S(2)}) async-start(s8[8388608]{0:T(1024)(128)(4,1)} %bitcast.90), calls=%async_computation.16 | async-start | bytes 8388608
  36.5 16.8 %slice-start.3 = ((s8[8388608]{0:T(1024)(128)(4,1)}), s8[4194304]{0:T(1024)(128)(4,1)S(1)}, s32[]{:S(2)}) async-start(s8[8388608]{0:T(1024)(128)(4,1)} %bitcast.90), calls=%async_computation.17 | async-start | bytes 8388608
  45.3 8.1 %copy-start.16 = (bf16[1024,1024]{1,0:T(8,128)(2,1)S(1)}, bf16[1024,1024]{1,0:T(8,128)(2,1)}, u32[]{:S(2)}) copy-start(bf16[1024,1024]{1,0:T(8,128)(2,1)} %all-gather.3.cloned.1.call-done) | copy-start | bytes 6291460
  47.8 31.6 %collective-permute-start.1 = (bf16[256,4096]{1,0:T(8,128)(2,1)}, bf16[256,4096]{1,0:T(8,128)(2,1)}, u32[]{:S(2)}, u32[]{:S(2)}) collective-permute-start(bf16[256,4096]{1,0:T(8,128)(2,1)} %get-tuple-element.45), channel_id=1, source_target_pairs={{12,8},{13,9},{14,10},{15,11},{28,24},{29,25},{30,26},{31,27}} | collective-permute-start | bytes 6291464 | tf_op jit(solution)/shard_map/ppermute | solution.py:106
  49.8 49.0 %collective-permute-start = (bf16[256,4096]{1,0:T(8,128)(2,1)}, bf16[256,4096]{1,0:T(8,128)(2,1)S(1)}, u32[]{:S(2)}, u32[]{:S(2)}) collective-permute-start(bf16[256,4096]{1,0:T(8,128)(2,1)} %get-tuple-element.46), channel_id=1, source_target_pairs={{0,4},{1,5},{2,6},{3,7},{16,20},{17,21},{18,22},{19,23}} | collective-permute-start | bytes 6291464 | tf_op jit(solution)/shard_map/ppermute | solution.py:106
  79.4 19.7 %copy-start = (bf16[1024,4096]{1,0:T(8,128)(2,1)S(1)}, bf16[1024,4096]{1,0:T(8,128)(2,1)}, u32[]{:S(2)}) copy-start(bf16[1024,4096]{1,0:T(8,128)(2,1)} %fusion.26) | copy-start | bytes 25165828
  102.6 49.1 %collective-permute-start.2 = (bf16[256,4096]{1,0:T(8,128)(2,1)}, bf16[256,4096]{1,0:T(8,128)(2,1)S(1)}, u32[]{:S(2)}, u32[]{:S(2)}) collective-permute-start(bf16[256,4096]{1,0:T(8,128)(2,1)} %get-tuple-element.42), channel_id=1, source_target_pairs={{0,4},{4,8},{1,5},{5,9},{2,6},{6,10},{3,7},{7,11},{16,20},{20,24},... | collective-permute-start | bytes 6291464 | tf_op jit(solution)/shard_map/ppermute | solution.py:106
  107.0 44.7 %collective-permute-start.4 = (bf16[256,4096]{1,0:T(8,128)(2,1)}, bf16[256,4096]{1,0:T(8,128)(2,1)}, u32[]{:S(2)}, u32[]{:S(2)}) collective-permute-start(bf16[256,4096]{1,0:T(8,128)(2,1)} %get-tuple-element.43), channel_id=1, source_target_pairs={{8,4},{12,8},{9,5},{13,9},{10,6},{14,10},{11,7},{15,11},{24,20},{2... | collective-permute-start | bytes 6291464 | tf_op jit(solution)/shard_map/ppermute | solution.py:106
  157.7 53.5 %collective-permute-start.3 = (bf16[256,4096]{1,0:T(8,128)(2,1)}, bf16[256,4096]{1,0:T(8,128)(2,1)S(1)}, u32[]{:S(2)}, u32[]{:S(2)}) collective-permute-start(bf16[256,4096]{1,0:T(8,128)(2,1)} %get-tuple-element.40), channel_id=1, source_target_pairs={{0,4},{4,8},{8,12},{1,5},{5,9},{9,13},{2,6},{6,10},{10,14},{3,7},{... | collective-permute-start | bytes 6291464 | tf_op jit(solution)/shard_map/ppermute | solution.py:106
  167.8 47.7 %collective-permute-start.5 = (bf16[256,4096]{1,0:T(8,128)(2,1)}, bf16[256,4096]{1,0:T(8,128)(2,1)}, u32[]{:S(2)}, u32[]{:S(2)}) collective-permute-start(bf16[256,4096]{1,0:T(8,128)(2,1)} %get-tuple-element.41), channel_id=1, source_target_pairs={{4,0},{8,4},{12,8},{5,1},{9,5},{13,9},{6,2},{10,6},{14,10},{7,3},{... | collective-permute-start | bytes 6291464 | tf_op jit(solution)/shard_map/ppermute | solution.py:106
  221.6 44.7 %collective-permute-start.6 = (bf16[256,4096]{1,0:T(8,128)(2,1)}, bf16[256,4096]{1,0:T(8,128)(2,1)S(1)}, u32[]{:S(2)}, u32[]{:S(2)}) collective-permute-start(bf16[256,4096]{1,0:T(8,128)(2,1)} %get-tuple-element.33), channel_id=1, source_target_pairs={{0,4},{4,8},{8,12},{1,5},{5,9},{9,13},{2,6},{6,10},{10,14},{3,7},{... | collective-permute-start | bytes 6291464 | tf_op jit(solution)/shard_map/ppermute | solution.py:106
  223.8 46.8 %collective-permute-start.8 = (bf16[256,4096]{1,0:T(8,128)(2,1)}, bf16[256,4096]{1,0:T(8,128)(2,1)}, u32[]{:S(2)}, u32[]{:S(2)}) collective-permute-start(bf16[256,4096]{1,0:T(8,128)(2,1)} %get-tuple-element.33), channel_id=1, source_target_pairs={{4,0},{8,4},{12,8},{5,1},{9,5},{13,9},{6,2},{10,6},{14,10},{7,3},{... | collective-permute-start | bytes 6291464 | tf_op jit(solution)/shard_map/ppermute | solution.py:106
  266.3 9.6 %copy-start.3 = (bf16[256,4096]{1,0:T(8,128)(2,1)}, bf16[256,4096]{1,0:T(8,128)(2,1)S(1)}, u32[]{:S(2)}) copy-start(bf16[256,4096]{1,0:T(8,128)(2,1)S(1)} %collective-permute-done.6) | copy-start | bytes 6291460
  275.9 45.7 %collective-permute-start.9 = (bf16[256,4096]{1,0:T(8,128)(2,1)}, bf16[256,4096]{1,0:T(8,128)(2,1)S(1)}, u32[]{:S(2)}, u32[]{:S(2)}) collective-permute-start(bf16[256,4096]{1,0:T(8,128)(2,1)} %get-tuple-element.38), channel_id=1, source_target_pairs={{4,0},{8,4},{12,8},{5,1},{9,5},{13,9},{6,2},{10,6},{14,10},{7,3},{... | collective-permute-start | bytes 6291464 | tf_op jit(solution)/shard_map/ppermute | solution.py:106
  277.2 45.7 %collective-permute-start.7 = (bf16[256,4096]{1,0:T(8,128)(2,1)}, bf16[256,4096]{1,0:T(8,128)(2,1)}, u32[]{:S(2)}, u32[]{:S(2)}) collective-permute-start(bf16[256,4096]{1,0:T(8,128)(2,1)} %get-tuple-element.39), channel_id=1, source_target_pairs={{4,8},{8,12},{0,4},{5,9},{9,13},{1,5},{6,10},{10,14},{2,6},{7,11},... | collective-permute-start | bytes 6291464 | tf_op jit(solution)/shard_map/ppermute | solution.py:106
  323.2 54.2 %slice-start = ((s8[8388608]{0:T(1024)(128)(4,1)}), s8[4194304]{0:T(1024)(128)(4,1)S(1)}, s32[]{:S(2)}) async-start(s8[8388608]{0:T(1024)(128)(4,1)} %bitcast.84), calls=%async_computation.14 | async-start | bytes 8388608
  323.3 54.2 %slice-start.1 = ((s8[8388608]{0:T(1024)(128)(4,1)}), s8[4194304]{0:T(1024)(128)(4,1)S(1)}, s32[]{:S(2)}) async-start(s8[8388608]{0:T(1024)(128)(4,1)} %bitcast.84), calls=%async_computation.15 | async-start | bytes 8388608
  327.2 63.0 %copy-start.5 = (bf16[256,4096]{1,0:T(8,128)(2,1)}, bf16[256,4096]{1,0:T(8,128)(2,1)S(1)}, u32[]{:S(2)}) copy-start(bf16[256,4096]{1,0:T(8,128)(2,1)S(1)} %get-tuple-element.44) | copy-start | bytes 6291460
  327.2 45.9 %collective-permute-start.10 = (bf16[256,4096]{1,0:T(8,128)(2,1)S(1)}, bf16[256,4096]{1,0:T(8,128)(2,1)S(1)}, u32[]{:S(2)}, u32[]{:S(2)}) collective-permute-start(bf16[256,4096]{1,0:T(8,128)(2,1)S(1)} %get-tuple-element.37), channel_id=1, source_target_pairs={{8,12},{0,4},{4,8},{9,13},{1,5},{5,9},{10,14},{2,6},{6,10},{11,15}... | collective-permute-start | bytes 6291464 | tf_op jit(solution)/shard_map/ppermute | solution.py:106
  333.3 44.1 %collective-permute-start.12 = (bf16[256,4096]{1,0:T(8,128)(2,1)S(1)}, bf16[256,4096]{1,0:T(8,128)(2,1)S(1)}, u32[]{:S(2)}, u32[]{:S(2)}) collective-permute-start(bf16[256,4096]{1,0:T(8,128)(2,1)S(1)} %get-tuple-element.36), channel_id=1, source_target_pairs={{4,0},{8,4},{12,8},{5,1},{9,5},{13,9},{6,2},{10,6},{14,10},{7,3},{... | collective-permute-start | bytes 6291464 | tf_op jit(solution)/shard_map/ppermute | solution.py:106
  380.5 43.5 %collective-permute-start.13 = (bf16[256,4096]{1,0:T(8,128)(2,1)}, bf16[256,4096]{1,0:T(8,128)(2,1)}, u32[]{:S(2)}, u32[]{:S(2)}) collective-permute-start(bf16[256,4096]{1,0:T(8,128)(2,1)} %get-tuple-element.34), channel_id=1, source_target_pairs={{4,0},{8,4},{12,8},{5,1},{9,5},{13,9},{6,2},{10,6},{14,10},{7,3},{... | collective-permute-start | bytes 6291464 | tf_op jit(solution)/shard_map/ppermute | solution.py:106
  381.8 8.1 %copy-start.4 = (bf16[256,4096]{1,0:T(8,128)(2,1)S(1)}, bf16[256,4096]{1,0:T(8,128)(2,1)}, u32[]{:S(2)}) copy-start(bf16[256,4096]{1,0:T(8,128)(2,1)} %copy-done.3) | copy-start | bytes 6291460
  381.8 46.0 %collective-permute-start.11 = (bf16[256,4096]{1,0:T(8,128)(2,1)S(1)}, bf16[256,4096]{1,0:T(8,128)(2,1)}, u32[]{:S(2)}, u32[]{:S(2)}) collective-permute-start(bf16[256,4096]{1,0:T(8,128)(2,1)S(1)} %get-tuple-element.35), channel_id=1, source_target_pairs={{0,4},{4,8},{8,12},{1,5},{5,9},{9,13},{2,6},{6,10},{10,14},{3,7},{... | collective-permute-start | bytes 6291464 | tf_op jit(solution)/shard_map/ppermute | solution.py:106
  390.2 1.7 copy-start.10
  430.2 168.5 %reduce-scatter.9.cloned.1.call-start = ((), (), s32[]{:S(2)}) async-start(), calls=%async_computation.9 | async-start | bytes 1310720 | tf_op jit(solution)/shard_map/reduce_scatter | solution.py:208
  439.0 42.7 %collective-permute-start.16 = (bf16[256,4096]{1,0:T(8,128)(2,1)}, bf16[256,4096]{1,0:T(8,128)(2,1)}, u32[]{:S(2)}, u32[]{:S(2)}) collective-permute-start(bf16[256,4096]{1,0:T(8,128)(2,1)} %fusion.43), channel_id=1, source_target_pairs={{4,0},{8,4},{12,8},{5,1},{9,5},{13,9},{6,2},{10,6},{14,10},{7,3},{... | collective-permute-start | bytes 6291464 | tf_op jit(solution)/shard_map/ppermute | solution.py:106
  440.3 45.8 %collective-permute-start.14 = (bf16[256,4096]{1,0:T(8,128)(2,1)}, bf16[256,4096]{1,0:T(8,128)(2,1)S(1)}, u32[]{:S(2)}, u32[]{:S(2)}) collective-permute-start(bf16[256,4096]{1,0:T(8,128)(2,1)} %fusion.43), channel_id=1, source_target_pairs={{0,4},{4,8},{8,12},{1,5},{5,9},{9,13},{2,6},{6,10},{10,14},{3,7},{... | collective-permute-start | bytes 6291464 | tf_op jit(solution)/shard_map/ppermute | solution.py:106
  453.1 145.6 %reduce-scatter.13.cloned.1.call-start = ((), (), s32[]{:S(2)}) async-start(), calls=%async_computation.11 | async-start | bytes 1310720 | tf_op jit(solution)/shard_map/reduce_scatter | solution.py:208
  484.8 41.6 %collective-permute-start.17 = (bf16[256,4096]{1,0:T(8,128)(2,1)}, bf16[256,4096]{1,0:T(8,128)(2,1)}, u32[]{:S(2)}, u32[]{:S(2)}) collective-permute-start(bf16[256,4096]{1,0:T(8,128)(2,1)} %broadcast_select_fusion.1), channel_id=1, source_target_pairs={{4,0},{8,4},{5,1},{9,5},{6,2},{10,6},{7,3},{11,7},{20,16},{24,20},... | collective-permute-start | bytes 6291464 | tf_op jit(solution)/shard_map/ppermute | solution.py:106
  486.1 1.9 copy-start.1
  488.0 40.1 %collective-permute-start.15 = (bf16[256,4096]{1,0:T(8,128)(2,1)}, bf16[256,4096]{1,0:T(8,128)(2,1)}, u32[]{:S(2)}, u32[]{:S(2)}) collective-permute-start(bf16[256,4096]{1,0:T(8,128)(2,1)} %broadcast_select_fusion.6), channel_id=1, source_target_pairs={{4,8},{8,12},{5,9},{9,13},{6,10},{10,14},{7,11},{11,15},{20,24},{2... | collective-permute-start | bytes 6291464 | tf_op jit(solution)/shard_map/ppermute | solution.py:106
  490.2 7.8 %copy-start.6 = (bf16[256,4096]{1,0:T(8,128)(2,1)S(1)}, bf16[256,4096]{1,0:T(8,128)(2,1)}, u32[]{:S(2)}) copy-start(bf16[256,4096]{1,0:T(8,128)(2,1)} %copy-done.5) | copy-start | bytes 6291460
  497.9 100.9 %reduce-scatter.11.cloned.1.call-start = ((), (), s32[]{:S(2)}) async-start(), calls=%async_computation.10 | async-start | bytes 1310720 | tf_op jit(solution)/shard_map/reduce_scatter | solution.py:208
  519.4 79.4 %reduce-scatter.15.cloned.1.call-start = ((), (), s32[]{:S(2)}) async-start(), calls=%async_computation.12 | async-start | bytes 1310720 | tf_op jit(solution)/shard_map/reduce_scatter | solution.py:208
  529.7 18.1 %collective-permute-start.18 = (bf16[256,4096]{1,0:T(8,128)(2,1)}, bf16[256,4096]{1,0:T(8,128)(2,1)}, u32[]{:S(2)}, u32[]{:S(2)}) collective-permute-start(bf16[256,4096]{1,0:T(8,128)(2,1)} %broadcast_select_fusion.8), channel_id=1, source_target_pairs={{8,12},{9,13},{10,14},{11,15},{24,28},{25,29},{26,30},{27,31}} | collective-permute-start | bytes 6291464 | tf_op jit(solution)/shard_map/ppermute | solution.py:106
  531.7 40.8 %collective-permute-start.19 = (bf16[256,4096]{1,0:T(8,128)(2,1)S(1)}, bf16[256,4096]{1,0:T(8,128)(2,1)}, u32[]{:S(2)}, u32[]{:S(2)}) collective-permute-start(bf16[256,4096]{1,0:T(8,128)(2,1)S(1)} %broadcast_select_fusion.4), channel_id=1, source_target_pairs={{4,0},{5,1},{6,2},{7,3},{20,16},{21,17},{22,18},{23,19}} | collective-permute-start | bytes 6291464 | tf_op jit(solution)/shard_map/ppermute | solution.py:106
  535.6 1.3 copy-start.7
  544.0 67.4 %reduce-scatter.17.cloned.1.call-start = ((), (), s32[]{:S(2)}) async-start(), calls=%async_computation.13 | async-start | bytes 1310720 | tf_op jit(solution)/shard_map/reduce_scatter | solution.py:208
  580.1 2.3 copy-start.2
  582.4 2.3 copy-start.8
  598.7 14.1 %copy-start.11 = (f32[256,256]{1,0:T(8,128)S(1)}, f32[256,256]{1,0:T(8,128)}, u32[]{:S(2)}) copy-start(f32[256,256]{1,0:T(8,128)} %reduce-scatter.9.cloned.1.call-done) | copy-start | bytes 786436
  598.7 14.1 %copy-start.12 = (f32[256,256]{1,0:T(8,128)S(1)}, f32[256,256]{1,0:T(8,128)}, u32[]{:S(2)}) copy-start(f32[256,256]{1,0:T(8,128)} %reduce-scatter.13.cloned.1.call-done) | copy-start | bytes 786436
  598.8 14.1 %copy-start.13 = (f32[256,256]{1,0:T(8,128)S(1)}, f32[256,256]{1,0:T(8,128)}, u32[]{:S(2)}) copy-start(f32[256,256]{1,0:T(8,128)} %reduce-scatter.11.cloned.1.call-done) | copy-start | bytes 786436
  598.8 14.1 %copy-start.14 = (f32[256,256]{1,0:T(8,128)S(1)}, f32[256,256]{1,0:T(8,128)}, u32[]{:S(2)}) copy-start(f32[256,256]{1,0:T(8,128)} %reduce-scatter.15.cloned.1.call-done) | copy-start | bytes 786436
  611.4 1.5 copy-start.15
  (1 other events, 1.3 us)
Sparse Core Ops, SparseCore 0:
  9.6 25.5 all-gather.2
  36.7 22.8 all-gather.4
  430.3 43.5 reduce-scatter.6
  476.5 24.8 reduce-scatter.8
  503.8 24.9 reduce-scatter.12
  531.3 24.8 reduce-scatter.10
  558.8 24.9 reduce-scatter.14
  586.4 24.8 reduce-scatter.16

commit v4 on v2

--- a/solution.py
+++ b/solution.py
@@ -150,8 +150,13 @@
     act_gather = LineGather(gelu_value(preact).astype(jnp.bfloat16))
     if count > 1:
         run_slot([(act_gather, 0)])
+    slope = gelu_slope(preact)
     for step in range(1, count - 1):
         run_slot([(act_gather, step), (grad_sum, step - 1)])
+        if step == 1:
+            grad_sum.up_in, grad_sum.down_in, slope = lax.optimization_barrier(
+                (grad_sum.up_in, grad_sum.down_in, slope)
+            )
     tokens = x_rows.shape[0]
     turn = lax.axis_index("r") * (tokens // count)
     grad_turned = rotate_rows(grad_rows, turn)
@@ -167,7 +172,7 @@
         )
     out_sum = lax.psum_scatter(out_part, "p", scatter_dimension=1, tiled=True)
     act_grad = grad_sum.result()
-    pre_gather = LineGather((act_grad * gelu_slope(preact)).astype(jnp.bfloat16))
+    pre_gather = LineGather((act_grad * slope).astype(jnp.bfloat16))
     for step in range(count - 1):
         run_slot([(pre_gather, step)])
         if step == min(1, count - 2):

time: 627 us -> 627 us (level)
  starting transfers between devices: 75.1 us -> 61.4 us
  waiting for transfers between devices: 342 us -> 354 us
    ppermute x20, starting transfers between devices: 74 us -> 61 us  [run_slot(): received.append(lax.ppermute(combined, 'r', pairs))]
    ppermute x20, waiting for transfers between devices: 305 us -> 315 us  [run_slot(): received.append(lax.ppermute(combined, 'r', pairs))]
  transfers between devices with their start and end apart: 28 -> 28, of which waited for: 18 -> 16; matrix products, arithmetic and copies ran while one was open for 23% -> 25% of each run, Pallas kernels for 0% -> 0%
where the time goes in v4:
time: 627 us; the launch traced here: 623 us
  waiting for transfers between devices  354 us (56%)
  matrix products  122 us (19%)
  other arithmetic  66.7 us (11%)
  starting transfers between devices  61.4 us (10%)
  between operations  15 us (2%)
    ppermute x20, waiting for transfers between devices, run_slot(): received.append(lax.ppermute(combined, 'r', pairs))  315 us
    ppermute x20, starting transfers between devices, run_slot(): received.append(lax.ppermute(combined, 'r', pairs))  61 us
    dot_general x5, matrix products, on_device(): lax.dot_general(piece, up_tile, (((1,), (1,)), ((), ())), preferred_eleme...  37.8 us
    all_gather x1, waiting for transfers between devices, on_device(): x_rows = lax.all_gather(hidden_in, 'p', axis=1, tiled=True)  26.4 us
    dot_general x2, matrix products, block_terms(): jnp.dot(x_block, up_tile, preferred_element_type=jnp.float32)  15.3 us
    dot_general x1, matrix products, on_device(): jnp.dot(activation, down_tile, preferred_element_type=jnp.float32)  14.8 us
    dot_general x1, matrix products, on_device(): lax.dot_general(grad_rows, down_tile, (((1,), (1,)), ((), ())), preferred...  14.8 us
    dot_general x1, matrix products, on_device(): lax.dot_general(rotate_rows(x_rows, turn), pre_grad, (((0,), (0,)), ((),...  14.1 us
  transfers between devices with their start and end apart: 28, of which 16 were waited for; matrix products, arithmetic and copies ran while one was open for 25% of the time, Pallas kernels for 0%

profile of v4, /device:TPU:0, one launch (start us, length us, event | category | flops | bytes accessed | tf_op | source)
XLA Modules:
  0.0 622.7 jit_solution(4276510831514972851)
XLA Ops:
  8.7 26.4 %all-gather.3.cloned.1.call-done = bf16[1024,1024]{1,0:T(8,128)(2,1)} async-done(((bf16[1024,256]{1,0:T(8,128)(2,1)}), bf16[1024,1024]{1,0:T(8,128)(2,1)}) %all-gather.3.cloned.1.call-update) | async-done | bytes 2097168 | tf_op jit(solution)/shard_map/all_gather | solution.py:124
  35.1 7.4 %fusion.39 = bf16[256,4096]{1,0:T(8,128)(2,1)} fusion(bf16[1,1024,4096]{2,1,0:T(8,128)(2,1)} %param.5, bf16[1024,1024]{1,0:T(8,128)(2,1)} %all-gather.3.cloned.1.call-done, s32[]{:T(128)S(6)} %select_n.298), kind=kOutput, calls=%fused_computation.35 | convolution fusion | flops 2148532224 | bytes 11010052 | tf_op jit(solution)/shard_map/dot_general | solution.py:139
  43.4 7.9 %fusion.36 = bf16[256,4096]{1,0:T(8,128)(2,1)} fusion(bf16[1,1024,4096]{2,1,0:T(8,128)(2,1)} %param.5, bf16[1024,1024]{1,0:T(8,128)(2,1)S(1)} %copy-done.16, s32[]{:T(128)S(6)} %select_n.295), kind=kOutput, calls=%fused_computation.34 | convolution fusion | flops 2148532224 | bytes 11010052 | tf_op jit(solution)/shard_map/dot_general | solution.py:139
  51.4 4.9 collective-permute-start
  56.4 10.8 %fusion.28 = bf16[1024,4096]{1,0:T(8,128)(2,1)} fusion(bf16[1024,1024]{1,0:T(8,128)(2,1)S(1)} %copy-done.16, bf16[1,1024,4096]{2,1,0:T(8,128)(2,1)S(1)} %bitcast.95), kind=kOutput, calls=%fused_computation.30 | convolution fusion | flops 8594128896 | bytes 18874368 | tf_op jit(solution)/shard_map/dot_general | solution.py:125
  67.2 14.8 %fusion.31 = bf16[1024,4096]{1,0:T(8,128)(2,1)} fusion(bf16[1024,1024]{1,0:T(8,128)(2,1)} %all-gather.5.cloned.1.call-done, bf16[1,4096,1024]{2,1,0:T(8,128)(2,1)} %param.6), kind=kOutput, calls=%fused_computation.31 | convolution fusion | flops 8594128896 | bytes 18874368 | tf_op jit(solution)/shard_map/dot_general | solution.py:127
  82.3 18.1 %collective-permute-done = bf16[256,4096]{1,0:T(8,128)(2,1)} collective-permute-done((bf16[256,4096]{1,0:T(8,128)(2,1)}, bf16[256,4096]{1,0:T(8,128)(2,1)}, u32[]{:S(2)}, u32[]{:S(2)}) %collective-permute-start) | collective-permute-done | bytes 2097184 | tf_op jit(solution)/shard_map/ppermute | solution.py:106
  100.7 3.5 fusion.57
  104.2 6.1 collective-permute-start.2
  112.4 42.6 %collective-permute-done.2 = bf16[256,4096]{1,0:T(8,128)(2,1)S(1)} collective-permute-done((bf16[256,4096]{1,0:T(8,128)(2,1)}, bf16[256,4096]{1,0:T(8,128)(2,1)S(1)}, u32[]{:S(2)}, u32[]{:S(2)}) %collective-permute-start.2) | collective-permute-done | bytes 2097184 | tf_op jit(solution)/shard_map/ppermute | solution.py:106
  155.0 6.0 fusion.56
  161.0 7.1 %collective-permute-start.3 = (bf16[256,4096]{1,0:T(8,128)(2,1)}, bf16[256,4096]{1,0:T(8,128)(2,1)S(1)}, u32[]{:S(2)}, u32[]{:S(2)}) collective-permute-start(bf16[256,4096]{1,0:T(8,128)(2,1)} %get-tuple-element.40), channel_id=1, source_target_pairs={{0,4},{4,8},{8,12},{1,5},{5,9},{9,13},{2,6},{6,10},{10,14},{3,7},{... | collective-permute-start | bytes 6291464 | tf_op jit(solution)/shard_map/ppermute | solution.py:106
  169.4 42.4 %collective-permute-done.3 = bf16[256,4096]{1,0:T(8,128)(2,1)S(1)} collective-permute-done((bf16[256,4096]{1,0:T(8,128)(2,1)}, bf16[256,4096]{1,0:T(8,128)(2,1)S(1)}, u32[]{:S(2)}, u32[]{:S(2)}) %collective-permute-start.3) | collective-permute-done | bytes 2097184 | tf_op jit(solution)/shard_map/ppermute | solution.py:106
  211.8 4.2 collective-permute-done.5
  216.0 6.1 fusion.45
  222.1 2.6 collective-permute-start.6
  226.0 41.1 %collective-permute-done.6 = bf16[256,4096]{1,0:T(8,128)(2,1)S(1)} collective-permute-done((bf16[256,4096]{1,0:T(8,128)(2,1)}, bf16[256,4096]{1,0:T(8,128)(2,1)S(1)}, u32[]{:S(2)}, u32[]{:S(2)}) %collective-permute-start.6) | collective-permute-done | bytes 2097184 | tf_op jit(solution)/shard_map/ppermute | solution.py:106
  267.1 4.7 collective-permute-done.8
  271.8 5.4 bitcast_select_fusion
  278.4 5.9 collective-permute-start.7
  284.3 38.9 %collective-permute-done.9 = bf16[256,4096]{1,0:T(8,128)(2,1)S(1)} collective-permute-done((bf16[256,4096]{1,0:T(8,128)(2,1)}, bf16[256,4096]{1,0:T(8,128)(2,1)S(1)}, u32[]{:S(2)}, u32[]{:S(2)}) %collective-permute-start.9) | collective-permute-done | bytes 2097184 | tf_op jit(solution)/shard_map/ppermute | solution.py:106
  324.8 3.9 fusion.59
  328.7 6.1 collective-permute-start.10
  336.1 38.8 %collective-permute-done.10 = bf16[256,4096]{1,0:T(8,128)(2,1)S(1)} collective-permute-done((bf16[256,4096]{1,0:T(8,128)(2,1)S(1)}, bf16[256,4096]{1,0:T(8,128)(2,1)S(1)}, u32[]{:S(2)}, u32[]{:S(2)}) %collective-permute-start.10) | collective-permute-done | bytes 2097184 | tf_op jit(solution)/shard_map/ppermute | solution.py:106
  374.9 4.2 collective-permute-done.12
  379.2 3.1 fusion.49
  383.6 6.1 collective-permute-start.11
  393.5 14.8 %fusion.8 = f32[1024,1024]{1,0:T(8,128)} fusion(bf16[1,4096,1024]{2,1,0:T(8,128)(2,1)} %param.6, bf16[256,4096]{1,0:T(8,128)(2,1)S(1)} %select_add_fusion, bf16[256,4096]{1,0:T(8,128)(2,1)S(1)} %get-tuple-element.44, bf16[256,4096]{1,0:T(8,128)(2,1)S(1)} %select_add_fusion.1, bf16[256,4096]{1,0:T(8,128)(2,1)} %get-tuple-element.33), kind=kOutput, calls=%fused_computation.9 | convolution fusion | flops 8623489024 | bytes 20971520 | tf_op jit(solution)/shard_map/dot_general | solution.py:164
  408.4 17.7 %collective-permute-done.13 = bf16[256,4096]{1,0:T(8,128)(2,1)} collective-permute-done((bf16[256,4096]{1,0:T(8,128)(2,1)}, bf16[256,4096]{1,0:T(8,128)(2,1)}, u32[]{:S(2)}, u32[]{:S(2)}) %collective-permute-start.13) | collective-permute-done | bytes 2097184 | tf_op jit(solution)/shard_map/ppermute | solution.py:106
  426.0 3.9 select_convert_fusion
  429.9 2.3 select_convert_fusion.1
  432.3 8.7 %fusion.48 = bf16[256,4096]{1,0:T(8,128)(2,1)} fusion(f32[256,4096]{1,0:T(8,128)} %get-tuple-element.26, f32[256,4096]{1,0:T(8,128)} %select_convert_fusion, f32[256,4096]{1,0:T(8,128)} %select_convert_fusion.1, bf16[4,256,4096]{2,1,0:T(8,128)(2,1)} %bitcast.87, s32[]{:T(128)S(6)} %select_n.302), kind=kLoop, calls=%fused_computation.47 | loop fusion | flops 5242880 | bytes 16777220 | tf_op jit(solution)/shard_map/convert_element_type | solution.py:175
  442.3 4.7 collective-permute-start.14
  447.1 8.1 %fusion.20 = f32[256,1024]{1,0:T(8,128)} fusion(bf16[256,4096]{1,0:T(8,128)(2,1)} %fusion.48, bf16[1,1024,4096]{2,1,0:T(8,128)(2,1)} %param.5), kind=kOutput, calls=%fused_computation.21 | convolution fusion | flops 2147483648 | bytes 11534336 | tf_op jit(solution)/shard_map/dot_general | solution.py:201
  455.2 28.6 %collective-permute-done.16 = bf16[256,4096]{1,0:T(8,128)(2,1)} collective-permute-done((bf16[256,4096]{1,0:T(8,128)(2,1)}, bf16[256,4096]{1,0:T(8,128)(2,1)}, u32[]{:S(2)}, u32[]{:S(2)}) %collective-permute-start.16) | collective-permute-done | bytes 2097184 | tf_op jit(solution)/shard_map/ppermute | solution.py:106
  483.8 3.1 broadcast_select_fusion.1
  490.1 2.1 collective-permute-start.15
  492.3 7.7 %fusion.16 = f32[256,1024]{1,0:T(8,128)} fusion(bf16[256,4096]{1,0:T(8,128)(2,1)} %broadcast_select_fusion.1, bf16[1,1024,4096]{2,1,0:T(8,128)(2,1)} %param.5), kind=kOutput, calls=%fused_computation.17 | convolution fusion | flops 2147483648 | bytes 11534336 | tf_op jit(solution)/shard_map/dot_general | solution.py:201
  500.0 14.0 %convolution_convert_fusion = bf16[4096,1024]{1,0:T(8,128)(2,1)} fusion(s32[]{:T(128)S(6)} %select_n.327, bf16[1024,1024]{1,0:T(8,128)(2,1)} %all-gather.5.cloned.1.call-done, bf16[256,4096]{1,0:T(8,128)(2,1)} %copy-done.10, bf16[256,4096]{1,0:T(8,128)(2,1)S(1)} %copy-done.6, bf16[256,4096]{1,0:T(8,128)(2,1)} %copy-done.9, ...), kind=kOutput, calls=%fused_computation.32 | convolution fusion | flops 8631877632 | bytes 18874372 | tf_op jit(solution)/shard_map/dot_general | solution.py:165
  514.0 7.4 %fusion.18 = f32[256,1024]{1,0:T(8,128)} fusion(bf16[256,4096]{1,0:T(8,128)(2,1)} %broadcast_select_fusion.6, bf16[1,1024,4096]{2,1,0:T(8,128)(2,1)} %param.5), kind=kOutput, calls=%fused_computation.19 | convolution fusion | flops 2147483648 | bytes 11534336 | tf_op jit(solution)/shard_map/dot_general | solution.py:201
  521.5 7.2 %collective-permute-done.17 = bf16[256,4096]{1,0:T(8,128)(2,1)} collective-permute-done((bf16[256,4096]{1,0:T(8,128)(2,1)}, bf16[256,4096]{1,0:T(8,128)(2,1)}, u32[]{:S(2)}, u32[]{:S(2)}) %collective-permute-start.17) | collective-permute-done | bytes 2097184 | tf_op jit(solution)/shard_map/ppermute | solution.py:106
  535.5 2.4 add.237
  539.2 7.1 %fusion.14 = f32[256,1024]{1,0:T(8,128)} fusion(bf16[256,4096]{1,0:T(8,128)(2,1)S(1)} %add.237, bf16[1,1024,4096]{2,1,0:T(8,128)(2,1)} %param.5), kind=kOutput, calls=%fused_computation.15 | convolution fusion | flops 2147483648 | bytes 11534336 | tf_op jit(solution)/shard_map/dot_general | solution.py:201
  547.5 2.5 fusion.70
  550.0 25.5 %collective-permute-done.19 = bf16[256,4096]{1,0:T(8,128)(2,1)} collective-permute-done((bf16[256,4096]{1,0:T(8,128)(2,1)S(1)}, bf16[256,4096]{1,0:T(8,128)(2,1)}, u32[]{:S(2)}, u32[]{:S(2)}) %collective-permute-start.19) | collective-permute-done | bytes 2097184 | tf_op jit(solution)/shard_map/ppermute | solution.py:106
  575.5 7.6 %fusion.12 = f32[256,1024]{1,0:T(8,128)} fusion(bf16[1,1024,4096]{2,1,0:T(8,128)(2,1)} %param.5, bf16[256,4096]{1,0:T(8,128)(2,1)} %collective-permute-done.19, pred[]{:T(512)S(6)} %and.24, bf16[256,4096]{1,0:T(8,128)(2,1)} %collective-permute-done.18, pred[]{:T(512)S(6)} %and.27), kind=kOutput, calls=%fused_computation.13 | convolution fusion | flops 2150629376 | bytes 13631490 | tf_op jit(solution)/shard_map/dot_general | solution.py:201
  587.6 14.1 %convert_bitcast_fusion = bf16[1,1024,4096]{2,1,0:T(8,128)(2,1)} fusion(bf16[256,4096]{1,0:T(8,128)(2,1)S(1)} %fusion.66, bf16[256,4096]{1,0:T(8,128)(2,1)S(1)} %copy-done.8, bf16[256,4096]{1,0:T(8,128)(2,1)S(1)} %fusion.67, bf16[256,4096]{1,0:T(8,128)(2,1)} %fusion.48, s32[]{:T(128)S(6)} %select_n.327, bf16[1024,1024]{1,0:T(8,128)(2,1)} %all-gather.3.cloned.1.call-done), kind=kOutput, calls=%fused_computation.29 | convolution fusion | flops 8631877632 | bytes 18874372 | tf_op jit(solution)/shard_map/dot_general | solution.py:187
  601.8 11.2 %reduce-scatter.17.cloned.1.call-done = f32[256,256]{1,0:T(8,128)} async-done(((f32[256,1024]{1,0:T(8,128)}), f32[256,256]{1,0:T(8,128)}) %reduce-scatter.17.cloned.1.call-update) | async-done | bytes 262160 | tf_op jit(solution)/shard_map/reduce_scatter | solution.py:204
  (99 shorter events, 37.9 us)
Async XLA Ops:
  7.2 28.0 %all-gather.3.cloned.1.call-start = ((), (), s32[]{:S(2)}) async-start(), calls=%async_computation.6 | async-start | bytes 2621440 | tf_op jit(solution)/shard_map/all_gather | solution.py:124
  7.9 59.3 %all-gather.5.cloned.1.call-start = ((), (), s32[]{:S(2)}) async-start(), calls=%async_computation.7 | async-start | bytes 2621440 | tf_op jit(solution)/shard_map/all_gather | solution.py:126
  8.6 523.3 %reduce-scatter.7.cloned.1.call-start = ((), (), s32[]{:S(2)}) async-start(), calls=%async_computation.8 | async-start | bytes 5242880 | tf_op jit(solution)/shard_map/reduce_scatter | solution.py:173
  35.1 8.3 %copy-start.16 = (bf16[1024,1024]{1,0:T(8,128)(2,1)S(1)}, bf16[1024,1024]{1,0:T(8,128)(2,1)}, u32[]{:S(2)}) copy-start(bf16[1024,1024]{1,0:T(8,128)(2,1)} %all-gather.3.cloned.1.call-done) | copy-start | bytes 6291460
  35.1 21.2 %slice-start.2 = ((s8[8388608]{0:T(1024)(128)(4,1)}), s8[4194304]{0:T(1024)(128)(4,1)S(1)}, s32[]{:S(2)}) async-start(s8[8388608]{0:T(1024)(128)(4,1)} %bitcast.94), calls=%async_computation.16 | async-start | bytes 8388608
  42.5 13.8 %slice-start.3 = ((s8[8388608]{0:T(1024)(128)(4,1)}), s8[4194304]{0:T(1024)(128)(4,1)S(1)}, s32[]{:S(2)}) async-start(s8[8388608]{0:T(1024)(128)(4,1)} %bitcast.94), calls=%async_computation.17 | async-start | bytes 8388608
  42.5 39.5 %collective-permute-start.1 = (bf16[256,4096]{1,0:T(8,128)(2,1)}, bf16[256,4096]{1,0:T(8,128)(2,1)S(1)}, u32[]{:S(2)}, u32[]{:S(2)}) collective-permute-start(bf16[256,4096]{1,0:T(8,128)(2,1)} %fusion.39), channel_id=1, source_target_pairs={{12,8},{13,9},{14,10},{15,11},{28,24},{29,25},{30,26},{31,27}} | collective-permute-start | bytes 6291464 | tf_op jit(solution)/shard_map/ppermute | solution.py:106
  51.4 49.0 %collective-permute-start = (bf16[256,4096]{1,0:T(8,128)(2,1)}, bf16[256,4096]{1,0:T(8,128)(2,1)}, u32[]{:S(2)}, u32[]{:S(2)}) collective-permute-start(bf16[256,4096]{1,0:T(8,128)(2,1)} %fusion.36), channel_id=1, source_target_pairs={{0,4},{1,5},{2,6},{3,7},{16,20},{17,21},{18,22},{19,23}} | collective-permute-start | bytes 6291464 | tf_op jit(solution)/shard_map/ppermute | solution.py:106
  82.0 18.7 %copy-start = (bf16[1024,4096]{1,0:T(8,128)(2,1)S(1)}, bf16[1024,4096]{1,0:T(8,128)(2,1)}, u32[]{:S(2)}) copy-start(bf16[1024,4096]{1,0:T(8,128)(2,1)} %fusion.28) | copy-start | bytes 25165828
  104.2 50.8 %collective-permute-start.2 = (bf16[256,4096]{1,0:T(8,128)(2,1)}, bf16[256,4096]{1,0:T(8,128)(2,1)S(1)}, u32[]{:S(2)}, u32[]{:S(2)}) collective-permute-start(bf16[256,4096]{1,0:T(8,128)(2,1)} %get-tuple-element.42), channel_id=1, source_target_pairs={{0,4},{4,8},{1,5},{5,9},{2,6},{6,10},{3,7},{7,11},{16,20},{20,24},... | collective-permute-start | bytes 6291464 | tf_op jit(solution)/shard_map/ppermute | solution.py:106
  110.3 44.7 %collective-permute-start.4 = (bf16[256,4096]{1,0:T(8,128)(2,1)}, bf16[256,4096]{1,0:T(8,128)(2,1)}, u32[]{:S(2)}, u32[]{:S(2)}) collective-permute-start(bf16[256,4096]{1,0:T(8,128)(2,1)} %get-tuple-element.43), channel_id=1, source_target_pairs={{8,4},{12,8},{9,5},{13,9},{10,6},{14,10},{11,7},{15,11},{24,20},{2... | collective-permute-start | bytes 6291464 | tf_op jit(solution)/shard_map/ppermute | solution.py:106
  161.0 50.8 %collective-permute-start.3 = (bf16[256,4096]{1,0:T(8,128)(2,1)}, bf16[256,4096]{1,0:T(8,128)(2,1)S(1)}, u32[]{:S(2)}, u32[]{:S(2)}) collective-permute-start(bf16[256,4096]{1,0:T(8,128)(2,1)} %get-tuple-element.40), channel_id=1, source_target_pairs={{0,4},{4,8},{8,12},{1,5},{5,9},{9,13},{2,6},{6,10},{10,14},{3,7},{... | collective-permute-start | bytes 6291464 | tf_op jit(solution)/shard_map/ppermute | solution.py:106
  168.0 48.0 %collective-permute-start.5 = (bf16[256,4096]{1,0:T(8,128)(2,1)}, bf16[256,4096]{1,0:T(8,128)(2,1)}, u32[]{:S(2)}, u32[]{:S(2)}) collective-permute-start(bf16[256,4096]{1,0:T(8,128)(2,1)} %get-tuple-element.41), channel_id=1, source_target_pairs={{4,0},{8,4},{12,8},{5,1},{9,5},{13,9},{6,2},{10,6},{14,10},{7,3},{... | collective-permute-start | bytes 6291464 | tf_op jit(solution)/shard_map/ppermute | solution.py:106
  222.1 45.0 %collective-permute-start.6 = (bf16[256,4096]{1,0:T(8,128)(2,1)}, bf16[256,4096]{1,0:T(8,128)(2,1)S(1)}, u32[]{:S(2)}, u32[]{:S(2)}) collective-permute-start(bf16[256,4096]{1,0:T(8,128)(2,1)} %get-tuple-element.33), channel_id=1, source_target_pairs={{0,4},{4,8},{8,12},{1,5},{5,9},{9,13},{2,6},{6,10},{10,14},{3,7},{... | collective-permute-start | bytes 6291464 | tf_op jit(solution)/shard_map/ppermute | solution.py:106
  224.7 47.1 %collective-permute-start.8 = (bf16[256,4096]{1,0:T(8,128)(2,1)}, bf16[256,4096]{1,0:T(8,128)(2,1)}, u32[]{:S(2)}, u32[]{:S(2)}) collective-permute-start(bf16[256,4096]{1,0:T(8,128)(2,1)} %get-tuple-element.33), channel_id=1, source_target_pairs={{4,0},{8,4},{12,8},{5,1},{9,5},{13,9},{6,2},{10,6},{14,10},{7,3},{... | collective-permute-start | bytes 6291464 | tf_op jit(solution)/shard_map/ppermute | solution.py:106
  267.1 10.0 %copy-start.3 = (bf16[256,4096]{1,0:T(8,128)(2,1)}, bf16[256,4096]{1,0:T(8,128)(2,1)S(1)}, u32[]{:S(2)}) copy-start(bf16[256,4096]{1,0:T(8,128)(2,1)S(1)} %collective-permute-done.6) | copy-start | bytes 6291460
  277.2 46.0 %collective-permute-start.9 = (bf16[256,4096]{1,0:T(8,128)(2,1)}, bf16[256,4096]{1,0:T(8,128)(2,1)S(1)}, u32[]{:S(2)}, u32[]{:S(2)}) collective-permute-start(bf16[256,4096]{1,0:T(8,128)(2,1)} %get-tuple-element.38), channel_id=1, source_target_pairs={{4,0},{8,4},{12,8},{5,1},{9,5},{13,9},{6,2},{10,6},{14,10},{7,3},{... | collective-permute-start | bytes 6291464 | tf_op jit(solution)/shard_map/ppermute | solution.py:106
  278.4 46.0 %collective-permute-start.7 = (bf16[256,4096]{1,0:T(8,128)(2,1)}, bf16[256,4096]{1,0:T(8,128)(2,1)}, u32[]{:S(2)}, u32[]{:S(2)}) collective-permute-start(bf16[256,4096]{1,0:T(8,128)(2,1)} %get-tuple-element.39), channel_id=1, source_target_pairs={{4,8},{8,12},{0,4},{5,9},{9,13},{1,5},{6,10},{10,14},{2,6},{7,11},... | collective-permute-start | bytes 6291464 | tf_op jit(solution)/shard_map/ppermute | solution.py:106
  324.7 54.4 %slice-start = ((s8[8388608]{0:T(1024)(128)(4,1)}), s8[4194304]{0:T(1024)(128)(4,1)S(1)}, s32[]{:S(2)}) async-start(s8[8388608]{0:T(1024)(128)(4,1)} %bitcast.88), calls=%async_computation.14 | async-start | bytes 8388608
  324.8 54.4 %slice-start.1 = ((s8[8388608]{0:T(1024)(128)(4,1)}), s8[4194304]{0:T(1024)(128)(4,1)S(1)}, s32[]{:S(2)}) async-start(s8[8388608]{0:T(1024)(128)(4,1)} %bitcast.88), calls=%async_computation.15 | async-start | bytes 8388608
  328.7 63.1 %copy-start.5 = (bf16[256,4096]{1,0:T(8,128)(2,1)}, bf16[256,4096]{1,0:T(8,128)(2,1)S(1)}, u32[]{:S(2)}) copy-start(bf16[256,4096]{1,0:T(8,128)(2,1)S(1)} %get-tuple-element.44) | copy-start | bytes 6291460
  328.7 46.2 %collective-permute-start.10 = (bf16[256,4096]{1,0:T(8,128)(2,1)S(1)}, bf16[256,4096]{1,0:T(8,128)(2,1)S(1)}, u32[]{:S(2)}, u32[]{:S(2)}) collective-permute-start(bf16[256,4096]{1,0:T(8,128)(2,1)S(1)} %get-tuple-element.37), channel_id=1, source_target_pairs={{8,12},{0,4},{4,8},{9,13},{1,5},{5,9},{10,14},{2,6},{6,10},{11,15}... | collective-permute-start | bytes 6291464 | tf_op jit(solution)/shard_map/ppermute | solution.py:106
  334.8 44.3 %collective-permute-start.12 = (bf16[256,4096]{1,0:T(8,128)(2,1)S(1)}, bf16[256,4096]{1,0:T(8,128)(2,1)S(1)}, u32[]{:S(2)}, u32[]{:S(2)}) collective-permute-start(bf16[256,4096]{1,0:T(8,128)(2,1)S(1)} %get-tuple-element.36), channel_id=1, source_target_pairs={{4,0},{8,4},{12,8},{5,1},{9,5},{13,9},{6,2},{10,6},{14,10},{7,3},{... | collective-permute-start | bytes 6291464 | tf_op jit(solution)/shard_map/ppermute | solution.py:106
  382.3 43.7 %collective-permute-start.13 = (bf16[256,4096]{1,0:T(8,128)(2,1)}, bf16[256,4096]{1,0:T(8,128)(2,1)}, u32[]{:S(2)}, u32[]{:S(2)}) collective-permute-start(bf16[256,4096]{1,0:T(8,128)(2,1)} %get-tuple-element.34), channel_id=1, source_target_pairs={{4,0},{8,4},{12,8},{5,1},{9,5},{13,9},{6,2},{10,6},{14,10},{7,3},{... | collective-permute-start | bytes 6291464 | tf_op jit(solution)/shard_map/ppermute | solution.py:106
  383.6 7.9 %copy-start.4 = (bf16[256,4096]{1,0:T(8,128)(2,1)S(1)}, bf16[256,4096]{1,0:T(8,128)(2,1)}, u32[]{:S(2)}) copy-start(bf16[256,4096]{1,0:T(8,128)(2,1)} %copy-done.3) | copy-start | bytes 6291460
  383.6 46.3 %collective-permute-start.11 = (bf16[256,4096]{1,0:T(8,128)(2,1)S(1)}, bf16[256,4096]{1,0:T(8,128)(2,1)}, u32[]{:S(2)}, u32[]{:S(2)}) collective-permute-start(bf16[256,4096]{1,0:T(8,128)(2,1)S(1)} %get-tuple-element.35), channel_id=1, source_target_pairs={{0,4},{4,8},{8,12},{1,5},{5,9},{9,13},{2,6},{6,10},{10,14},{3,7},{... | collective-permute-start | bytes 6291464 | tf_op jit(solution)/shard_map/ppermute | solution.py:106
  391.6 1.3 copy-start.9
  391.8 1.7 copy-start.10
  432.3 169.5 %reduce-scatter.9.cloned.1.call-start = ((), (), s32[]{:S(2)}) async-start(), calls=%async_computation.9 | async-start | bytes 1310720 | tf_op jit(solution)/shard_map/reduce_scatter | solution.py:204
  441.1 42.7 %collective-permute-start.16 = (bf16[256,4096]{1,0:T(8,128)(2,1)}, bf16[256,4096]{1,0:T(8,128)(2,1)}, u32[]{:S(2)}, u32[]{:S(2)}) collective-permute-start(bf16[256,4096]{1,0:T(8,128)(2,1)} %fusion.48), channel_id=1, source_target_pairs={{4,0},{8,4},{12,8},{5,1},{9,5},{13,9},{6,2},{10,6},{14,10},{7,3},{... | collective-permute-start | bytes 6291464 | tf_op jit(solution)/shard_map/ppermute | solution.py:106
  442.3 45.8 %collective-permute-start.14 = (bf16[256,4096]{1,0:T(8,128)(2,1)}, bf16[256,4096]{1,0:T(8,128)(2,1)S(1)}, u32[]{:S(2)}, u32[]{:S(2)}) collective-permute-start(bf16[256,4096]{1,0:T(8,128)(2,1)} %fusion.48), channel_id=1, source_target_pairs={{0,4},{4,8},{8,12},{1,5},{5,9},{9,13},{2,6},{6,10},{10,14},{3,7},{... | collective-permute-start | bytes 6291464 | tf_op jit(solution)/shard_map/ppermute | solution.py:106
  455.1 146.6 %reduce-scatter.13.cloned.1.call-start = ((), (), s32[]{:S(2)}) async-start(), calls=%async_computation.11 | async-start | bytes 1310720 | tf_op jit(solution)/shard_map/reduce_scatter | solution.py:204
  486.9 41.8 %collective-permute-start.17 = (bf16[256,4096]{1,0:T(8,128)(2,1)}, bf16[256,4096]{1,0:T(8,128)(2,1)}, u32[]{:S(2)}, u32[]{:S(2)}) collective-permute-start(bf16[256,4096]{1,0:T(8,128)(2,1)} %broadcast_select_fusion.1), channel_id=1, source_target_pairs={{4,0},{8,4},{5,1},{9,5},{6,2},{10,6},{7,3},{11,7},{20,16},{24,20},... | collective-permute-start | bytes 6291464 | tf_op jit(solution)/shard_map/ppermute | solution.py:106
  488.2 1.9 copy-start.1
  490.1 40.3 %collective-permute-start.15 = (bf16[256,4096]{1,0:T(8,128)(2,1)}, bf16[256,4096]{1,0:T(8,128)(2,1)}, u32[]{:S(2)}, u32[]{:S(2)}) collective-permute-start(bf16[256,4096]{1,0:T(8,128)(2,1)} %broadcast_select_fusion.6), channel_id=1, source_target_pairs={{4,8},{8,12},{5,9},{9,13},{6,10},{10,14},{7,11},{11,15},{20,24},{2... | collective-permute-start | bytes 6291464 | tf_op jit(solution)/shard_map/ppermute | solution.py:106
  492.3 7.8 %copy-start.6 = (bf16[256,4096]{1,0:T(8,128)(2,1)S(1)}, bf16[256,4096]{1,0:T(8,128)(2,1)}, u32[]{:S(2)}) copy-start(bf16[256,4096]{1,0:T(8,128)(2,1)} %copy-done.5) | copy-start | bytes 6291460
  500.0 101.8 %reduce-scatter.11.cloned.1.call-start = ((), (), s32[]{:S(2)}) async-start(), calls=%async_computation.10 | async-start | bytes 1310720 | tf_op jit(solution)/shard_map/reduce_scatter | solution.py:204
  521.4 80.4 %reduce-scatter.15.cloned.1.call-start = ((), (), s32[]{:S(2)}) async-start(), calls=%async_computation.12 | async-start | bytes 1310720 | tf_op jit(solution)/shard_map/reduce_scatter | solution.py:204
  532.0 18.1 %collective-permute-start.18 = (bf16[256,4096]{1,0:T(8,128)(2,1)}, bf16[256,4096]{1,0:T(8,128)(2,1)}, u32[]{:S(2)}, u32[]{:S(2)}) collective-permute-start(bf16[256,4096]{1,0:T(8,128)(2,1)} %broadcast_select_fusion.8), channel_id=1, source_target_pairs={{8,12},{9,13},{10,14},{11,15},{24,28},{25,29},{26,30},{27,31}} | collective-permute-start | bytes 6291464 | tf_op jit(solution)/shard_map/ppermute | solution.py:106
  534.0 41.5 %collective-permute-start.19 = (bf16[256,4096]{1,0:T(8,128)(2,1)S(1)}, bf16[256,4096]{1,0:T(8,128)(2,1)}, u32[]{:S(2)}, u32[]{:S(2)}) collective-permute-start(bf16[256,4096]{1,0:T(8,128)(2,1)S(1)} %broadcast_select_fusion.4), channel_id=1, source_target_pairs={{4,0},{5,1},{6,2},{7,3},{20,16},{21,17},{22,18},{23,19}} | collective-permute-start | bytes 6291464 | tf_op jit(solution)/shard_map/ppermute | solution.py:106
  546.3 66.8 %reduce-scatter.17.cloned.1.call-start = ((), (), s32[]{:S(2)}) async-start(), calls=%async_computation.13 | async-start | bytes 1310720 | tf_op jit(solution)/shard_map/reduce_scatter | solution.py:204
  583.1 2.3 copy-start.2
  585.4 2.2 copy-start.8
  601.7 12.8 %copy-start.11 = (f32[256,256]{1,0:T(8,128)S(1)}, f32[256,256]{1,0:T(8,128)}, u32[]{:S(2)}) copy-start(f32[256,256]{1,0:T(8,128)} %reduce-scatter.9.cloned.1.call-done) | copy-start | bytes 786436
  601.7 12.8 %copy-start.12 = (f32[256,256]{1,0:T(8,128)S(1)}, f32[256,256]{1,0:T(8,128)}, u32[]{:S(2)}) copy-start(f32[256,256]{1,0:T(8,128)} %reduce-scatter.13.cloned.1.call-done) | copy-start | bytes 786436
  601.8 12.8 %copy-start.13 = (f32[256,256]{1,0:T(8,128)S(1)}, f32[256,256]{1,0:T(8,128)}, u32[]{:S(2)}) copy-start(f32[256,256]{1,0:T(8,128)} %reduce-scatter.11.cloned.1.call-done) | copy-start | bytes 786436
  601.8 12.7 %copy-start.14 = (f32[256,256]{1,0:T(8,128)S(1)}, f32[256,256]{1,0:T(8,128)}, u32[]{:S(2)}) copy-start(f32[256,256]{1,0:T(8,128)} %reduce-scatter.15.cloned.1.call-done) | copy-start | bytes 786436
  613.0 1.5 copy-start.15
  (1 other events, 1.3 us)
Sparse Core Ops, SparseCore 0:
  9.6 25.5 all-gather.2
  36.7 22.8 all-gather.4
  432.4 43.3 reduce-scatter.6
  478.3 24.8 reduce-scatter.8
  505.6 24.8 reduce-scatter.12
  533.1 24.8 reduce-scatter.10
  560.5 24.8 reduce-scatter.14
  588.1 24.8 reduce-scatter.16

commit v5 on v3

--- a/solution.py
+++ b/solution.py
@@ -134,13 +134,14 @@
         last = count - 1
         pos = lax.axis_index("r")
 
-        first_rows = jnp.concatenate(
+        own_rows = jnp.concatenate(
             [
-                lax.dynamic_slice_in_dim(x_rows, jnp.clip(last + pos, 0, last) * rows, rows, axis=0),
-                lax.dynamic_slice_in_dim(x_rows, jnp.clip(pos - last, 0, last) * rows, rows, axis=0),
+                lax.dynamic_slice_in_dim(hidden_in, jnp.clip(last + pos, 0, last) * rows, rows, axis=0),
+                lax.dynamic_slice_in_dim(hidden_in, jnp.clip(pos - last, 0, last) * rows, rows, axis=0),
             ],
             axis=0,
         )
+        first_rows = lax.all_gather(own_rows, "p", axis=1, tiled=True)
         first = jnp.dot(first_rows, up_tile, preferred_element_type=jnp.float32).astype(jnp.bfloat16)
         up_sum.first = (first[:rows], first[rows:])
         run_slot([(up_sum, 0)])

time: 630 us -> 626 us (level)
    all_gather x0 -> x1, waiting for transfers between devices: none -> 19.2 us  [on_device(): first_rows = lax.all_gather(own_rows, 'p', axis=1, tiled=True)]
    all_gather x1, waiting for transfers between devices: 26.4 us -> 8.18 us  [on_device(): x_rows = lax.all_gather(hidden_in, 'p', axis=1, tiled=True)]
    ppermute x20, waiting for transfers between devices: 313 us -> 303 us  [run_slot(): received.append(lax.ppermute(combined, 'r', pairs))]
    all_gather x1, waiting for transfers between devices: 0.01 us -> 9.67 us  [on_device(): grad_rows = lax.all_gather(out_grad, 'p', axis=1, tiled=True)]
  transfers between devices with their start and end apart: 28 -> 29, of which waited for: 16 -> 17; matrix products, arithmetic and copies ran while one was open for 25% -> 25% of each run, Pallas kernels for 0% -> 0%
where the time goes in v5:
time: 626 us; the launch traced here: 622 us
  waiting for transfers between devices  351 us (56%)
  matrix products  118 us (19%)
  other arithmetic  67.2 us (11%)
  starting transfers between devices  60.8 us (10%)
  between operations  14.7 us (2%)
  local copies, waits for them, and re-layouts  9.91 us (2%)
    ppermute x20, waiting for transfers between devices, run_slot(): received.append(lax.ppermute(combined, 'r', pairs))  303 us
    ppermute x20, starting transfers between devices, run_slot(): received.append(lax.ppermute(combined, 'r', pairs))  60.5 us
    dot_general x5, matrix products, on_device(): lax.dot_general(piece, up_tile, (((1,), (1,)), ((), ())), preferred_eleme...  37.4 us
    all_gather x1, waiting for transfers between devices, on_device(): first_rows = lax.all_gather(own_rows, 'p', axis=1, tiled=True)  19.2 us
    dot_general x1, matrix products, on_device(): jnp.dot(activation, down_tile, preferred_element_type=jnp.float32)  14.8 us
    dot_general x1, matrix products, on_device(): lax.dot_general(grad_rows, down_tile, (((1,), (1,)), ((), ())), preferred...  14.8 us
    dot_general x1, matrix products, on_device(): jnp.dot(x_rows, up_tile, preferred_element_type=jnp.float32)  14.8 us
    dot_general x1, matrix products, on_device(): lax.dot_general(rotate_rows(x_rows, turn), pre_grad, (((0,), (0,)), ((),...  14.1 us
  transfers between devices with their start and end apart: 29, of which 17 were waited for; matrix products, arithmetic and copies ran while one was open for 25% of the time, Pallas kernels for 0%

profile of v5, /device:TPU:0, one launch (start us, length us, event | category | flops | bytes accessed | tf_op | source)
XLA Modules:
  0.0 621.7 jit_solution(15696862370833054765)
XLA Ops:
  10.5 19.2 %all-gather.4.cloned.1.call-done = bf16[512,1024]{1,0:T(8,128)(2,1)} async-done(((bf16[512,256]{1,0:T(8,128)(2,1)}), bf16[512,1024]{1,0:T(8,128)(2,1)}) %all-gather.4.cloned.1.call-update) | async-done | bytes 1048592 | tf_op jit(solution)/shard_map/all_gather | solution.py:144
  29.7 8.2 %fusion.34 = bf16[512,4096]{1,0:T(8,128)(2,1)S(1)} fusion(bf16[512,1024]{1,0:T(8,128)(2,1)} %all-gather.4.cloned.1.call-done, bf16[1,1024,4096]{2,1,0:T(8,128)(2,1)} %param.5), kind=kOutput, calls=%fused_computation.32 | convolution fusion | flops 4297064448 | bytes 13631488 | tf_op jit(solution)/shard_map/dot_general | solution.py:145
  37.9 2.3 fusion.93
  42.3 3.7 collective-permute-start
  46.0 8.2 %all-gather.6.cloned.1.call-done = bf16[1024,1024]{1,0:T(8,128)(2,1)} async-done(((bf16[1024,256]{1,0:T(8,128)(2,1)}), bf16[1024,1024]{1,0:T(8,128)(2,1)}) %all-gather.6.cloned.1.call-update) | async-done | bytes 2097168 | tf_op jit(solution)/shard_map/all_gather | solution.py:124
  54.1 14.8 %fusion.26 = bf16[1024,4096]{1,0:T(8,128)(2,1)} fusion(bf16[1024,1024]{1,0:T(8,128)(2,1)} %all-gather.6.cloned.1.call-done, bf16[1,1024,4096]{2,1,0:T(8,128)(2,1)} %param.5), kind=kOutput, calls=%fused_computation.28 | convolution fusion | flops 8594128896 | bytes 18874368 | tf_op jit(solution)/shard_map/dot_general | solution.py:125
  68.9 9.7 %all-gather.8.cloned.1.call-done = bf16[1024,1024]{1,0:T(8,128)(2,1)} async-done(((bf16[1024,256]{1,0:T(8,128)(2,1)}), bf16[1024,1024]{1,0:T(8,128)(2,1)}) %all-gather.8.cloned.1.call-update) | async-done | bytes 2097168 | tf_op jit(solution)/shard_map/all_gather | solution.py:126
  78.6 14.8 %fusion.29 = bf16[1024,4096]{1,0:T(8,128)(2,1)} fusion(bf16[1024,1024]{1,0:T(8,128)(2,1)} %all-gather.8.cloned.1.call-done, bf16[1,4096,1024]{2,1,0:T(8,128)(2,1)} %param.6), kind=kOutput, calls=%fused_computation.29 | convolution fusion | flops 8594128896 | bytes 18874368 | tf_op jit(solution)/shard_map/dot_general | solution.py:127
  94.0 2.8 copy-done
  96.8 3.5 fusion.52
  100.3 3.5 collective-permute-start.2
  105.8 43.5 %collective-permute-done.2 = bf16[256,4096]{1,0:T(8,128)(2,1)S(1)} collective-permute-done((bf16[256,4096]{1,0:T(8,128)(2,1)}, bf16[256,4096]{1,0:T(8,128)(2,1)S(1)}, u32[]{:S(2)}, u32[]{:S(2)}) %collective-permute-start.2) | collective-permute-done | bytes 2097184 | tf_op jit(solution)/shard_map/ppermute | solution.py:106
  149.3 6.0 fusion.51
  155.3 8.9 %collective-permute-start.3 = (bf16[256,4096]{1,0:T(8,128)(2,1)}, bf16[256,4096]{1,0:T(8,128)(2,1)S(1)}, u32[]{:S(2)}, u32[]{:S(2)}) collective-permute-start(bf16[256,4096]{1,0:T(8,128)(2,1)} %get-tuple-element.40), channel_id=1, source_target_pairs={{0,4},{4,8},{8,12},{1,5},{5,9},{9,13},{2,6},{6,10},{10,14},{3,7},{... | collective-permute-start | bytes 6291464 | tf_op jit(solution)/shard_map/ppermute | solution.py:106
  165.7 42.8 %collective-permute-done.3 = bf16[256,4096]{1,0:T(8,128)(2,1)S(1)} collective-permute-done((bf16[256,4096]{1,0:T(8,128)(2,1)}, bf16[256,4096]{1,0:T(8,128)(2,1)S(1)}, u32[]{:S(2)}, u32[]{:S(2)}) %collective-permute-start.3) | collective-permute-done | bytes 2097184 | tf_op jit(solution)/shard_map/ppermute | solution.py:106
  208.5 4.2 collective-permute-done.5
  212.8 6.1 fusion.40
  222.3 42.1 %collective-permute-done.6 = bf16[256,4096]{1,0:T(8,128)(2,1)S(1)} collective-permute-done((bf16[256,4096]{1,0:T(8,128)(2,1)}, bf16[256,4096]{1,0:T(8,128)(2,1)S(1)}, u32[]{:S(2)}, u32[]{:S(2)}) %collective-permute-start.6) | collective-permute-done | bytes 2097184 | tf_op jit(solution)/shard_map/ppermute | solution.py:106
  264.5 4.2 collective-permute-done.8
  268.7 5.4 bitcast_select_fusion
  275.4 5.9 collective-permute-start.7
  281.2 39.5 %collective-permute-done.9 = bf16[256,4096]{1,0:T(8,128)(2,1)S(1)} collective-permute-done((bf16[256,4096]{1,0:T(8,128)(2,1)}, bf16[256,4096]{1,0:T(8,128)(2,1)S(1)}, u32[]{:S(2)}, u32[]{:S(2)}) %collective-permute-start.9) | collective-permute-done | bytes 2097184 | tf_op jit(solution)/shard_map/ppermute | solution.py:106
  322.3 3.9 fusion.54
  326.3 6.1 collective-permute-start.10
  333.7 39.4 %collective-permute-done.10 = bf16[256,4096]{1,0:T(8,128)(2,1)S(1)} collective-permute-done((bf16[256,4096]{1,0:T(8,128)(2,1)S(1)}, bf16[256,4096]{1,0:T(8,128)(2,1)S(1)}, u32[]{:S(2)}, u32[]{:S(2)}) %collective-permute-start.10) | collective-permute-done | bytes 2097184 | tf_op jit(solution)/shard_map/ppermute | solution.py:106
  373.1 4.2 collective-permute-done.12
  377.3 3.1 fusion.44
  381.8 6.5 %collective-permute-start.11 = (bf16[256,4096]{1,0:T(8,128)(2,1)S(1)}, bf16[256,4096]{1,0:T(8,128)(2,1)}, u32[]{:S(2)}, u32[]{:S(2)}) collective-permute-start(bf16[256,4096]{1,0:T(8,128)(2,1)S(1)} %get-tuple-element.35), channel_id=1, source_target_pairs={{0,4},{4,8},{8,12},{1,5},{5,9},{9,13},{2,6},{6,10},{10,14},{3,7},{... | collective-permute-start | bytes 6291464 | tf_op jit(solution)/shard_map/ppermute | solution.py:106
  392.1 14.8 %fusion.8 = f32[1024,1024]{1,0:T(8,128)} fusion(bf16[1,4096,1024]{2,1,0:T(8,128)(2,1)} %param.6, bf16[256,4096]{1,0:T(8,128)(2,1)S(1)} %select_add_fusion, bf16[256,4096]{1,0:T(8,128)(2,1)S(1)} %get-tuple-element.44, bf16[256,4096]{1,0:T(8,128)(2,1)S(1)} %select_add_fusion.1, bf16[256,4096]{1,0:T(8,128)(2,1)} %get-tuple-element.33), kind=kOutput, calls=%fused_computation.9 | convolution fusion | flops 8623489024 | bytes 20971520 | tf_op jit(solution)/shard_map/dot_general | solution.py:169
  406.9 17.9 %collective-permute-done.13 = bf16[256,4096]{1,0:T(8,128)(2,1)} collective-permute-done((bf16[256,4096]{1,0:T(8,128)(2,1)}, bf16[256,4096]{1,0:T(8,128)(2,1)}, u32[]{:S(2)}, u32[]{:S(2)}) %collective-permute-start.13) | collective-permute-done | bytes 2097184 | tf_op jit(solution)/shard_map/ppermute | solution.py:106
  424.8 3.9 select_convert_fusion
  428.7 2.3 select_convert_fusion.1
  431.1 8.6 %fusion.43 = bf16[256,4096]{1,0:T(8,128)(2,1)} fusion(f32[256,4096]{1,0:T(8,128)} %get-tuple-element.26, f32[256,4096]{1,0:T(8,128)} %select_convert_fusion, f32[256,4096]{1,0:T(8,128)} %select_convert_fusion.1, bf16[4,256,4096]{2,1,0:T(8,128)(2,1)} %bitcast.84, s32[]{:T(128)S(6)} %select_n.302), kind=kLoop, calls=%fused_computation.44 | loop fusion | flops 5242880 | bytes 16777220 | tf_op jit(solution)/shard_map/convert_element_type | solution.py:180
  440.9 4.9 collective-permute-start.14
  445.8 8.0 %fusion.20 = f32[256,1024]{1,0:T(8,128)} fusion(bf16[256,4096]{1,0:T(8,128)(2,1)} %fusion.43, bf16[1,1024,4096]{2,1,0:T(8,128)(2,1)} %param.5), kind=kOutput, calls=%fused_computation.21 | convolution fusion | flops 2147483648 | bytes 11534336 | tf_op jit(solution)/shard_map/dot_general | solution.py:206
  453.8 29.3 %collective-permute-done.16 = bf16[256,4096]{1,0:T(8,128)(2,1)} collective-permute-done((bf16[256,4096]{1,0:T(8,128)(2,1)}, bf16[256,4096]{1,0:T(8,128)(2,1)}, u32[]{:S(2)}, u32[]{:S(2)}) %collective-permute-start.16) | collective-permute-done | bytes 2097184 | tf_op jit(solution)/shard_map/ppermute | solution.py:106
  483.1 3.1 broadcast_select_fusion.1
  491.6 7.7 %fusion.16 = f32[256,1024]{1,0:T(8,128)} fusion(bf16[256,4096]{1,0:T(8,128)(2,1)} %broadcast_select_fusion.1, bf16[1,1024,4096]{2,1,0:T(8,128)(2,1)} %param.5), kind=kOutput, calls=%fused_computation.17 | convolution fusion | flops 2147483648 | bytes 11534336 | tf_op jit(solution)/shard_map/dot_general | solution.py:206
  499.4 14.0 %convolution_convert_fusion = bf16[4096,1024]{1,0:T(8,128)(2,1)} fusion(s32[]{:T(128)S(6)} %select_n.327, bf16[1024,1024]{1,0:T(8,128)(2,1)} %all-gather.8.cloned.1.call-done, bf16[256,4096]{1,0:T(8,128)(2,1)} %copy-done.10, bf16[256,4096]{1,0:T(8,128)(2,1)S(1)} %copy-done.6, bf16[256,4096]{1,0:T(8,128)(2,1)} %copy-done.9, ...), kind=kOutput, calls=%fused_computation.30 | convolution fusion | flops 8631877632 | bytes 18874372 | tf_op jit(solution)/shard_map/dot_general | solution.py:170
  513.4 7.4 %fusion.18 = f32[256,1024]{1,0:T(8,128)} fusion(bf16[256,4096]{1,0:T(8,128)(2,1)} %broadcast_select_fusion.6, bf16[1,1024,4096]{2,1,0:T(8,128)(2,1)} %param.5), kind=kOutput, calls=%fused_computation.19 | convolution fusion | flops 2147483648 | bytes 11534336 | tf_op jit(solution)/shard_map/dot_general | solution.py:206
  520.8 7.8 %collective-permute-done.17 = bf16[256,4096]{1,0:T(8,128)(2,1)} collective-permute-done((bf16[256,4096]{1,0:T(8,128)(2,1)}, bf16[256,4096]{1,0:T(8,128)(2,1)}, u32[]{:S(2)}, u32[]{:S(2)}) %collective-permute-start.17) | collective-permute-done | bytes 2097184 | tf_op jit(solution)/shard_map/ppermute | solution.py:106
  535.3 2.4 add.237
  539.0 7.0 %fusion.14 = f32[256,1024]{1,0:T(8,128)} fusion(bf16[256,4096]{1,0:T(8,128)(2,1)S(1)} %add.237, bf16[1,1024,4096]{2,1,0:T(8,128)(2,1)} %param.5), kind=kOutput, calls=%fused_computation.15 | convolution fusion | flops 2147483648 | bytes 11534336 | tf_op jit(solution)/shard_map/dot_general | solution.py:206
  547.3 2.5 fusion.65
  549.8 26.7 %collective-permute-done.19 = bf16[256,4096]{1,0:T(8,128)(2,1)} collective-permute-done((bf16[256,4096]{1,0:T(8,128)(2,1)S(1)}, bf16[256,4096]{1,0:T(8,128)(2,1)}, u32[]{:S(2)}, u32[]{:S(2)}) %collective-permute-start.19) | collective-permute-done | bytes 2097184 | tf_op jit(solution)/shard_map/ppermute | solution.py:106
  576.5 7.4 %fusion.12 = f32[256,1024]{1,0:T(8,128)} fusion(bf16[1,1024,4096]{2,1,0:T(8,128)(2,1)} %param.5, bf16[256,4096]{1,0:T(8,128)(2,1)} %collective-permute-done.19, pred[]{:T(512)S(6)} %and.24, bf16[256,4096]{1,0:T(8,128)(2,1)} %collective-permute-done.18, pred[]{:T(512)S(6)} %and.27), kind=kOutput, calls=%fused_computation.13 | convolution fusion | flops 2150629376 | bytes 13631490 | tf_op jit(solution)/shard_map/dot_general | solution.py:206
  588.4 14.1 %convert_bitcast_fusion = bf16[1,1024,4096]{2,1,0:T(8,128)(2,1)} fusion(bf16[256,4096]{1,0:T(8,128)(2,1)S(1)} %fusion.61, bf16[256,4096]{1,0:T(8,128)(2,1)S(1)} %copy-done.8, bf16[256,4096]{1,0:T(8,128)(2,1)S(1)} %fusion.62, bf16[256,4096]{1,0:T(8,128)(2,1)} %fusion.43, s32[]{:T(128)S(6)} %select_n.327, bf16[1024,1024]{1,0:T(8,128)(2,1)} %all-gather.6.cloned.1.call-done), kind=kOutput, calls=%fused_computation.27 | convolution fusion | flops 8631877632 | bytes 18874372 | tf_op jit(solution)/shard_map/dot_general | solution.py:192
  602.6 9.7 %reduce-scatter.17.cloned.1.call-done = f32[256,256]{1,0:T(8,128)} async-done(((f32[256,1024]{1,0:T(8,128)}), f32[256,256]{1,0:T(8,128)}) %reduce-scatter.17.cloned.1.call-update) | async-done | bytes 262160 | tf_op jit(solution)/shard_map/reduce_scatter | solution.py:209
  (97 shorter events, 45.3 us)
Async XLA Ops:
  7.2 22.5 %all-gather.4.cloned.1.call-start = ((), (), s32[]{:S(2)}) async-start(), calls=%async_computation.6 | async-start | bytes 1310720 | tf_op jit(solution)/shard_map/all_gather | solution.py:144
  9.0 45.2 %all-gather.6.cloned.1.call-start = ((), (), s32[]{:S(2)}) async-start(), calls=%async_computation.7 | async-start | bytes 2621440 | tf_op jit(solution)/shard_map/all_gather | solution.py:124
  9.7 68.8 %all-gather.8.cloned.1.call-start = ((), (), s32[]{:S(2)}) async-start(), calls=%async_computation.8 | async-start | bytes 2621440 | tf_op jit(solution)/shard_map/all_gather | solution.py:126
  10.5 521.4 %reduce-scatter.7.cloned.1.call-start = ((), (), s32[]{:S(2)}) async-start(), calls=%async_computation.9 | async-start | bytes 5242880 | tf_op jit(solution)/shard_map/reduce_scatter | solution.py:178
  40.3 53.1 %collective-permute-start.1 = (bf16[256,4096]{1,0:T(8,128)(2,1)}, bf16[256,4096]{1,0:T(8,128)(2,1)}, u32[]{:S(2)}, u32[]{:S(2)}) collective-permute-start(bf16[256,4096]{1,0:T(8,128)(2,1)} %get-tuple-element.45), channel_id=1, source_target_pairs={{12,8},{13,9},{14,10},{15,11},{28,24},{29,25},{30,26},{31,27}} | collective-permute-start | bytes 6291464 | tf_op jit(solution)/shard_map/ppermute | solution.py:106
  42.3 51.4 %collective-permute-start = (bf16[256,4096]{1,0:T(8,128)(2,1)}, bf16[256,4096]{1,0:T(8,128)(2,1)S(1)}, u32[]{:S(2)}, u32[]{:S(2)}) collective-permute-start(bf16[256,4096]{1,0:T(8,128)(2,1)} %get-tuple-element.46), channel_id=1, source_target_pairs={{0,4},{1,5},{2,6},{3,7},{16,20},{17,21},{18,22},{19,23}} | collective-permute-start | bytes 6291464 | tf_op jit(solution)/shard_map/ppermute | solution.py:106
  93.4 3.4 copy-start
  100.3 49.0 %collective-permute-start.2 = (bf16[256,4096]{1,0:T(8,128)(2,1)}, bf16[256,4096]{1,0:T(8,128)(2,1)S(1)}, u32[]{:S(2)}, u32[]{:S(2)}) collective-permute-start(bf16[256,4096]{1,0:T(8,128)(2,1)} %get-tuple-element.42), channel_id=1, source_target_pairs={{0,4},{4,8},{1,5},{5,9},{2,6},{6,10},{3,7},{7,11},{16,20},{20,24},... | collective-permute-start | bytes 6291464 | tf_op jit(solution)/shard_map/ppermute | solution.py:106
  103.8 45.5 %collective-permute-start.4 = (bf16[256,4096]{1,0:T(8,128)(2,1)}, bf16[256,4096]{1,0:T(8,128)(2,1)}, u32[]{:S(2)}, u32[]{:S(2)}) collective-permute-start(bf16[256,4096]{1,0:T(8,128)(2,1)} %get-tuple-element.43), channel_id=1, source_target_pairs={{8,4},{12,8},{9,5},{13,9},{10,6},{14,10},{11,7},{15,11},{24,20},{2... | collective-permute-start | bytes 6291464 | tf_op jit(solution)/shard_map/ppermute | solution.py:106
  155.3 53.2 %collective-permute-start.3 = (bf16[256,4096]{1,0:T(8,128)(2,1)}, bf16[256,4096]{1,0:T(8,128)(2,1)S(1)}, u32[]{:S(2)}, u32[]{:S(2)}) collective-permute-start(bf16[256,4096]{1,0:T(8,128)(2,1)} %get-tuple-element.40), channel_id=1, source_target_pairs={{0,4},{4,8},{8,12},{1,5},{5,9},{9,13},{2,6},{6,10},{10,14},{3,7},{... | collective-permute-start | bytes 6291464 | tf_op jit(solution)/shard_map/ppermute | solution.py:106
  164.2 48.6 %collective-permute-start.5 = (bf16[256,4096]{1,0:T(8,128)(2,1)}, bf16[256,4096]{1,0:T(8,128)(2,1)}, u32[]{:S(2)}, u32[]{:S(2)}) collective-permute-start(bf16[256,4096]{1,0:T(8,128)(2,1)} %get-tuple-element.41), channel_id=1, source_target_pairs={{4,0},{8,4},{12,8},{5,1},{9,5},{13,9},{6,2},{10,6},{14,10},{7,3},{... | collective-permute-start | bytes 6291464 | tf_op jit(solution)/shard_map/ppermute | solution.py:106
  218.8 45.6 %collective-permute-start.6 = (bf16[256,4096]{1,0:T(8,128)(2,1)}, bf16[256,4096]{1,0:T(8,128)(2,1)S(1)}, u32[]{:S(2)}, u32[]{:S(2)}) collective-permute-start(bf16[256,4096]{1,0:T(8,128)(2,1)} %get-tuple-element.33), channel_id=1, source_target_pairs={{0,4},{4,8},{8,12},{1,5},{5,9},{9,13},{2,6},{6,10},{10,14},{3,7},{... | collective-permute-start | bytes 6291464 | tf_op jit(solution)/shard_map/ppermute | solution.py:106
  221.0 47.7 %collective-permute-start.8 = (bf16[256,4096]{1,0:T(8,128)(2,1)}, bf16[256,4096]{1,0:T(8,128)(2,1)}, u32[]{:S(2)}, u32[]{:S(2)}) collective-permute-start(bf16[256,4096]{1,0:T(8,128)(2,1)} %get-tuple-element.33), channel_id=1, source_target_pairs={{4,0},{8,4},{12,8},{5,1},{9,5},{13,9},{6,2},{10,6},{14,10},{7,3},{... | collective-permute-start | bytes 6291464 | tf_op jit(solution)/shard_map/ppermute | solution.py:106
  264.5 9.6 %copy-start.3 = (bf16[256,4096]{1,0:T(8,128)(2,1)}, bf16[256,4096]{1,0:T(8,128)(2,1)S(1)}, u32[]{:S(2)}) copy-start(bf16[256,4096]{1,0:T(8,128)(2,1)S(1)} %collective-permute-done.6) | copy-start | bytes 6291460
  274.1 46.6 %collective-permute-start.9 = (bf16[256,4096]{1,0:T(8,128)(2,1)}, bf16[256,4096]{1,0:T(8,128)(2,1)S(1)}, u32[]{:S(2)}, u32[]{:S(2)}) collective-permute-start(bf16[256,4096]{1,0:T(8,128)(2,1)} %get-tuple-element.38), channel_id=1, source_target_pairs={{4,0},{8,4},{12,8},{5,1},{9,5},{13,9},{6,2},{10,6},{14,10},{7,3},{... | collective-permute-start | bytes 6291464 | tf_op jit(solution)/shard_map/ppermute | solution.py:106
  275.4 46.6 %collective-permute-start.7 = (bf16[256,4096]{1,0:T(8,128)(2,1)}, bf16[256,4096]{1,0:T(8,128)(2,1)}, u32[]{:S(2)}, u32[]{:S(2)}) collective-permute-start(bf16[256,4096]{1,0:T(8,128)(2,1)} %get-tuple-element.39), channel_id=1, source_target_pairs={{4,8},{8,12},{0,4},{5,9},{9,13},{1,5},{6,10},{10,14},{2,6},{7,11},... | collective-permute-start | bytes 6291464 | tf_op jit(solution)/shard_map/ppermute | solution.py:106
  322.3 55.1 %slice-start = ((s8[8388608]{0:T(1024)(128)(4,1)}), s8[4194304]{0:T(1024)(128)(4,1)S(1)}, s32[]{:S(2)}) async-start(s8[8388608]{0:T(1024)(128)(4,1)} %bitcast.85), calls=%async_computation.15 | async-start | bytes 8388608
  322.3 55.0 %slice-start.1 = ((s8[8388608]{0:T(1024)(128)(4,1)}), s8[4194304]{0:T(1024)(128)(4,1)S(1)}, s32[]{:S(2)}) async-start(s8[8388608]{0:T(1024)(128)(4,1)} %bitcast.85), calls=%async_computation.16 | async-start | bytes 8388608
  326.3 64.1 %copy-start.5 = (bf16[256,4096]{1,0:T(8,128)(2,1)}, bf16[256,4096]{1,0:T(8,128)(2,1)S(1)}, u32[]{:S(2)}) copy-start(bf16[256,4096]{1,0:T(8,128)(2,1)S(1)} %get-tuple-element.44) | copy-start | bytes 6291460
  326.3 46.8 %collective-permute-start.10 = (bf16[256,4096]{1,0:T(8,128)(2,1)S(1)}, bf16[256,4096]{1,0:T(8,128)(2,1)S(1)}, u32[]{:S(2)}, u32[]{:S(2)}) collective-permute-start(bf16[256,4096]{1,0:T(8,128)(2,1)S(1)} %get-tuple-element.37), channel_id=1, source_target_pairs={{8,12},{0,4},{4,8},{9,13},{1,5},{5,9},{10,14},{2,6},{6,10},{11,15}... | collective-permute-start | bytes 6291464 | tf_op jit(solution)/shard_map/ppermute | solution.py:106
  332.4 45.0 %collective-permute-start.12 = (bf16[256,4096]{1,0:T(8,128)(2,1)S(1)}, bf16[256,4096]{1,0:T(8,128)(2,1)S(1)}, u32[]{:S(2)}, u32[]{:S(2)}) collective-permute-start(bf16[256,4096]{1,0:T(8,128)(2,1)S(1)} %get-tuple-element.36), channel_id=1, source_target_pairs={{4,0},{8,4},{12,8},{5,1},{9,5},{13,9},{6,2},{10,6},{14,10},{7,3},{... | collective-permute-start | bytes 6291464 | tf_op jit(solution)/shard_map/ppermute | solution.py:106
  380.5 44.3 %collective-permute-start.13 = (bf16[256,4096]{1,0:T(8,128)(2,1)}, bf16[256,4096]{1,0:T(8,128)(2,1)}, u32[]{:S(2)}, u32[]{:S(2)}) collective-permute-start(bf16[256,4096]{1,0:T(8,128)(2,1)} %get-tuple-element.34), channel_id=1, source_target_pairs={{4,0},{8,4},{12,8},{5,1},{9,5},{13,9},{6,2},{10,6},{14,10},{7,3},{... | collective-permute-start | bytes 6291464 | tf_op jit(solution)/shard_map/ppermute | solution.py:106
  381.7 8.3 %copy-start.4 = (bf16[256,4096]{1,0:T(8,128)(2,1)S(1)}, bf16[256,4096]{1,0:T(8,128)(2,1)}, u32[]{:S(2)}) copy-start(bf16[256,4096]{1,0:T(8,128)(2,1)} %copy-done.3) | copy-start | bytes 6291460
  381.8 46.9 %collective-permute-start.11 = (bf16[256,4096]{1,0:T(8,128)(2,1)S(1)}, bf16[256,4096]{1,0:T(8,128)(2,1)}, u32[]{:S(2)}, u32[]{:S(2)}) collective-permute-start(bf16[256,4096]{1,0:T(8,128)(2,1)S(1)} %get-tuple-element.35), channel_id=1, source_target_pairs={{0,4},{4,8},{8,12},{1,5},{5,9},{9,13},{2,6},{6,10},{10,14},{3,7},{... | collective-permute-start | bytes 6291464 | tf_op jit(solution)/shard_map/ppermute | solution.py:106
  390.1 1.3 copy-start.9
  390.4 1.7 copy-start.10
  431.0 171.5 %reduce-scatter.9.cloned.1.call-start = ((), (), s32[]{:S(2)}) async-start(), calls=%async_computation.10 | async-start | bytes 1310720 | tf_op jit(solution)/shard_map/reduce_scatter | solution.py:209
  439.6 43.5 %collective-permute-start.16 = (bf16[256,4096]{1,0:T(8,128)(2,1)}, bf16[256,4096]{1,0:T(8,128)(2,1)}, u32[]{:S(2)}, u32[]{:S(2)}) collective-permute-start(bf16[256,4096]{1,0:T(8,128)(2,1)} %fusion.43), channel_id=1, source_target_pairs={{4,0},{8,4},{12,8},{5,1},{9,5},{13,9},{6,2},{10,6},{14,10},{7,3},{... | collective-permute-start | bytes 6291464 | tf_op jit(solution)/shard_map/ppermute | solution.py:106
  440.9 46.6 %collective-permute-start.14 = (bf16[256,4096]{1,0:T(8,128)(2,1)}, bf16[256,4096]{1,0:T(8,128)(2,1)S(1)}, u32[]{:S(2)}, u32[]{:S(2)}) collective-permute-start(bf16[256,4096]{1,0:T(8,128)(2,1)} %fusion.43), channel_id=1, source_target_pairs={{0,4},{4,8},{8,12},{1,5},{5,9},{9,13},{2,6},{6,10},{10,14},{3,7},{... | collective-permute-start | bytes 6291464 | tf_op jit(solution)/shard_map/ppermute | solution.py:106
  453.8 148.7 %reduce-scatter.13.cloned.1.call-start = ((), (), s32[]{:S(2)}) async-start(), calls=%async_computation.12 | async-start | bytes 1310720 | tf_op jit(solution)/shard_map/reduce_scatter | solution.py:209
  486.2 42.3 %collective-permute-start.17 = (bf16[256,4096]{1,0:T(8,128)(2,1)}, bf16[256,4096]{1,0:T(8,128)(2,1)}, u32[]{:S(2)}, u32[]{:S(2)}) collective-permute-start(bf16[256,4096]{1,0:T(8,128)(2,1)} %broadcast_select_fusion.1), channel_id=1, source_target_pairs={{4,0},{8,4},{5,1},{9,5},{6,2},{10,6},{7,3},{11,7},{20,16},{24,20},... | collective-permute-start | bytes 6291464 | tf_op jit(solution)/shard_map/ppermute | solution.py:106
  487.5 1.9 copy-start.1
  489.5 40.8 %collective-permute-start.15 = (bf16[256,4096]{1,0:T(8,128)(2,1)}, bf16[256,4096]{1,0:T(8,128)(2,1)}, u32[]{:S(2)}, u32[]{:S(2)}) collective-permute-start(bf16[256,4096]{1,0:T(8,128)(2,1)} %broadcast_select_fusion.6), channel_id=1, source_target_pairs={{4,8},{8,12},{5,9},{9,13},{6,10},{10,14},{7,11},{11,15},{20,24},{2... | collective-permute-start | bytes 6291464 | tf_op jit(solution)/shard_map/ppermute | solution.py:106
  491.6 7.8 %copy-start.6 = (bf16[256,4096]{1,0:T(8,128)(2,1)S(1)}, bf16[256,4096]{1,0:T(8,128)(2,1)}, u32[]{:S(2)}) copy-start(bf16[256,4096]{1,0:T(8,128)(2,1)} %copy-done.5) | copy-start | bytes 6291460
  499.3 103.2 %reduce-scatter.11.cloned.1.call-start = ((), (), s32[]{:S(2)}) async-start(), calls=%async_computation.11 | async-start | bytes 1310720 | tf_op jit(solution)/shard_map/reduce_scatter | solution.py:209
  520.8 81.8 %reduce-scatter.15.cloned.1.call-start = ((), (), s32[]{:S(2)}) async-start(), calls=%async_computation.13 | async-start | bytes 1310720 | tf_op jit(solution)/shard_map/reduce_scatter | solution.py:209
  531.8 18.0 %collective-permute-start.18 = (bf16[256,4096]{1,0:T(8,128)(2,1)}, bf16[256,4096]{1,0:T(8,128)(2,1)}, u32[]{:S(2)}, u32[]{:S(2)}) collective-permute-start(bf16[256,4096]{1,0:T(8,128)(2,1)} %broadcast_select_fusion.8), channel_id=1, source_target_pairs={{8,12},{9,13},{10,14},{11,15},{24,28},{25,29},{26,30},{27,31}} | collective-permute-start | bytes 6291464 | tf_op jit(solution)/shard_map/ppermute | solution.py:106
  533.8 42.7 %collective-permute-start.19 = (bf16[256,4096]{1,0:T(8,128)(2,1)S(1)}, bf16[256,4096]{1,0:T(8,128)(2,1)}, u32[]{:S(2)}, u32[]{:S(2)}) collective-permute-start(bf16[256,4096]{1,0:T(8,128)(2,1)S(1)} %broadcast_select_fusion.4), channel_id=1, source_target_pairs={{4,0},{5,1},{6,2},{7,3},{20,16},{21,17},{22,18},{23,19}} | collective-permute-start | bytes 6291464 | tf_op jit(solution)/shard_map/ppermute | solution.py:106
  537.7 1.3 copy-start.7
  546.0 66.3 %reduce-scatter.17.cloned.1.call-start = ((), (), s32[]{:S(2)}) async-start(), calls=%async_computation.14 | async-start | bytes 1310720 | tf_op jit(solution)/shard_map/reduce_scatter | solution.py:209
  584.0 2.3 copy-start.2
  586.2 2.2 copy-start.8
  602.5 11.4 %copy-start.11 = (f32[256,256]{1,0:T(8,128)S(1)}, f32[256,256]{1,0:T(8,128)}, u32[]{:S(2)}) copy-start(f32[256,256]{1,0:T(8,128)} %reduce-scatter.9.cloned.1.call-done) | copy-start | bytes 786436
  602.5 11.3 %copy-start.12 = (f32[256,256]{1,0:T(8,128)S(1)}, f32[256,256]{1,0:T(8,128)}, u32[]{:S(2)}) copy-start(f32[256,256]{1,0:T(8,128)} %reduce-scatter.13.cloned.1.call-done) | copy-start | bytes 786436
  602.6 11.3 %copy-start.13 = (f32[256,256]{1,0:T(8,128)S(1)}, f32[256,256]{1,0:T(8,128)}, u32[]{:S(2)}) copy-start(f32[256,256]{1,0:T(8,128)} %reduce-scatter.11.cloned.1.call-done) | copy-start | bytes 786436
  602.6 11.3 %copy-start.14 = (f32[256,256]{1,0:T(8,128)S(1)}, f32[256,256]{1,0:T(8,128)}, u32[]{:S(2)}) copy-start(f32[256,256]{1,0:T(8,128)} %reduce-scatter.15.cloned.1.call-done) | copy-start | bytes 786436
  612.3 1.5 copy-start.15
Sparse Core Ops, SparseCore 0:
  10.1 19.5 all-gather.3
  31.3 22.8 all-gather.5
  55.7 22.8 all-gather.7
  431.1 43.7 reduce-scatter.6
  477.5 24.8 reduce-scatter.8
  504.8 24.8 reduce-scatter.12
  532.4 24.8 reduce-scatter.10
  559.8 24.8 reduce-scatter.14
  587.4 24.8 reduce-scatter.16

commit v6 on v5

--- a/solution.py
+++ b/solution.py
@@ -145,12 +145,16 @@
         first = jnp.dot(first_rows, up_tile, preferred_element_type=jnp.float32).astype(jnp.bfloat16)
         up_sum.first = (first[:rows], first[rows:])
         run_slot([(up_sum, 0)])
-        up_sum.up_in, up_sum.down_in, up_sum.shares, grad_terms = lax.optimization_barrier(
-            (up_sum.up_in, up_sum.down_in, up_sum.shares, grad_terms)
-        )
-    grad_sum = LineReduce(grad_terms)
+        up_sum.up_in, up_sum.down_in, up_sum.shares = lax.optimization_barrier(
+            (up_sum.up_in, up_sum.down_in, up_sum.shares)
+        )
     for step in range(1, count - 1):
         run_slot([(up_sum, step)])
+        if step == 1:
+            up_sum.up_in, up_sum.down_in, grad_terms = lax.optimization_barrier(
+                (up_sum.up_in, up_sum.down_in, grad_terms)
+            )
+    grad_sum = LineReduce(grad_terms)
     preact = up_sum.result()
     act_gather = LineGather(gelu_value(preact).astype(jnp.bfloat16))
     if count > 1:

time: 626 us -> 617 us (0.986)
  waiting for transfers between devices: 351 us -> 333 us
  starting transfers between devices: 60.8 us -> 73.8 us
    ppermute x20, waiting for transfers between devices: 303 us -> 290 us  [run_slot(): received.append(lax.ppermute(combined, 'r', pairs))]
    ppermute x20, starting transfers between devices: 60.5 us -> 73 us  [run_slot(): received.append(lax.ppermute(combined, 'r', pairs))]
    all_gather x1, waiting for transfers between devices: 9.67 us -> 0.02 us  [on_device(): grad_rows = lax.all_gather(out_grad, 'p', axis=1, tiled=True)]
where the time goes in v6:
time: 617 us; the launch traced here: 609 us
  waiting for transfers between devices  333 us (54%)
  matrix products  116 us (19%)
  starting transfers between devices  73.8 us (12%)
  other arithmetic  64.4 us (10%)
  between operations  14.9 us (2%)
  local copies, waits for them, and re-layouts  7.14 us (1%)
    ppermute x20, waiting for transfers between devices, run_slot(): received.append(lax.ppermute(combined, 'r', pairs))  290 us
    ppermute x20, starting transfers between devices, run_slot(): received.append(lax.ppermute(combined, 'r', pairs))  73 us
    dot_general x5, matrix products, on_device(): lax.dot_general(piece, up_tile, (((1,), (1,)), ((), ())), preferred_eleme...  37.4 us
    all_gather x1, waiting for transfers between devices, on_device(): first_rows = lax.all_gather(own_rows, 'p', axis=1, tiled=True)  19.9 us
    dot_general x1, matrix products, on_device(): lax.dot_general(grad_rows, down_tile, (((1,), (1,)), ((), ())), preferred...  14.8 us
    dot_general x1, matrix products, on_device(): jnp.dot(activation, down_tile, preferred_element_type=jnp.float32)  14.8 us
    dot_general x1, matrix products, on_device(): lax.dot_general(rotate_rows(x_rows, turn), pre_grad, (((0,), (0,)), ((),...  14.1 us
    dot_general x1, matrix products, on_device(): lax.dot_general(activation, grad_turned, (((0,), (0,)), ((), ())), prefer...  14 us
  transfers between devices with their start and end apart: 29, of which 17 were waited for; matrix products, arithmetic and copies ran while one was open for 25% of the time, Pallas kernels for 0%

profile of v6, /device:TPU:0, one launch (start us, length us, event | category | flops | bytes accessed | tf_op | source)
XLA Modules:
  0.0 609.4 jit_solution(12808142847637678107)
XLA Ops:
  9.8 19.9 %all-gather.4.cloned.1.call-done = bf16[512,1024]{1,0:T(8,128)(2,1)} async-done(((bf16[512,256]{1,0:T(8,128)(2,1)}), bf16[512,1024]{1,0:T(8,128)(2,1)}) %all-gather.4.cloned.1.call-update) | async-done | bytes 1048592 | tf_op jit(solution)/shard_map/all_gather | solution.py:144
  29.7 8.2 %fusion.34 = bf16[512,4096]{1,0:T(8,128)(2,1)S(1)} fusion(bf16[512,1024]{1,0:T(8,128)(2,1)} %all-gather.4.cloned.1.call-done, bf16[1,1024,4096]{2,1,0:T(8,128)(2,1)} %param.5), kind=kOutput, calls=%fused_computation.32 | convolution fusion | flops 4297064448 | bytes 13631488 | tf_op jit(solution)/shard_map/dot_general | solution.py:145
  41.1 4.8 collective-permute-start
  45.9 8.2 %all-gather.6.cloned.1.call-done = bf16[1024,1024]{1,0:T(8,128)(2,1)} async-done(((bf16[1024,256]{1,0:T(8,128)(2,1)}), bf16[1024,1024]{1,0:T(8,128)(2,1)}) %all-gather.6.cloned.1.call-update) | async-done | bytes 2097168 | tf_op jit(solution)/shard_map/all_gather | solution.py:124
  54.1 12.8 %fusion.26 = bf16[1024,4096]{1,0:T(8,128)(2,1)S(1)} fusion(bf16[1024,1024]{1,0:T(8,128)(2,1)} %all-gather.6.cloned.1.call-done, bf16[1,1024,4096]{2,1,0:T(8,128)(2,1)} %param.5), kind=kOutput, calls=%fused_computation.28 | convolution fusion | flops 8594128896 | bytes 18874368 | tf_op jit(solution)/shard_map/dot_general | solution.py:125
  67.2 22.9 %collective-permute-done = bf16[256,4096]{1,0:T(8,128)(2,1)} collective-permute-done((bf16[256,4096]{1,0:T(8,128)(2,1)}, bf16[256,4096]{1,0:T(8,128)(2,1)}, u32[]{:S(2)}, u32[]{:S(2)}) %collective-permute-start) | collective-permute-done | bytes 2097184 | tf_op jit(solution)/shard_map/ppermute | solution.py:106
  90.4 2.8 fusion.51
  95.2 6.9 %collective-permute-start.2 = (bf16[256,4096]{1,0:T(8,128)(2,1)S(1)}, bf16[256,4096]{1,0:T(8,128)(2,1)}, u32[]{:S(2)}, u32[]{:S(2)}) collective-permute-start(bf16[256,4096]{1,0:T(8,128)(2,1)S(1)} %get-tuple-element.47), channel_id=1, source_target_pairs={{0,4},{4,8},{1,5},{5,9},{2,6},{6,10},{3,7},{7,11},{16,20},{20,24},... | collective-permute-start | bytes 6291464 | tf_op jit(solution)/shard_map/ppermute | solution.py:106
  102.1 14.8 %fusion.29 = bf16[1024,4096]{1,0:T(8,128)(2,1)} fusion(bf16[1024,1024]{1,0:T(8,128)(2,1)} %all-gather.8.cloned.1.call-done, bf16[1,4096,1024]{2,1,0:T(8,128)(2,1)} %param.6), kind=kOutput, calls=%fused_computation.29 | convolution fusion | flops 8594128896 | bytes 18874368 | tf_op jit(solution)/shard_map/dot_general | solution.py:127
  117.3 27.7 %collective-permute-done.2 = bf16[256,4096]{1,0:T(8,128)(2,1)} collective-permute-done((bf16[256,4096]{1,0:T(8,128)(2,1)S(1)}, bf16[256,4096]{1,0:T(8,128)(2,1)}, u32[]{:S(2)}, u32[]{:S(2)}) %collective-permute-start.2) | collective-permute-done | bytes 2097184 | tf_op jit(solution)/shard_map/ppermute | solution.py:106
  145.2 3.5 fusion.50
  148.7 7.9 %collective-permute-start.4 = (bf16[256,4096]{1,0:T(8,128)(2,1)}, bf16[256,4096]{1,0:T(8,128)(2,1)S(1)}, u32[]{:S(2)}, u32[]{:S(2)}) collective-permute-start(bf16[256,4096]{1,0:T(8,128)(2,1)} %get-tuple-element.44), channel_id=1, source_target_pairs={{0,4},{4,8},{8,12},{1,5},{5,9},{9,13},{2,6},{6,10},{10,14},{3,7},{... | collective-permute-start | bytes 6291464 | tf_op jit(solution)/shard_map/ppermute | solution.py:106
  157.9 42.4 %collective-permute-done.4 = bf16[256,4096]{1,0:T(8,128)(2,1)S(1)} collective-permute-done((bf16[256,4096]{1,0:T(8,128)(2,1)}, bf16[256,4096]{1,0:T(8,128)(2,1)S(1)}, u32[]{:S(2)}, u32[]{:S(2)}) %collective-permute-start.4) | collective-permute-done | bytes 2097184 | tf_op jit(solution)/shard_map/ppermute | solution.py:106
  200.3 4.2 collective-permute-done.5
  204.5 6.1 %fusion.40 = (f32[256,4096]{1,0:T(8,128)}, bf16[256,4096]{1,0:T(8,128)(2,1)}) fusion(bf16[256,4096]{1,0:T(8,128)(2,1)} %collective-permute-done.5, pred[]{:T(512)S(6)} %and.26, bf16[4,256,4096]{2,1,0:T(8,128)(2,1)} %bitcast.89, s32[]{:T(128)S(6)} %select_n.303, bf16[256,4096]{1,0:T(8,128)(2,1)S(1)} %collective-permute-done.4, pred[]{:T(512)S(6)} %and.20), kind=kLoop, calls=%fused_computation.36 | loop fusion | flops 18874368 | bytes 12582918 | tf_op jit(solution)/shard_map/add | solution.py:19
  210.7 2.3 collective-permute-start.6
  214.3 40.9 %collective-permute-done.6 = bf16[256,4096]{1,0:T(8,128)(2,1)S(1)} collective-permute-done((bf16[256,4096]{1,0:T(8,128)(2,1)}, bf16[256,4096]{1,0:T(8,128)(2,1)S(1)}, u32[]{:S(2)}, u32[]{:S(2)}) %collective-permute-start.6) | collective-permute-done | bytes 2097184 | tf_op jit(solution)/shard_map/ppermute | solution.py:106
  255.2 4.2 collective-permute-done.8
  259.5 5.4 bitcast_select_fusion
  266.1 5.9 collective-permute-start.7
  272.0 38.3 %collective-permute-done.9 = bf16[256,4096]{1,0:T(8,128)(2,1)S(1)} collective-permute-done((bf16[256,4096]{1,0:T(8,128)(2,1)}, bf16[256,4096]{1,0:T(8,128)(2,1)S(1)}, u32[]{:S(2)}, u32[]{:S(2)}) %collective-permute-start.9) | collective-permute-done | bytes 2097184 | tf_op jit(solution)/shard_map/ppermute | solution.py:106
  311.9 3.9 fusion.54
  315.9 6.1 %collective-permute-start.10 = (bf16[256,4096]{1,0:T(8,128)(2,1)S(1)}, bf16[256,4096]{1,0:T(8,128)(2,1)S(1)}, u32[]{:S(2)}, u32[]{:S(2)}) collective-permute-start(bf16[256,4096]{1,0:T(8,128)(2,1)S(1)} %get-tuple-element.41), channel_id=1, source_target_pairs={{8,12},{0,4},{4,8},{9,13},{1,5},{5,9},{10,14},{2,6},{6,10},{11,15}... | collective-permute-start | bytes 6291464 | tf_op jit(solution)/shard_map/ppermute | solution.py:106
  322.0 12.5 %collective-permute-start.12 = (bf16[256,4096]{1,0:T(8,128)(2,1)S(1)}, bf16[256,4096]{1,0:T(8,128)(2,1)S(1)}, u32[]{:S(2)}, u32[]{:S(2)}) collective-permute-start(bf16[256,4096]{1,0:T(8,128)(2,1)S(1)} %get-tuple-element.40), channel_id=1, source_target_pairs={{4,0},{8,4},{12,8},{5,1},{9,5},{13,9},{6,2},{10,6},{14,10},{7,3},{... | collective-permute-start | bytes 6291464 | tf_op jit(solution)/shard_map/ppermute | solution.py:106
  334.4 27.1 %collective-permute-done.10 = bf16[256,4096]{1,0:T(8,128)(2,1)S(1)} collective-permute-done((bf16[256,4096]{1,0:T(8,128)(2,1)S(1)}, bf16[256,4096]{1,0:T(8,128)(2,1)S(1)}, u32[]{:S(2)}, u32[]{:S(2)}) %collective-permute-start.10) | collective-permute-done | bytes 2097184 | tf_op jit(solution)/shard_map/ppermute | solution.py:106
  361.5 4.2 collective-permute-done.12
  365.8 3.1 fusion.44
  370.2 6.1 %collective-permute-start.11 = (bf16[256,4096]{1,0:T(8,128)(2,1)S(1)}, bf16[256,4096]{1,0:T(8,128)(2,1)}, u32[]{:S(2)}, u32[]{:S(2)}) collective-permute-start(bf16[256,4096]{1,0:T(8,128)(2,1)S(1)} %get-tuple-element.39), channel_id=1, source_target_pairs={{0,4},{4,8},{8,12},{1,5},{5,9},{9,13},{2,6},{6,10},{10,14},{3,7},{... | collective-permute-start | bytes 6291464 | tf_op jit(solution)/shard_map/ppermute | solution.py:106
  380.1 14.8 %fusion.8 = f32[1024,1024]{1,0:T(8,128)} fusion(bf16[1,4096,1024]{2,1,0:T(8,128)(2,1)} %param.6, bf16[256,4096]{1,0:T(8,128)(2,1)S(1)} %select_add_fusion, bf16[256,4096]{1,0:T(8,128)(2,1)S(1)} %get-tuple-element.48, bf16[256,4096]{1,0:T(8,128)(2,1)S(1)} %select_add_fusion.1, bf16[256,4096]{1,0:T(8,128)(2,1)} %get-tuple-element.37), kind=kOutput, calls=%fused_computation.9 | convolution fusion | flops 8623489024 | bytes 20971520 | tf_op jit(solution)/shard_map/dot_general | solution.py:173
  394.9 17.1 %collective-permute-done.13 = bf16[256,4096]{1,0:T(8,128)(2,1)} collective-permute-done((bf16[256,4096]{1,0:T(8,128)(2,1)}, bf16[256,4096]{1,0:T(8,128)(2,1)}, u32[]{:S(2)}, u32[]{:S(2)}) %collective-permute-start.13) | collective-permute-done | bytes 2097184 | tf_op jit(solution)/shard_map/ppermute | solution.py:106
  412.0 3.9 select_convert_fusion
  415.9 2.3 select_convert_fusion.1
  418.3 8.4 %fusion.43 = bf16[256,4096]{1,0:T(8,128)(2,1)} fusion(f32[256,4096]{1,0:T(8,128)} %get-tuple-element.30, f32[256,4096]{1,0:T(8,128)} %select_convert_fusion, f32[256,4096]{1,0:T(8,128)} %select_convert_fusion.1, bf16[4,256,4096]{2,1,0:T(8,128)(2,1)} %bitcast.84, s32[]{:T(128)S(6)} %select_n.303), kind=kLoop, calls=%fused_computation.44 | loop fusion | flops 5242880 | bytes 16777220 | tf_op jit(solution)/shard_map/convert_element_type | solution.py:184
  428.0 4.9 collective-permute-start.14
  432.8 7.7 %fusion.20 = f32[256,1024]{1,0:T(8,128)} fusion(bf16[256,4096]{1,0:T(8,128)(2,1)} %fusion.43, bf16[1,1024,4096]{2,1,0:T(8,128)(2,1)} %param.5), kind=kOutput, calls=%fused_computation.21 | convolution fusion | flops 2147483648 | bytes 11534336 | tf_op jit(solution)/shard_map/dot_general | solution.py:210
  440.6 28.9 %collective-permute-done.16 = bf16[256,4096]{1,0:T(8,128)(2,1)} collective-permute-done((bf16[256,4096]{1,0:T(8,128)(2,1)}, bf16[256,4096]{1,0:T(8,128)(2,1)}, u32[]{:S(2)}, u32[]{:S(2)}) %collective-permute-start.16) | collective-permute-done | bytes 2097184 | tf_op jit(solution)/shard_map/ppermute | solution.py:106
  469.5 3.2 broadcast_select_fusion.1
  477.9 7.7 %fusion.16 = f32[256,1024]{1,0:T(8,128)} fusion(bf16[256,4096]{1,0:T(8,128)(2,1)} %broadcast_select_fusion.1, bf16[1,1024,4096]{2,1,0:T(8,128)(2,1)} %param.5), kind=kOutput, calls=%fused_computation.17 | convolution fusion | flops 2147483648 | bytes 11534336 | tf_op jit(solution)/shard_map/dot_general | solution.py:210
  485.9 14.0 %convolution_convert_fusion = bf16[4096,1024]{1,0:T(8,128)(2,1)} fusion(s32[]{:T(128)S(6)} %select_n.327, bf16[1024,1024]{1,0:T(8,128)(2,1)} %all-gather.8.cloned.1.call-done, bf16[256,4096]{1,0:T(8,128)(2,1)} %copy-done.11, bf16[256,4096]{1,0:T(8,128)(2,1)S(1)} %copy-done.7, bf16[256,4096]{1,0:T(8,128)(2,1)} %copy-done.10, ...), kind=kOutput, calls=%fused_computation.30 | convolution fusion | flops 8631877632 | bytes 18874372 | tf_op jit(solution)/shard_map/dot_general | solution.py:174
  499.9 7.5 %fusion.18 = f32[256,1024]{1,0:T(8,128)} fusion(bf16[256,4096]{1,0:T(8,128)(2,1)} %broadcast_select_fusion.6, bf16[1,1024,4096]{2,1,0:T(8,128)(2,1)} %param.5), kind=kOutput, calls=%fused_computation.19 | convolution fusion | flops 2147483648 | bytes 11534336 | tf_op jit(solution)/shard_map/dot_general | solution.py:210
  507.4 6.7 %collective-permute-done.17 = bf16[256,4096]{1,0:T(8,128)(2,1)} collective-permute-done((bf16[256,4096]{1,0:T(8,128)(2,1)}, bf16[256,4096]{1,0:T(8,128)(2,1)}, u32[]{:S(2)}, u32[]{:S(2)}) %collective-permute-start.17) | collective-permute-done | bytes 2097184 | tf_op jit(solution)/shard_map/ppermute | solution.py:106
  520.7 2.4 add.237
  524.4 7.1 %fusion.14 = f32[256,1024]{1,0:T(8,128)} fusion(bf16[256,4096]{1,0:T(8,128)(2,1)S(1)} %add.237, bf16[1,1024,4096]{2,1,0:T(8,128)(2,1)} %param.5), kind=kOutput, calls=%fused_computation.15 | convolution fusion | flops 2147483648 | bytes 11534336 | tf_op jit(solution)/shard_map/dot_general | solution.py:210
  533.0 2.5 fusion.65
  535.5 24.2 %collective-permute-done.19 = bf16[256,4096]{1,0:T(8,128)(2,1)} collective-permute-done((bf16[256,4096]{1,0:T(8,128)(2,1)S(1)}, bf16[256,4096]{1,0:T(8,128)(2,1)}, u32[]{:S(2)}, u32[]{:S(2)}) %collective-permute-start.19) | collective-permute-done | bytes 2097184 | tf_op jit(solution)/shard_map/ppermute | solution.py:106
  559.8 7.5 %fusion.12 = f32[256,1024]{1,0:T(8,128)} fusion(bf16[1,1024,4096]{2,1,0:T(8,128)(2,1)} %param.5, bf16[256,4096]{1,0:T(8,128)(2,1)} %collective-permute-done.19, pred[]{:T(512)S(6)} %and.24, bf16[256,4096]{1,0:T(8,128)(2,1)} %collective-permute-done.18, pred[]{:T(512)S(6)} %and.27), kind=kOutput, calls=%fused_computation.13 | convolution fusion | flops 2150629376 | bytes 13631490 | tf_op jit(solution)/shard_map/dot_general | solution.py:210
  571.8 14.1 %convert_bitcast_fusion = bf16[1,1024,4096]{2,1,0:T(8,128)(2,1)} fusion(bf16[256,4096]{1,0:T(8,128)(2,1)S(1)} %fusion.61, bf16[256,4096]{1,0:T(8,128)(2,1)S(1)} %copy-done.9, bf16[256,4096]{1,0:T(8,128)(2,1)S(1)} %fusion.62, bf16[256,4096]{1,0:T(8,128)(2,1)} %fusion.43, s32[]{:T(128)S(6)} %select_n.327, bf16[1024,1024]{1,0:T(8,128)(2,1)} %all-gather.6.cloned.1.call-done), kind=kOutput, calls=%fused_computation.27 | convolution fusion | flops 8631877632 | bytes 18874372 | tf_op jit(solution)/shard_map/dot_general | solution.py:196
  586.0 13.9 %reduce-scatter.17.cloned.1.call-done = f32[256,256]{1,0:T(8,128)} async-done(((f32[256,1024]{1,0:T(8,128)}), f32[256,256]{1,0:T(8,128)}) %reduce-scatter.17.cloned.1.call-update) | async-done | bytes 262160 | tf_op jit(solution)/shard_map/reduce_scatter | solution.py:213
  (101 shorter events, 42.7 us)
Async XLA Ops:
  7.2 22.5 %all-gather.4.cloned.1.call-start = ((), (), s32[]{:S(2)}) async-start(), calls=%async_computation.6 | async-start | bytes 1310720 | tf_op jit(solution)/shard_map/all_gather | solution.py:144
  9.0 45.2 %all-gather.6.cloned.1.call-start = ((), (), s32[]{:S(2)}) async-start(), calls=%async_computation.7 | async-start | bytes 2621440 | tf_op jit(solution)/shard_map/all_gather | solution.py:124
  9.7 92.4 %all-gather.8.cloned.1.call-start = ((), (), s32[]{:S(2)}) async-start(), calls=%async_computation.8 | async-start | bytes 2621440 | tf_op jit(solution)/shard_map/all_gather | solution.py:126
  40.2 26.7 %collective-permute-start.1 = (bf16[256,4096]{1,0:T(8,128)(2,1)}, bf16[256,4096]{1,0:T(8,128)(2,1)S(1)}, u32[]{:S(2)}, u32[]{:S(2)}) collective-permute-start(bf16[256,4096]{1,0:T(8,128)(2,1)} %get-tuple-element.49), channel_id=1, source_target_pairs={{12,8},{13,9},{14,10},{15,11},{28,24},{29,25},{30,26},{31,27}} | collective-permute-start | bytes 6291464 | tf_op jit(solution)/shard_map/ppermute | solution.py:106
  41.1 476.3 %reduce-scatter.7.cloned.1.call-start = ((), (), s32[]{:S(2)}) async-start(), calls=%async_computation.9 | async-start | bytes 5242880 | tf_op jit(solution)/shard_map/reduce_scatter | solution.py:182
  41.1 49.0 %collective-permute-start = (bf16[256,4096]{1,0:T(8,128)(2,1)}, bf16[256,4096]{1,0:T(8,128)(2,1)}, u32[]{:S(2)}, u32[]{:S(2)}) collective-permute-start(bf16[256,4096]{1,0:T(8,128)(2,1)} %get-tuple-element.50), channel_id=1, source_target_pairs={{0,4},{1,5},{2,6},{3,7},{16,20},{17,21},{18,22},{19,23}} | collective-permute-start | bytes 6291464 | tf_op jit(solution)/shard_map/ppermute | solution.py:106
  66.9 23.5 %copy-start = (bf16[1024,4096]{1,0:T(8,128)(2,1)}, bf16[1024,4096]{1,0:T(8,128)(2,1)S(1)}, u32[]{:S(2)}) copy-start(bf16[1024,4096]{1,0:T(8,128)(2,1)S(1)} %fusion.26) | copy-start | bytes 25165828
  93.2 23.8 %collective-permute-start.3 = (bf16[256,4096]{1,0:T(8,128)(2,1)}, bf16[256,4096]{1,0:T(8,128)(2,1)}, u32[]{:S(2)}, u32[]{:S(2)}) collective-permute-start(bf16[256,4096]{1,0:T(8,128)(2,1)} %get-tuple-element.46), channel_id=1, source_target_pairs={{8,4},{12,8},{9,5},{13,9},{10,6},{14,10},{11,7},{15,11},{24,20},{2... | collective-permute-start | bytes 6291464 | tf_op jit(solution)/shard_map/ppermute | solution.py:106
  95.2 49.7 %collective-permute-start.2 = (bf16[256,4096]{1,0:T(8,128)(2,1)S(1)}, bf16[256,4096]{1,0:T(8,128)(2,1)}, u32[]{:S(2)}, u32[]{:S(2)}) collective-permute-start(bf16[256,4096]{1,0:T(8,128)(2,1)S(1)} %get-tuple-element.47), channel_id=1, source_target_pairs={{0,4},{4,8},{1,5},{5,9},{2,6},{6,10},{3,7},{7,11},{16,20},{20,24},... | collective-permute-start | bytes 6291464 | tf_op jit(solution)/shard_map/ppermute | solution.py:106
  117.0 28.3 %copy-start.1 = (bf16[1024,4096]{1,0:T(8,128)(2,1)S(1)}, bf16[1024,4096]{1,0:T(8,128)(2,1)}, u32[]{:S(2)}) copy-start(bf16[1024,4096]{1,0:T(8,128)(2,1)} %copy-done) | copy-start | bytes 25165828
  148.7 51.6 %collective-permute-start.4 = (bf16[256,4096]{1,0:T(8,128)(2,1)}, bf16[256,4096]{1,0:T(8,128)(2,1)S(1)}, u32[]{:S(2)}, u32[]{:S(2)}) collective-permute-start(bf16[256,4096]{1,0:T(8,128)(2,1)} %get-tuple-element.44), channel_id=1, source_target_pairs={{0,4},{4,8},{8,12},{1,5},{5,9},{9,13},{2,6},{6,10},{10,14},{3,7},{... | collective-permute-start | bytes 6291464 | tf_op jit(solution)/shard_map/ppermute | solution.py:106
  156.6 48.0 %collective-permute-start.5 = (bf16[256,4096]{1,0:T(8,128)(2,1)}, bf16[256,4096]{1,0:T(8,128)(2,1)}, u32[]{:S(2)}, u32[]{:S(2)}) collective-permute-start(bf16[256,4096]{1,0:T(8,128)(2,1)} %get-tuple-element.45), channel_id=1, source_target_pairs={{4,0},{8,4},{12,8},{5,1},{9,5},{13,9},{6,2},{10,6},{14,10},{7,3},{... | collective-permute-start | bytes 6291464 | tf_op jit(solution)/shard_map/ppermute | solution.py:106
  210.7 44.6 %collective-permute-start.6 = (bf16[256,4096]{1,0:T(8,128)(2,1)}, bf16[256,4096]{1,0:T(8,128)(2,1)S(1)}, u32[]{:S(2)}, u32[]{:S(2)}) collective-permute-start(bf16[256,4096]{1,0:T(8,128)(2,1)} %get-tuple-element.37), channel_id=1, source_target_pairs={{0,4},{4,8},{8,12},{1,5},{5,9},{9,13},{2,6},{6,10},{10,14},{3,7},{... | collective-permute-start | bytes 6291464 | tf_op jit(solution)/shard_map/ppermute | solution.py:106
  213.0 46.5 %collective-permute-start.8 = (bf16[256,4096]{1,0:T(8,128)(2,1)}, bf16[256,4096]{1,0:T(8,128)(2,1)}, u32[]{:S(2)}, u32[]{:S(2)}) collective-permute-start(bf16[256,4096]{1,0:T(8,128)(2,1)} %get-tuple-element.37), channel_id=1, source_target_pairs={{4,0},{8,4},{12,8},{5,1},{9,5},{13,9},{6,2},{10,6},{14,10},{7,3},{... | collective-permute-start | bytes 6291464 | tf_op jit(solution)/shard_map/ppermute | solution.py:106
  255.2 9.6 %copy-start.4 = (bf16[256,4096]{1,0:T(8,128)(2,1)}, bf16[256,4096]{1,0:T(8,128)(2,1)S(1)}, u32[]{:S(2)}) copy-start(bf16[256,4096]{1,0:T(8,128)(2,1)S(1)} %collective-permute-done.6) | copy-start | bytes 6291460
  264.9 45.5 %collective-permute-start.9 = (bf16[256,4096]{1,0:T(8,128)(2,1)}, bf16[256,4096]{1,0:T(8,128)(2,1)S(1)}, u32[]{:S(2)}, u32[]{:S(2)}) collective-permute-start(bf16[256,4096]{1,0:T(8,128)(2,1)} %get-tuple-element.42), channel_id=1, source_target_pairs={{4,0},{8,4},{12,8},{5,1},{9,5},{13,9},{6,2},{10,6},{14,10},{7,3},{... | collective-permute-start | bytes 6291464 | tf_op jit(solution)/shard_map/ppermute | solution.py:106
  266.1 45.5 %collective-permute-start.7 = (bf16[256,4096]{1,0:T(8,128)(2,1)}, bf16[256,4096]{1,0:T(8,128)(2,1)}, u32[]{:S(2)}, u32[]{:S(2)}) collective-permute-start(bf16[256,4096]{1,0:T(8,128)(2,1)} %get-tuple-element.43), channel_id=1, source_target_pairs={{4,8},{8,12},{0,4},{5,9},{9,13},{1,5},{6,10},{10,14},{2,6},{7,11},... | collective-permute-start | bytes 6291464 | tf_op jit(solution)/shard_map/ppermute | solution.py:106
  311.9 53.9 %slice-start = ((s8[8388608]{0:T(1024)(128)(4,1)}), s8[4194304]{0:T(1024)(128)(4,1)S(1)}, s32[]{:S(2)}) async-start(s8[8388608]{0:T(1024)(128)(4,1)} %bitcast.85), calls=%async_computation.15 | async-start | bytes 8388608
  311.9 53.9 %slice-start.1 = ((s8[8388608]{0:T(1024)(128)(4,1)}), s8[4194304]{0:T(1024)(128)(4,1)S(1)}, s32[]{:S(2)}) async-start(s8[8388608]{0:T(1024)(128)(4,1)} %bitcast.85), calls=%async_computation.16 | async-start | bytes 8388608
  315.9 62.5 %copy-start.6 = (bf16[256,4096]{1,0:T(8,128)(2,1)}, bf16[256,4096]{1,0:T(8,128)(2,1)S(1)}, u32[]{:S(2)}) copy-start(bf16[256,4096]{1,0:T(8,128)(2,1)S(1)} %get-tuple-element.48) | copy-start | bytes 6291460
  315.9 45.6 %collective-permute-start.10 = (bf16[256,4096]{1,0:T(8,128)(2,1)S(1)}, bf16[256,4096]{1,0:T(8,128)(2,1)S(1)}, u32[]{:S(2)}, u32[]{:S(2)}) collective-permute-start(bf16[256,4096]{1,0:T(8,128)(2,1)S(1)} %get-tuple-element.41), channel_id=1, source_target_pairs={{8,12},{0,4},{4,8},{9,13},{1,5},{5,9},{10,14},{2,6},{6,10},{11,15}... | collective-permute-start | bytes 6291464 | tf_op jit(solution)/shard_map/ppermute | solution.py:106
  322.0 43.8 %collective-permute-start.12 = (bf16[256,4096]{1,0:T(8,128)(2,1)S(1)}, bf16[256,4096]{1,0:T(8,128)(2,1)S(1)}, u32[]{:S(2)}, u32[]{:S(2)}) collective-permute-start(bf16[256,4096]{1,0:T(8,128)(2,1)S(1)} %get-tuple-element.40), channel_id=1, source_target_pairs={{4,0},{8,4},{12,8},{5,1},{9,5},{13,9},{6,2},{10,6},{14,10},{7,3},{... | collective-permute-start | bytes 6291464 | tf_op jit(solution)/shard_map/ppermute | solution.py:106
  368.9 43.2 %collective-permute-start.13 = (bf16[256,4096]{1,0:T(8,128)(2,1)}, bf16[256,4096]{1,0:T(8,128)(2,1)}, u32[]{:S(2)}, u32[]{:S(2)}) collective-permute-start(bf16[256,4096]{1,0:T(8,128)(2,1)} %get-tuple-element.38), channel_id=1, source_target_pairs={{4,0},{8,4},{12,8},{5,1},{9,5},{13,9},{6,2},{10,6},{14,10},{7,3},{... | collective-permute-start | bytes 6291464 | tf_op jit(solution)/shard_map/ppermute | solution.py:106
  370.1 8.0 %copy-start.5 = (bf16[256,4096]{1,0:T(8,128)(2,1)S(1)}, bf16[256,4096]{1,0:T(8,128)(2,1)}, u32[]{:S(2)}) copy-start(bf16[256,4096]{1,0:T(8,128)(2,1)} %copy-done.4) | copy-start | bytes 6291460
  370.2 45.7 %collective-permute-start.11 = (bf16[256,4096]{1,0:T(8,128)(2,1)S(1)}, bf16[256,4096]{1,0:T(8,128)(2,1)}, u32[]{:S(2)}, u32[]{:S(2)}) collective-permute-start(bf16[256,4096]{1,0:T(8,128)(2,1)S(1)} %get-tuple-element.39), channel_id=1, source_target_pairs={{0,4},{4,8},{8,12},{1,5},{5,9},{9,13},{2,6},{6,10},{10,14},{3,7},{... | collective-permute-start | bytes 6291464 | tf_op jit(solution)/shard_map/ppermute | solution.py:106
  378.1 1.3 copy-start.10
  378.4 1.7 copy-start.11
  418.2 167.6 %reduce-scatter.9.cloned.1.call-start = ((), (), s32[]{:S(2)}) async-start(), calls=%async_computation.10 | async-start | bytes 1310720 | tf_op jit(solution)/shard_map/reduce_scatter | solution.py:213
  426.7 42.9 %collective-permute-start.16 = (bf16[256,4096]{1,0:T(8,128)(2,1)}, bf16[256,4096]{1,0:T(8,128)(2,1)}, u32[]{:S(2)}, u32[]{:S(2)}) collective-permute-start(bf16[256,4096]{1,0:T(8,128)(2,1)} %fusion.43), channel_id=1, source_target_pairs={{4,0},{8,4},{12,8},{5,1},{9,5},{13,9},{6,2},{10,6},{14,10},{7,3},{... | collective-permute-start | bytes 6291464 | tf_op jit(solution)/shard_map/ppermute | solution.py:106
  428.0 46.0 %collective-permute-start.14 = (bf16[256,4096]{1,0:T(8,128)(2,1)}, bf16[256,4096]{1,0:T(8,128)(2,1)S(1)}, u32[]{:S(2)}, u32[]{:S(2)}) collective-permute-start(bf16[256,4096]{1,0:T(8,128)(2,1)} %fusion.43), channel_id=1, source_target_pairs={{0,4},{4,8},{8,12},{1,5},{5,9},{9,13},{2,6},{6,10},{10,14},{3,7},{... | collective-permute-start | bytes 6291464 | tf_op jit(solution)/shard_map/ppermute | solution.py:106
  440.6 145.3 %reduce-scatter.13.cloned.1.call-start = ((), (), s32[]{:S(2)}) async-start(), calls=%async_computation.12 | async-start | bytes 1310720 | tf_op jit(solution)/shard_map/reduce_scatter | solution.py:213
  472.7 41.4 %collective-permute-start.17 = (bf16[256,4096]{1,0:T(8,128)(2,1)}, bf16[256,4096]{1,0:T(8,128)(2,1)}, u32[]{:S(2)}, u32[]{:S(2)}) collective-permute-start(bf16[256,4096]{1,0:T(8,128)(2,1)} %broadcast_select_fusion.1), channel_id=1, source_target_pairs={{4,0},{8,4},{5,1},{9,5},{6,2},{10,6},{7,3},{11,7},{20,16},{24,20},... | collective-permute-start | bytes 6291464 | tf_op jit(solution)/shard_map/ppermute | solution.py:106
  474.0 2.0 copy-start.2
  476.0 39.9 %collective-permute-start.15 = (bf16[256,4096]{1,0:T(8,128)(2,1)}, bf16[256,4096]{1,0:T(8,128)(2,1)}, u32[]{:S(2)}, u32[]{:S(2)}) collective-permute-start(bf16[256,4096]{1,0:T(8,128)(2,1)} %broadcast_select_fusion.6), channel_id=1, source_target_pairs={{4,8},{8,12},{5,9},{9,13},{6,10},{10,14},{7,11},{11,15},{20,24},{2... | collective-permute-start | bytes 6291464 | tf_op jit(solution)/shard_map/ppermute | solution.py:106
  477.9 8.0 %copy-start.7 = (bf16[256,4096]{1,0:T(8,128)(2,1)S(1)}, bf16[256,4096]{1,0:T(8,128)(2,1)}, u32[]{:S(2)}) copy-start(bf16[256,4096]{1,0:T(8,128)(2,1)} %copy-done.6) | copy-start | bytes 6291460
  485.6 100.3 %reduce-scatter.11.cloned.1.call-start = ((), (), s32[]{:S(2)}) async-start(), calls=%async_computation.11 | async-start | bytes 1310720 | tf_op jit(solution)/shard_map/reduce_scatter | solution.py:213
  507.4 78.6 %reduce-scatter.15.cloned.1.call-start = ((), (), s32[]{:S(2)}) async-start(), calls=%async_computation.13 | async-start | bytes 1310720 | tf_op jit(solution)/shard_map/reduce_scatter | solution.py:213
  517.4 18.1 %collective-permute-start.18 = (bf16[256,4096]{1,0:T(8,128)(2,1)}, bf16[256,4096]{1,0:T(8,128)(2,1)}, u32[]{:S(2)}, u32[]{:S(2)}) collective-permute-start(bf16[256,4096]{1,0:T(8,128)(2,1)} %broadcast_select_fusion.8), channel_id=1, source_target_pairs={{8,12},{9,13},{10,14},{11,15},{24,28},{25,29},{26,30},{27,31}} | collective-permute-start | bytes 6291464 | tf_op jit(solution)/shard_map/ppermute | solution.py:106
  519.4 40.4 %collective-permute-start.19 = (bf16[256,4096]{1,0:T(8,128)(2,1)S(1)}, bf16[256,4096]{1,0:T(8,128)(2,1)}, u32[]{:S(2)}, u32[]{:S(2)}) collective-permute-start(bf16[256,4096]{1,0:T(8,128)(2,1)S(1)} %broadcast_select_fusion.4), channel_id=1, source_target_pairs={{4,0},{5,1},{6,2},{7,3},{20,16},{21,17},{22,18},{23,19}} | collective-permute-start | bytes 6291464 | tf_op jit(solution)/shard_map/ppermute | solution.py:106
  523.1 1.3 copy-start.8
  531.5 68.3 %reduce-scatter.17.cloned.1.call-start = ((), (), s32[]{:S(2)}) async-start(), calls=%async_computation.14 | async-start | bytes 1310720 | tf_op jit(solution)/shard_map/reduce_scatter | solution.py:213
  567.3 2.3 copy-start.3
  569.5 2.2 copy-start.9
  585.9 15.5 %copy-start.12 = (f32[256,256]{1,0:T(8,128)S(1)}, f32[256,256]{1,0:T(8,128)}, u32[]{:S(2)}) copy-start(f32[256,256]{1,0:T(8,128)} %reduce-scatter.9.cloned.1.call-done) | copy-start | bytes 786436
  585.9 15.5 %copy-start.13 = (f32[256,256]{1,0:T(8,128)S(1)}, f32[256,256]{1,0:T(8,128)}, u32[]{:S(2)}) copy-start(f32[256,256]{1,0:T(8,128)} %reduce-scatter.13.cloned.1.call-done) | copy-start | bytes 786436
  585.9 15.4 %copy-start.14 = (f32[256,256]{1,0:T(8,128)S(1)}, f32[256,256]{1,0:T(8,128)}, u32[]{:S(2)}) copy-start(f32[256,256]{1,0:T(8,128)} %reduce-scatter.11.cloned.1.call-done) | copy-start | bytes 786436
  585.9 15.4 %copy-start.15 = (f32[256,256]{1,0:T(8,128)S(1)}, f32[256,256]{1,0:T(8,128)}, u32[]{:S(2)}) copy-start(f32[256,256]{1,0:T(8,128)} %reduce-scatter.15.cloned.1.call-done) | copy-start | bytes 786436
  599.8 1.5 copy-start.16
Sparse Core Ops, SparseCore 0:
  10.1 19.5 all-gather.3
  31.3 22.8 all-gather.5
  55.7 22.8 all-gather.7
  418.4 43.9 reduce-scatter.6
  464.9 24.8 reduce-scatter.8
  492.2 24.8 reduce-scatter.12
  519.8 24.9 reduce-scatter.10
  547.3 24.8 reduce-scatter.14
  574.9 24.8 reduce-scatter.16

commit v7 on v6

--- a/solution.py
+++ b/solution.py
@@ -134,14 +134,13 @@
         last = count - 1
         pos = lax.axis_index("r")
 
-        own_rows = jnp.concatenate(
+        first_rows = jnp.concatenate(
             [
-                lax.dynamic_slice_in_dim(hidden_in, jnp.clip(last + pos, 0, last) * rows, rows, axis=0),
-                lax.dynamic_slice_in_dim(hidden_in, jnp.clip(pos - last, 0, last) * rows, rows, axis=0),
+                lax.dynamic_slice_in_dim(x_rows, jnp.clip(last + pos, 0, last) * rows, rows, axis=0),
+                lax.dynamic_slice_in_dim(x_rows, jnp.clip(pos - last, 0, last) * rows, rows, axis=0),
             ],
             axis=0,
         )
-        first_rows = lax.all_gather(own_rows, "p", axis=1, tiled=True)
         first = jnp.dot(first_rows, up_tile, preferred_element_type=jnp.float32).astype(jnp.bfloat16)
         up_sum.first = (first[:rows], first[rows:])
         run_slot([(up_sum, 0)])

time: 617 us -> 623 us (level)
  waiting for transfers between devices: 333 us -> 352 us
  starting transfers between devices: 73.8 us -> 60.3 us
    ppermute x20, waiting for transfers between devices: 290 us -> 311 us  [run_slot(): received.append(lax.ppermute(combined, 'r', pairs))]
    all_gather x1 -> x0, waiting for transfers between devices: 19.9 us -> none  [on_device(): first_rows = lax.all_gather(own_rows, 'p', axis=1, tiled=True)]
    all_gather x1, waiting for transfers between devices: 8.22 us -> 27.2 us  [on_device(): x_rows = lax.all_gather(hidden_in, 'p', axis=1, tiled=True)]
    ppermute x20, starting transfers between devices: 73 us -> 59.6 us  [run_slot(): received.append(lax.ppermute(combined, 'r', pairs))]
  transfers between devices with their start and end apart: 29 -> 28, of which waited for: 17 -> 16; matrix products, arithmetic and copies ran while one was open for 25% -> 23% of each run, Pallas kernels for 0% -> 0%
where the time goes in v7:
time: 623 us; the launch traced here: 616 us
  waiting for transfers between devices  352 us (57%)
  matrix products  117 us (19%)
  other arithmetic  63.8 us (10%)
  starting transfers between devices  60.3 us (10%)
  between operations  15 us (2%)
  local copies, waits for them, and re-layouts  7.64 us (1%)
    ppermute x20, waiting for transfers between devices, run_slot(): received.append(lax.ppermute(combined, 'r', pairs))  311 us
    ppermute x20, starting transfers between devices, run_slot(): received.append(lax.ppermute(combined, 'r', pairs))  59.6 us
    dot_general x5, matrix products, on_device(): lax.dot_general(piece, up_tile, (((1,), (1,)), ((), ())), preferred_eleme...  37.6 us
    all_gather x1, waiting for transfers between devices, on_device(): x_rows = lax.all_gather(hidden_in, 'p', axis=1, tiled=True)  27.2 us
    dot_general x1, matrix products, on_device(): lax.dot_general(grad_rows, down_tile, (((1,), (1,)), ((), ())), preferred...  14.8 us
    dot_general x1, matrix products, on_device(): jnp.dot(activation, down_tile, preferred_element_type=jnp.float32)  14.8 us
    dot_general x1, matrix products, on_device(): lax.dot_general(rotate_rows(x_rows, turn), pre_grad, (((0,), (0,)), ((),...  14.1 us
    dot_general x1, matrix products, on_device(): lax.dot_general(activation, grad_turned, (((0,), (0,)), ((), ())), prefer...  14 us
  transfers between devices with their start and end apart: 28, of which 16 were waited for; matrix products, arithmetic and copies ran while one was open for 23% of the time, Pallas kernels for 0%

profile of v7, /device:TPU:0, one launch (start us, length us, event | category | flops | bytes accessed | tf_op | source)
XLA Modules:
  0.0 615.6 jit_solution(7127387396557680383)
XLA Ops:
  8.0 27.2 %all-gather.3.cloned.1.call-done = bf16[1024,1024]{1,0:T(8,128)(2,1)} async-done(((bf16[1024,256]{1,0:T(8,128)(2,1)}), bf16[1024,1024]{1,0:T(8,128)(2,1)}) %all-gather.3.cloned.1.call-update) | async-done | bytes 2097168 | tf_op jit(solution)/shard_map/all_gather | solution.py:124
  36.4 8.6 %fusion.34 = bf16[512,4096]{1,0:T(8,128)(2,1)S(1)} fusion(bf16[1,1024,4096]{2,1,0:T(8,128)(2,1)} %param.5, bf16[256,1024]{1,0:T(8,128)(2,1)S(1)} %get-tuple-element.56, bf16[256,1024]{1,0:T(8,128)(2,1)S(1)} %get-tuple-element.55), kind=kOutput, calls=%fused_computation.32 | convolution fusion | flops 4299161600 | bytes 13631488 | tf_op jit(solution)/shard_map/dot_general | solution.py:144
  45.0 2.5 fusion.97
  48.4 3.5 collective-permute-start
  51.9 12.8 %fusion.26 = bf16[1024,4096]{1,0:T(8,128)(2,1)S(1)} fusion(bf16[1024,1024]{1,0:T(8,128)(2,1)} %all-gather.3.cloned.1.call-done, bf16[1,1024,4096]{2,1,0:T(8,128)(2,1)} %param.5), kind=kOutput, calls=%fused_computation.28 | convolution fusion | flops 8594128896 | bytes 18874368 | tf_op jit(solution)/shard_map/dot_general | solution.py:125
  65.0 32.4 %collective-permute-done = bf16[256,4096]{1,0:T(8,128)(2,1)S(1)} collective-permute-done((bf16[256,4096]{1,0:T(8,128)(2,1)}, bf16[256,4096]{1,0:T(8,128)(2,1)S(1)}, u32[]{:S(2)}, u32[]{:S(2)}) %collective-permute-start) | collective-permute-done | bytes 2097184 | tf_op jit(solution)/shard_map/ppermute | solution.py:106
  97.7 2.8 fusion.51
  102.4 5.1 collective-permute-start.2
  107.6 14.8 %fusion.29 = bf16[1024,4096]{1,0:T(8,128)(2,1)} fusion(bf16[1024,1024]{1,0:T(8,128)(2,1)} %all-gather.5.cloned.1.call-done, bf16[1,4096,1024]{2,1,0:T(8,128)(2,1)} %param.6), kind=kOutput, calls=%fused_computation.29 | convolution fusion | flops 8594128896 | bytes 18874368 | tf_op jit(solution)/shard_map/dot_general | solution.py:127
  122.7 27.8 %collective-permute-done.2 = bf16[256,4096]{1,0:T(8,128)(2,1)} collective-permute-done((bf16[256,4096]{1,0:T(8,128)(2,1)S(1)}, bf16[256,4096]{1,0:T(8,128)(2,1)}, u32[]{:S(2)}, u32[]{:S(2)}) %collective-permute-start.2) | collective-permute-done | bytes 2097184 | tf_op jit(solution)/shard_map/ppermute | solution.py:106
  150.8 3.5 fusion.50
  154.3 7.9 %collective-permute-start.4 = (bf16[256,4096]{1,0:T(8,128)(2,1)}, bf16[256,4096]{1,0:T(8,128)(2,1)S(1)}, u32[]{:S(2)}, u32[]{:S(2)}) collective-permute-start(bf16[256,4096]{1,0:T(8,128)(2,1)} %get-tuple-element.44), channel_id=1, source_target_pairs={{0,4},{4,8},{8,12},{1,5},{5,9},{9,13},{2,6},{6,10},{10,14},{3,7},{... | collective-permute-start | bytes 6291464 | tf_op jit(solution)/shard_map/ppermute | solution.py:106
  163.4 42.4 %collective-permute-done.4 = bf16[256,4096]{1,0:T(8,128)(2,1)S(1)} collective-permute-done((bf16[256,4096]{1,0:T(8,128)(2,1)}, bf16[256,4096]{1,0:T(8,128)(2,1)S(1)}, u32[]{:S(2)}, u32[]{:S(2)}) %collective-permute-start.4) | collective-permute-done | bytes 2097184 | tf_op jit(solution)/shard_map/ppermute | solution.py:106
  205.9 4.2 collective-permute-done.5
  210.1 6.1 fusion.40
  216.2 2.8 collective-permute-start.6
  220.3 41.0 %collective-permute-done.6 = bf16[256,4096]{1,0:T(8,128)(2,1)S(1)} collective-permute-done((bf16[256,4096]{1,0:T(8,128)(2,1)}, bf16[256,4096]{1,0:T(8,128)(2,1)S(1)}, u32[]{:S(2)}, u32[]{:S(2)}) %collective-permute-start.6) | collective-permute-done | bytes 2097184 | tf_op jit(solution)/shard_map/ppermute | solution.py:106
  261.3 4.2 collective-permute-done.8
  265.6 5.4 bitcast_select_fusion
  272.2 5.9 collective-permute-start.7
  278.1 38.4 %collective-permute-done.9 = bf16[256,4096]{1,0:T(8,128)(2,1)S(1)} collective-permute-done((bf16[256,4096]{1,0:T(8,128)(2,1)}, bf16[256,4096]{1,0:T(8,128)(2,1)S(1)}, u32[]{:S(2)}, u32[]{:S(2)}) %collective-permute-start.9) | collective-permute-done | bytes 2097184 | tf_op jit(solution)/shard_map/ppermute | solution.py:106
  318.1 3.9 fusion.54
  322.0 6.1 collective-permute-start.10
  329.8 37.9 %collective-permute-done.10 = bf16[256,4096]{1,0:T(8,128)(2,1)S(1)} collective-permute-done((bf16[256,4096]{1,0:T(8,128)(2,1)S(1)}, bf16[256,4096]{1,0:T(8,128)(2,1)S(1)}, u32[]{:S(2)}, u32[]{:S(2)}) %collective-permute-start.10) | collective-permute-done | bytes 2097184 | tf_op jit(solution)/shard_map/ppermute | solution.py:106
  367.7 4.2 collective-permute-done.12
  372.0 3.1 fusion.44
  376.4 6.1 collective-permute-start.11
  386.4 14.8 %fusion.8 = f32[1024,1024]{1,0:T(8,128)} fusion(bf16[1,4096,1024]{2,1,0:T(8,128)(2,1)} %param.6, bf16[256,4096]{1,0:T(8,128)(2,1)S(1)} %select_add_fusion, bf16[256,4096]{1,0:T(8,128)(2,1)S(1)} %get-tuple-element.48, bf16[256,4096]{1,0:T(8,128)(2,1)S(1)} %select_add_fusion.1, bf16[256,4096]{1,0:T(8,128)(2,1)} %get-tuple-element.37), kind=kOutput, calls=%fused_computation.9 | convolution fusion | flops 8623489024 | bytes 20971520 | tf_op jit(solution)/shard_map/dot_general | solution.py:172
  401.2 17.1 %collective-permute-done.13 = bf16[256,4096]{1,0:T(8,128)(2,1)} collective-permute-done((bf16[256,4096]{1,0:T(8,128)(2,1)}, bf16[256,4096]{1,0:T(8,128)(2,1)}, u32[]{:S(2)}, u32[]{:S(2)}) %collective-permute-start.13) | collective-permute-done | bytes 2097184 | tf_op jit(solution)/shard_map/ppermute | solution.py:106
  418.3 3.9 select_convert_fusion
  422.2 2.3 select_convert_fusion.1
  424.6 8.5 %fusion.43 = bf16[256,4096]{1,0:T(8,128)(2,1)} fusion(f32[256,4096]{1,0:T(8,128)} %get-tuple-element.30, f32[256,4096]{1,0:T(8,128)} %select_convert_fusion, f32[256,4096]{1,0:T(8,128)} %select_convert_fusion.1, bf16[4,256,4096]{2,1,0:T(8,128)(2,1)} %bitcast.83, s32[]{:T(128)S(6)} %select_n.303), kind=kLoop, calls=%fused_computation.44 | loop fusion | flops 5242880 | bytes 16777220 | tf_op jit(solution)/shard_map/convert_element_type | solution.py:183
  434.4 4.8 collective-permute-start.14
  439.2 7.8 %fusion.20 = f32[256,1024]{1,0:T(8,128)} fusion(bf16[256,4096]{1,0:T(8,128)(2,1)} %fusion.43, bf16[1,1024,4096]{2,1,0:T(8,128)(2,1)} %param.5), kind=kOutput, calls=%fused_computation.21 | convolution fusion | flops 2147483648 | bytes 11534336 | tf_op jit(solution)/shard_map/dot_general | solution.py:209
  447.1 28.8 %collective-permute-done.16 = bf16[256,4096]{1,0:T(8,128)(2,1)} collective-permute-done((bf16[256,4096]{1,0:T(8,128)(2,1)}, bf16[256,4096]{1,0:T(8,128)(2,1)}, u32[]{:S(2)}, u32[]{:S(2)}) %collective-permute-start.16) | collective-permute-done | bytes 2097184 | tf_op jit(solution)/shard_map/ppermute | solution.py:106
  475.9 3.1 broadcast_select_fusion.1
  484.3 7.7 %fusion.16 = f32[256,1024]{1,0:T(8,128)} fusion(bf16[256,4096]{1,0:T(8,128)(2,1)} %broadcast_select_fusion.1, bf16[1,1024,4096]{2,1,0:T(8,128)(2,1)} %param.5), kind=kOutput, calls=%fused_computation.17 | convolution fusion | flops 2147483648 | bytes 11534336 | tf_op jit(solution)/shard_map/dot_general | solution.py:209
  492.2 14.0 %convolution_convert_fusion = bf16[4096,1024]{1,0:T(8,128)(2,1)} fusion(s32[]{:T(128)S(6)} %select_n.327, bf16[1024,1024]{1,0:T(8,128)(2,1)} %all-gather.5.cloned.1.call-done, bf16[256,4096]{1,0:T(8,128)(2,1)} %copy-done.11, bf16[256,4096]{1,0:T(8,128)(2,1)S(1)} %copy-done.7, bf16[256,4096]{1,0:T(8,128)(2,1)} %copy-done.10, ...), kind=kOutput, calls=%fused_computation.30 | convolution fusion | flops 8631877632 | bytes 18874372 | tf_op jit(solution)/shard_map/dot_general | solution.py:173
  506.2 7.5 %fusion.18 = f32[256,1024]{1,0:T(8,128)} fusion(bf16[256,4096]{1,0:T(8,128)(2,1)} %broadcast_select_fusion.6, bf16[1,1024,4096]{2,1,0:T(8,128)(2,1)} %param.5), kind=kOutput, calls=%fused_computation.19 | convolution fusion | flops 2147483648 | bytes 11534336 | tf_op jit(solution)/shard_map/dot_general | solution.py:209
  513.7 6.8 %collective-permute-done.17 = bf16[256,4096]{1,0:T(8,128)(2,1)} collective-permute-done((bf16[256,4096]{1,0:T(8,128)(2,1)}, bf16[256,4096]{1,0:T(8,128)(2,1)}, u32[]{:S(2)}, u32[]{:S(2)}) %collective-permute-start.17) | collective-permute-done | bytes 2097184 | tf_op jit(solution)/shard_map/ppermute | solution.py:106
  523.8 2.0 collective-permute-start.18
  527.1 2.4 add.237
  530.7 7.0 %fusion.14 = f32[256,1024]{1,0:T(8,128)} fusion(bf16[256,4096]{1,0:T(8,128)(2,1)S(1)} %add.237, bf16[1,1024,4096]{2,1,0:T(8,128)(2,1)} %param.5), kind=kOutput, calls=%fused_computation.15 | convolution fusion | flops 2147483648 | bytes 11534336 | tf_op jit(solution)/shard_map/dot_general | solution.py:209
  539.3 2.5 fusion.65
  541.8 24.4 %collective-permute-done.19 = bf16[256,4096]{1,0:T(8,128)(2,1)} collective-permute-done((bf16[256,4096]{1,0:T(8,128)(2,1)S(1)}, bf16[256,4096]{1,0:T(8,128)(2,1)}, u32[]{:S(2)}, u32[]{:S(2)}) %collective-permute-start.19) | collective-permute-done | bytes 2097184 | tf_op jit(solution)/shard_map/ppermute | solution.py:106
  566.2 7.6 %fusion.12 = f32[256,1024]{1,0:T(8,128)} fusion(bf16[1,1024,4096]{2,1,0:T(8,128)(2,1)} %param.5, bf16[256,4096]{1,0:T(8,128)(2,1)} %collective-permute-done.19, pred[]{:T(512)S(6)} %and.24, bf16[256,4096]{1,0:T(8,128)(2,1)} %collective-permute-done.18, pred[]{:T(512)S(6)} %and.27), kind=kOutput, calls=%fused_computation.13 | convolution fusion | flops 2150629376 | bytes 13631490 | tf_op jit(solution)/shard_map/dot_general | solution.py:209
  578.3 14.1 %convert_bitcast_fusion = bf16[1,1024,4096]{2,1,0:T(8,128)(2,1)} fusion(bf16[256,4096]{1,0:T(8,128)(2,1)S(1)} %fusion.61, bf16[256,4096]{1,0:T(8,128)(2,1)S(1)} %copy-done.9, bf16[256,4096]{1,0:T(8,128)(2,1)S(1)} %fusion.62, bf16[256,4096]{1,0:T(8,128)(2,1)} %fusion.43, s32[]{:T(128)S(6)} %select_n.327, bf16[1024,1024]{1,0:T(8,128)(2,1)} %all-gather.3.cloned.1.call-done), kind=kOutput, calls=%fused_computation.27 | convolution fusion | flops 8631877632 | bytes 18874372 | tf_op jit(solution)/shard_map/dot_general | solution.py:195
  592.5 13.4 %reduce-scatter.17.cloned.1.call-done = f32[256,256]{1,0:T(8,128)} async-done(((f32[256,1024]{1,0:T(8,128)}), f32[256,256]{1,0:T(8,128)}) %reduce-scatter.17.cloned.1.call-update) | async-done | bytes 262160 | tf_op jit(solution)/shard_map/reduce_scatter | solution.py:212
  (97 shorter events, 39.5 us)
Async XLA Ops:
  7.2 28.0 %all-gather.3.cloned.1.call-start = ((), (), s32[]{:S(2)}) async-start(), calls=%async_computation.6 | async-start | bytes 2621440 | tf_op jit(solution)/shard_map/all_gather | solution.py:124
  7.9 99.7 %all-gather.5.cloned.1.call-start = ((), (), s32[]{:S(2)}) async-start(), calls=%async_computation.7 | async-start | bytes 2621440 | tf_op jit(solution)/shard_map/all_gather | solution.py:126
  47.5 17.2 %collective-permute-start.1 = (bf16[256,4096]{1,0:T(8,128)(2,1)}, bf16[256,4096]{1,0:T(8,128)(2,1)S(1)}, u32[]{:S(2)}, u32[]{:S(2)}) collective-permute-start(bf16[256,4096]{1,0:T(8,128)(2,1)} %get-tuple-element.49), channel_id=1, source_target_pairs={{12,8},{13,9},{14,10},{15,11},{28,24},{29,25},{30,26},{31,27}} | collective-permute-start | bytes 6291464 | tf_op jit(solution)/shard_map/ppermute | solution.py:106
  48.3 475.4 %reduce-scatter.7.cloned.1.call-start = ((), (), s32[]{:S(2)}) async-start(), calls=%async_computation.8 | async-start | bytes 5242880 | tf_op jit(solution)/shard_map/reduce_scatter | solution.py:181
  48.4 49.0 %collective-permute-start = (bf16[256,4096]{1,0:T(8,128)(2,1)}, bf16[256,4096]{1,0:T(8,128)(2,1)S(1)}, u32[]{:S(2)}, u32[]{:S(2)}) collective-permute-start(bf16[256,4096]{1,0:T(8,128)(2,1)} %get-tuple-element.50), channel_id=1, source_target_pairs={{0,4},{1,5},{2,6},{3,7},{16,20},{17,21},{18,22},{19,23}} | collective-permute-start | bytes 6291464 | tf_op jit(solution)/shard_map/ppermute | solution.py:106
  64.7 33.0 %copy-start = (bf16[1024,4096]{1,0:T(8,128)(2,1)}, bf16[1024,4096]{1,0:T(8,128)(2,1)S(1)}, u32[]{:S(2)}) copy-start(bf16[1024,4096]{1,0:T(8,128)(2,1)S(1)} %fusion.26) | copy-start | bytes 25165828
  100.4 22.0 %collective-permute-start.3 = (bf16[256,4096]{1,0:T(8,128)(2,1)}, bf16[256,4096]{1,0:T(8,128)(2,1)}, u32[]{:S(2)}, u32[]{:S(2)}) collective-permute-start(bf16[256,4096]{1,0:T(8,128)(2,1)} %get-tuple-element.46), channel_id=1, source_target_pairs={{8,4},{12,8},{9,5},{13,9},{10,6},{14,10},{11,7},{15,11},{24,20},{2... | collective-permute-start | bytes 6291464 | tf_op jit(solution)/shard_map/ppermute | solution.py:106
  102.4 48.1 %collective-permute-start.2 = (bf16[256,4096]{1,0:T(8,128)(2,1)S(1)}, bf16[256,4096]{1,0:T(8,128)(2,1)}, u32[]{:S(2)}, u32[]{:S(2)}) collective-permute-start(bf16[256,4096]{1,0:T(8,128)(2,1)S(1)} %get-tuple-element.47), channel_id=1, source_target_pairs={{0,4},{4,8},{1,5},{5,9},{2,6},{6,10},{3,7},{7,11},{16,20},{20,24},... | collective-permute-start | bytes 6291464 | tf_op jit(solution)/shard_map/ppermute | solution.py:106
  122.4 28.4 %copy-start.1 = (bf16[1024,4096]{1,0:T(8,128)(2,1)S(1)}, bf16[1024,4096]{1,0:T(8,128)(2,1)}, u32[]{:S(2)}) copy-start(bf16[1024,4096]{1,0:T(8,128)(2,1)} %copy-done) | copy-start | bytes 25165828
  154.3 51.6 %collective-permute-start.4 = (bf16[256,4096]{1,0:T(8,128)(2,1)}, bf16[256,4096]{1,0:T(8,128)(2,1)S(1)}, u32[]{:S(2)}, u32[]{:S(2)}) collective-permute-start(bf16[256,4096]{1,0:T(8,128)(2,1)} %get-tuple-element.44), channel_id=1, source_target_pairs={{0,4},{4,8},{8,12},{1,5},{5,9},{9,13},{2,6},{6,10},{10,14},{3,7},{... | collective-permute-start | bytes 6291464 | tf_op jit(solution)/shard_map/ppermute | solution.py:106
  162.1 48.0 %collective-permute-start.5 = (bf16[256,4096]{1,0:T(8,128)(2,1)}, bf16[256,4096]{1,0:T(8,128)(2,1)}, u32[]{:S(2)}, u32[]{:S(2)}) collective-permute-start(bf16[256,4096]{1,0:T(8,128)(2,1)} %get-tuple-element.45), channel_id=1, source_target_pairs={{4,0},{8,4},{12,8},{5,1},{9,5},{13,9},{6,2},{10,6},{14,10},{7,3},{... | collective-permute-start | bytes 6291464 | tf_op jit(solution)/shard_map/ppermute | solution.py:106
  216.2 45.1 %collective-permute-start.6 = (bf16[256,4096]{1,0:T(8,128)(2,1)}, bf16[256,4096]{1,0:T(8,128)(2,1)S(1)}, u32[]{:S(2)}, u32[]{:S(2)}) collective-permute-start(bf16[256,4096]{1,0:T(8,128)(2,1)} %get-tuple-element.37), channel_id=1, source_target_pairs={{0,4},{4,8},{8,12},{1,5},{5,9},{9,13},{2,6},{6,10},{10,14},{3,7},{... | collective-permute-start | bytes 6291464 | tf_op jit(solution)/shard_map/ppermute | solution.py:106
  219.0 46.6 %collective-permute-start.8 = (bf16[256,4096]{1,0:T(8,128)(2,1)}, bf16[256,4096]{1,0:T(8,128)(2,1)}, u32[]{:S(2)}, u32[]{:S(2)}) collective-permute-start(bf16[256,4096]{1,0:T(8,128)(2,1)} %get-tuple-element.37), channel_id=1, source_target_pairs={{4,0},{8,4},{12,8},{5,1},{9,5},{13,9},{6,2},{10,6},{14,10},{7,3},{... | collective-permute-start | bytes 6291464 | tf_op jit(solution)/shard_map/ppermute | solution.py:106
  261.3 9.6 %copy-start.4 = (bf16[256,4096]{1,0:T(8,128)(2,1)}, bf16[256,4096]{1,0:T(8,128)(2,1)S(1)}, u32[]{:S(2)}) copy-start(bf16[256,4096]{1,0:T(8,128)(2,1)S(1)} %collective-permute-done.6) | copy-start | bytes 6291460
  271.0 45.5 %collective-permute-start.9 = (bf16[256,4096]{1,0:T(8,128)(2,1)}, bf16[256,4096]{1,0:T(8,128)(2,1)S(1)}, u32[]{:S(2)}, u32[]{:S(2)}) collective-permute-start(bf16[256,4096]{1,0:T(8,128)(2,1)} %get-tuple-element.42), channel_id=1, source_target_pairs={{4,0},{8,4},{12,8},{5,1},{9,5},{13,9},{6,2},{10,6},{14,10},{7,3},{... | collective-permute-start | bytes 6291464 | tf_op jit(solution)/shard_map/ppermute | solution.py:106
  272.2 45.5 %collective-permute-start.7 = (bf16[256,4096]{1,0:T(8,128)(2,1)}, bf16[256,4096]{1,0:T(8,128)(2,1)}, u32[]{:S(2)}, u32[]{:S(2)}) collective-permute-start(bf16[256,4096]{1,0:T(8,128)(2,1)} %get-tuple-element.43), channel_id=1, source_target_pairs={{4,8},{8,12},{0,4},{5,9},{9,13},{1,5},{6,10},{10,14},{2,6},{7,11},... | collective-permute-start | bytes 6291464 | tf_op jit(solution)/shard_map/ppermute | solution.py:106
  318.0 53.9 %slice-start = ((s8[8388608]{0:T(1024)(128)(4,1)}), s8[4194304]{0:T(1024)(128)(4,1)S(1)}, s32[]{:S(2)}) async-start(s8[8388608]{0:T(1024)(128)(4,1)} %bitcast.84), calls=%async_computation.14 | async-start | bytes 8388608
  318.1 53.9 %slice-start.1 = ((s8[8388608]{0:T(1024)(128)(4,1)}), s8[4194304]{0:T(1024)(128)(4,1)S(1)}, s32[]{:S(2)}) async-start(s8[8388608]{0:T(1024)(128)(4,1)} %bitcast.84), calls=%async_computation.15 | async-start | bytes 8388608
  322.0 62.6 %copy-start.6 = (bf16[256,4096]{1,0:T(8,128)(2,1)}, bf16[256,4096]{1,0:T(8,128)(2,1)S(1)}, u32[]{:S(2)}) copy-start(bf16[256,4096]{1,0:T(8,128)(2,1)S(1)} %get-tuple-element.48) | copy-start | bytes 6291460
  322.0 45.7 %collective-permute-start.10 = (bf16[256,4096]{1,0:T(8,128)(2,1)S(1)}, bf16[256,4096]{1,0:T(8,128)(2,1)S(1)}, u32[]{:S(2)}, u32[]{:S(2)}) collective-permute-start(bf16[256,4096]{1,0:T(8,128)(2,1)S(1)} %get-tuple-element.41), channel_id=1, source_target_pairs={{8,12},{0,4},{4,8},{9,13},{1,5},{5,9},{10,14},{2,6},{6,10},{11,15}... | collective-permute-start | bytes 6291464 | tf_op jit(solution)/shard_map/ppermute | solution.py:106
  328.1 43.8 %collective-permute-start.12 = (bf16[256,4096]{1,0:T(8,128)(2,1)S(1)}, bf16[256,4096]{1,0:T(8,128)(2,1)S(1)}, u32[]{:S(2)}, u32[]{:S(2)}) collective-permute-start(bf16[256,4096]{1,0:T(8,128)(2,1)S(1)} %get-tuple-element.40), channel_id=1, source_target_pairs={{4,0},{8,4},{12,8},{5,1},{9,5},{13,9},{6,2},{10,6},{14,10},{7,3},{... | collective-permute-start | bytes 6291464 | tf_op jit(solution)/shard_map/ppermute | solution.py:106
  375.1 43.2 %collective-permute-start.13 = (bf16[256,4096]{1,0:T(8,128)(2,1)}, bf16[256,4096]{1,0:T(8,128)(2,1)}, u32[]{:S(2)}, u32[]{:S(2)}) collective-permute-start(bf16[256,4096]{1,0:T(8,128)(2,1)} %get-tuple-element.38), channel_id=1, source_target_pairs={{4,0},{8,4},{12,8},{5,1},{9,5},{13,9},{6,2},{10,6},{14,10},{7,3},{... | collective-permute-start | bytes 6291464 | tf_op jit(solution)/shard_map/ppermute | solution.py:106
  376.4 8.0 %copy-start.5 = (bf16[256,4096]{1,0:T(8,128)(2,1)S(1)}, bf16[256,4096]{1,0:T(8,128)(2,1)}, u32[]{:S(2)}) copy-start(bf16[256,4096]{1,0:T(8,128)(2,1)} %copy-done.4) | copy-start | bytes 6291460
  376.4 45.8 %collective-permute-start.11 = (bf16[256,4096]{1,0:T(8,128)(2,1)S(1)}, bf16[256,4096]{1,0:T(8,128)(2,1)}, u32[]{:S(2)}, u32[]{:S(2)}) collective-permute-start(bf16[256,4096]{1,0:T(8,128)(2,1)S(1)} %get-tuple-element.39), channel_id=1, source_target_pairs={{0,4},{4,8},{8,12},{1,5},{5,9},{9,13},{2,6},{6,10},{10,14},{3,7},{... | collective-permute-start | bytes 6291464 | tf_op jit(solution)/shard_map/ppermute | solution.py:106
  384.4 1.3 copy-start.10
  384.6 1.7 copy-start.11
  424.6 167.8 %reduce-scatter.9.cloned.1.call-start = ((), (), s32[]{:S(2)}) async-start(), calls=%async_computation.9 | async-start | bytes 1310720 | tf_op jit(solution)/shard_map/reduce_scatter | solution.py:212
  433.1 42.8 %collective-permute-start.16 = (bf16[256,4096]{1,0:T(8,128)(2,1)}, bf16[256,4096]{1,0:T(8,128)(2,1)}, u32[]{:S(2)}, u32[]{:S(2)}) collective-permute-start(bf16[256,4096]{1,0:T(8,128)(2,1)} %fusion.43), channel_id=1, source_target_pairs={{4,0},{8,4},{12,8},{5,1},{9,5},{13,9},{6,2},{10,6},{14,10},{7,3},{... | collective-permute-start | bytes 6291464 | tf_op jit(solution)/shard_map/ppermute | solution.py:106
  434.4 45.9 %collective-permute-start.14 = (bf16[256,4096]{1,0:T(8,128)(2,1)}, bf16[256,4096]{1,0:T(8,128)(2,1)S(1)}, u32[]{:S(2)}, u32[]{:S(2)}) collective-permute-start(bf16[256,4096]{1,0:T(8,128)(2,1)} %fusion.43), channel_id=1, source_target_pairs={{0,4},{4,8},{8,12},{1,5},{5,9},{9,13},{2,6},{6,10},{10,14},{3,7},{... | collective-permute-start | bytes 6291464 | tf_op jit(solution)/shard_map/ppermute | solution.py:106
  447.1 145.3 %reduce-scatter.13.cloned.1.call-start = ((), (), s32[]{:S(2)}) async-start(), calls=%async_computation.11 | async-start | bytes 1310720 | tf_op jit(solution)/shard_map/reduce_scatter | solution.py:212
  479.0 41.4 %collective-permute-start.17 = (bf16[256,4096]{1,0:T(8,128)(2,1)}, bf16[256,4096]{1,0:T(8,128)(2,1)}, u32[]{:S(2)}, u32[]{:S(2)}) collective-permute-start(bf16[256,4096]{1,0:T(8,128)(2,1)} %broadcast_select_fusion.1), channel_id=1, source_target_pairs={{4,0},{8,4},{5,1},{9,5},{6,2},{10,6},{7,3},{11,7},{20,16},{24,20},... | collective-permute-start | bytes 6291464 | tf_op jit(solution)/shard_map/ppermute | solution.py:106
  480.3 1.9 copy-start.2
  482.3 39.9 %collective-permute-start.15 = (bf16[256,4096]{1,0:T(8,128)(2,1)}, bf16[256,4096]{1,0:T(8,128)(2,1)}, u32[]{:S(2)}, u32[]{:S(2)}) collective-permute-start(bf16[256,4096]{1,0:T(8,128)(2,1)} %broadcast_select_fusion.6), channel_id=1, source_target_pairs={{4,8},{8,12},{5,9},{9,13},{6,10},{10,14},{7,11},{11,15},{20,24},{2... | collective-permute-start | bytes 6291464 | tf_op jit(solution)/shard_map/ppermute | solution.py:106
  484.3 7.9 %copy-start.7 = (bf16[256,4096]{1,0:T(8,128)(2,1)S(1)}, bf16[256,4096]{1,0:T(8,128)(2,1)}, u32[]{:S(2)}) copy-start(bf16[256,4096]{1,0:T(8,128)(2,1)} %copy-done.6) | copy-start | bytes 6291460
  492.0 100.5 %reduce-scatter.11.cloned.1.call-start = ((), (), s32[]{:S(2)}) async-start(), calls=%async_computation.10 | async-start | bytes 1310720 | tf_op jit(solution)/shard_map/reduce_scatter | solution.py:212
  513.6 78.8 %reduce-scatter.15.cloned.1.call-start = ((), (), s32[]{:S(2)}) async-start(), calls=%async_computation.12 | async-start | bytes 1310720 | tf_op jit(solution)/shard_map/reduce_scatter | solution.py:212
  523.8 18.0 %collective-permute-start.18 = (bf16[256,4096]{1,0:T(8,128)(2,1)}, bf16[256,4096]{1,0:T(8,128)(2,1)}, u32[]{:S(2)}, u32[]{:S(2)}) collective-permute-start(bf16[256,4096]{1,0:T(8,128)(2,1)} %broadcast_select_fusion.8), channel_id=1, source_target_pairs={{8,12},{9,13},{10,14},{11,15},{24,28},{25,29},{26,30},{27,31}} | collective-permute-start | bytes 6291464 | tf_op jit(solution)/shard_map/ppermute | solution.py:106
  525.8 40.4 %collective-permute-start.19 = (bf16[256,4096]{1,0:T(8,128)(2,1)S(1)}, bf16[256,4096]{1,0:T(8,128)(2,1)}, u32[]{:S(2)}, u32[]{:S(2)}) collective-permute-start(bf16[256,4096]{1,0:T(8,128)(2,1)S(1)} %broadcast_select_fusion.4), channel_id=1, source_target_pairs={{4,0},{5,1},{6,2},{7,3},{20,16},{21,17},{22,18},{23,19}} | collective-permute-start | bytes 6291464 | tf_op jit(solution)/shard_map/ppermute | solution.py:106
  529.4 1.3 copy-start.8
  537.8 68.1 %reduce-scatter.17.cloned.1.call-start = ((), (), s32[]{:S(2)}) async-start(), calls=%async_computation.13 | async-start | bytes 1310720 | tf_op jit(solution)/shard_map/reduce_scatter | solution.py:212
  573.8 2.2 copy-start.3
  576.0 2.3 copy-start.9
  592.4 15.1 %copy-start.12 = (f32[256,256]{1,0:T(8,128)S(1)}, f32[256,256]{1,0:T(8,128)}, u32[]{:S(2)}) copy-start(f32[256,256]{1,0:T(8,128)} %reduce-scatter.9.cloned.1.call-done) | copy-start | bytes 786436
  592.4 15.0 %copy-start.13 = (f32[256,256]{1,0:T(8,128)S(1)}, f32[256,256]{1,0:T(8,128)}, u32[]{:S(2)}) copy-start(f32[256,256]{1,0:T(8,128)} %reduce-scatter.13.cloned.1.call-done) | copy-start | bytes 786436
  592.4 15.0 %copy-start.14 = (f32[256,256]{1,0:T(8,128)S(1)}, f32[256,256]{1,0:T(8,128)}, u32[]{:S(2)}) copy-start(f32[256,256]{1,0:T(8,128)} %reduce-scatter.11.cloned.1.call-done) | copy-start | bytes 786436
  592.5 15.0 %copy-start.15 = (f32[256,256]{1,0:T(8,128)S(1)}, f32[256,256]{1,0:T(8,128)}, u32[]{:S(2)}) copy-start(f32[256,256]{1,0:T(8,128)} %reduce-scatter.15.cloned.1.call-done) | copy-start | bytes 786436
  605.9 1.5 copy-start.16
Sparse Core Ops, SparseCore 0:
  9.6 25.5 all-gather.2
  48.4 24.6 all-gather.4
  424.7 43.8 reduce-scatter.6
  471.1 24.8 reduce-scatter.8
  498.5 24.8 reduce-scatter.12
  525.9 24.8 reduce-scatter.10
  553.4 24.8 reduce-scatter.14
  581.0 24.8 reduce-scatter.16

commit v8 on v6

--- a/solution.py
+++ b/solution.py
@@ -162,10 +162,6 @@
     slope = gelu_slope(preact)
     for step in range(1, count - 1):
         run_slot([(act_gather, step), (grad_sum, step - 1)])
-        if step == 1:
-            grad_sum.up_in, grad_sum.down_in, slope = lax.optimization_barrier(
-                (grad_sum.up_in, grad_sum.down_in, slope)
-            )
     tokens = x_rows.shape[0]
     turn = lax.axis_index("r") * (tokens // count)
     grad_turned = rotate_rows(grad_rows, turn)

time: 617 us -> 619 us (level)
    ppermute x20, waiting for transfers between devices: 290 us -> 301 us  [run_slot(): received.append(lax.ppermute(combined, 'r', pairs))]
  transfers between devices with their start and end apart: 29 -> 29, of which waited for: 17 -> 19; matrix products, arithmetic and copies ran while one was open for 25% -> 24% of each run, Pallas kernels for 0% -> 0%
where the time goes in v8:
time: 619 us; the launch traced here: 611 us
  waiting for transfers between devices  339 us (55%)
  matrix products  116 us (19%)
  starting transfers between devices  68.6 us (11%)
  other arithmetic  59.3 us (10%)
  between operations  14.8 us (2%)
  local copies, waits for them, and re-layouts  12.8 us (2%)
    ppermute x20, waiting for transfers between devices, run_slot(): received.append(lax.ppermute(combined, 'r', pairs))  301 us
    ppermute x20, starting transfers between devices, run_slot(): received.append(lax.ppermute(combined, 'r', pairs))  68.2 us
    dot_general x5, matrix products, on_device(): lax.dot_general(piece, up_tile, (((1,), (1,)), ((), ())), preferred_eleme...  37.5 us
    all_gather x1, waiting for transfers between devices, on_device(): first_rows = lax.all_gather(own_rows, 'p', axis=1, tiled=True)  19.9 us
    dot_general x1, matrix products, on_device(): lax.dot_general(grad_rows, down_tile, (((1,), (1,)), ((), ())), preferred...  14.8 us
    dot_general x1, matrix products, on_device(): jnp.dot(activation, down_tile, preferred_element_type=jnp.float32)  14.8 us
    dot_general x1, matrix products, on_device(): lax.dot_general(rotate_rows(x_rows, turn), pre_grad, (((0,), (0,)), ((),...  14.1 us
    dot_general x1, matrix products, on_device(): lax.dot_general(activation, grad_turned, (((0,), (0,)), ((), ())), prefer...  14 us
  transfers between devices with their start and end apart: 29, of which 19 were waited for; matrix products, arithmetic and copies ran while one was open for 24% of the time, Pallas kernels for 0%

profile of v8, /device:TPU:0, one launch (start us, length us, event | category | flops | bytes accessed | tf_op | source)
XLA Modules:
  0.0 610.5 jit_solution(5603125873487007700)
XLA Ops:
  9.8 19.9 %all-gather.4.cloned.1.call-done = bf16[512,1024]{1,0:T(8,128)(2,1)} async-done(((bf16[512,256]{1,0:T(8,128)(2,1)}), bf16[512,1024]{1,0:T(8,128)(2,1)}) %all-gather.4.cloned.1.call-update) | async-done | bytes 1048592 | tf_op jit(solution)/shard_map/all_gather | solution.py:144
  29.7 8.2 %fusion.34 = bf16[512,4096]{1,0:T(8,128)(2,1)S(1)} fusion(bf16[512,1024]{1,0:T(8,128)(2,1)} %all-gather.4.cloned.1.call-done, bf16[1,1024,4096]{2,1,0:T(8,128)(2,1)} %param.5), kind=kOutput, calls=%fused_computation.32 | convolution fusion | flops 4297064448 | bytes 13631488 | tf_op jit(solution)/shard_map/dot_general | solution.py:145
  37.9 2.3 fusion.93
  40.2 3.5 collective-permute-start
  45.9 8.2 %all-gather.6.cloned.1.call-done = bf16[1024,1024]{1,0:T(8,128)(2,1)} async-done(((bf16[1024,256]{1,0:T(8,128)(2,1)}), bf16[1024,1024]{1,0:T(8,128)(2,1)}) %all-gather.6.cloned.1.call-update) | async-done | bytes 2097168 | tf_op jit(solution)/shard_map/all_gather | solution.py:124
  54.1 12.8 %fusion.26 = bf16[1024,4096]{1,0:T(8,128)(2,1)S(1)} fusion(bf16[1024,1024]{1,0:T(8,128)(2,1)} %all-gather.6.cloned.1.call-done, bf16[1,1024,4096]{2,1,0:T(8,128)(2,1)} %param.5), kind=kOutput, calls=%fused_computation.28 | convolution fusion | flops 8594128896 | bytes 18874368 | tf_op jit(solution)/shard_map/dot_general | solution.py:125
  66.9 22.3 %collective-permute-done = bf16[256,4096]{1,0:T(8,128)(2,1)S(1)} collective-permute-done((bf16[256,4096]{1,0:T(8,128)(2,1)}, bf16[256,4096]{1,0:T(8,128)(2,1)S(1)}, u32[]{:S(2)}, u32[]{:S(2)}) %collective-permute-start) | collective-permute-done | bytes 2097184 | tf_op jit(solution)/shard_map/ppermute | solution.py:106
  89.8 2.8 fusion.51
  92.6 5.6 collective-permute-start.2
  98.2 2.5 collective-permute-start.3
  100.7 14.8 %fusion.29 = bf16[1024,4096]{1,0:T(8,128)(2,1)} fusion(bf16[1024,1024]{1,0:T(8,128)(2,1)} %all-gather.8.cloned.1.call-done, bf16[1,4096,1024]{2,1,0:T(8,128)(2,1)} %param.6), kind=kOutput, calls=%fused_computation.29 | convolution fusion | flops 8594128896 | bytes 18874368 | tf_op jit(solution)/shard_map/dot_general | solution.py:127
  115.6 26.1 %collective-permute-done.2 = bf16[256,4096]{1,0:T(8,128)(2,1)} collective-permute-done((bf16[256,4096]{1,0:T(8,128)(2,1)}, bf16[256,4096]{1,0:T(8,128)(2,1)}, u32[]{:S(2)}, u32[]{:S(2)}) %collective-permute-start.2) | collective-permute-done | bytes 2097184 | tf_op jit(solution)/shard_map/ppermute | solution.py:106
  142.2 2.8 copy-done.1
  145.0 3.4 fusion.50
  149.8 10.1 %collective-permute-start.4 = (bf16[256,4096]{1,0:T(8,128)(2,1)}, bf16[256,4096]{1,0:T(8,128)(2,1)}, u32[]{:S(2)}, u32[]{:S(2)}) collective-permute-start(bf16[256,4096]{1,0:T(8,128)(2,1)} %get-tuple-element.36), channel_id=1, source_target_pairs={{0,4},{4,8},{8,12},{1,5},{5,9},{9,13},{2,6},{6,10},{10,14},{3,7},{... | collective-permute-start | bytes 6291464 | tf_op jit(solution)/shard_map/ppermute | solution.py:106
  159.9 40.9 %collective-permute-done.5 = bf16[256,4096]{1,0:T(8,128)(2,1)S(1)} collective-permute-done((bf16[256,4096]{1,0:T(8,128)(2,1)}, bf16[256,4096]{1,0:T(8,128)(2,1)S(1)}, u32[]{:S(2)}, u32[]{:S(2)}) %collective-permute-start.5) | collective-permute-done | bytes 2097184 | tf_op jit(solution)/shard_map/ppermute | solution.py:106
  202.1 3.9 multiply_convert_fusion
  207.3 6.6 %collective-permute-start.6 = (bf16[256,4096]{1,0:T(8,128)(2,1)}, bf16[256,4096]{1,0:T(8,128)(2,1)}, u32[]{:S(2)}, u32[]{:S(2)}) collective-permute-start(bf16[256,4096]{1,0:T(8,128)(2,1)} %multiply_convert_fusion), channel_id=1, source_target_pairs={{0,4},{4,8},{8,12},{1,5},{5,9},{9,13},{2,6},{6,10},{10,14},{3,7},{... | collective-permute-start | bytes 6291464 | tf_op jit(solution)/shard_map/ppermute | solution.py:106
  214.0 40.0 %collective-permute-done.10 = bf16[256,4096]{1,0:T(8,128)(2,1)S(1)} collective-permute-done((bf16[256,4096]{1,0:T(8,128)(2,1)}, bf16[256,4096]{1,0:T(8,128)(2,1)S(1)}, u32[]{:S(2)}, u32[]{:S(2)}) %collective-permute-start.10) | collective-permute-done | bytes 2097184 | tf_op jit(solution)/shard_map/ppermute | solution.py:106
  255.3 4.7 bitcast_select_fusion
  261.3 7.0 %collective-permute-start.7 = (bf16[256,4096]{1,0:T(8,128)(2,1)}, bf16[256,4096]{1,0:T(8,128)(2,1)}, u32[]{:S(2)}, u32[]{:S(2)}) collective-permute-start(bf16[256,4096]{1,0:T(8,128)(2,1)} %get-tuple-element.35), channel_id=1, source_target_pairs={{4,8},{8,12},{0,4},{5,9},{9,13},{1,5},{6,10},{10,14},{2,6},{7,11},... | collective-permute-start | bytes 6291464 | tf_op jit(solution)/shard_map/ppermute | solution.py:106
  268.3 39.2 %collective-permute-done.11 = bf16[256,4096]{1,0:T(8,128)(2,1)} collective-permute-done((bf16[256,4096]{1,0:T(8,128)(2,1)}, bf16[256,4096]{1,0:T(8,128)(2,1)}, u32[]{:S(2)}, u32[]{:S(2)}) %collective-permute-start.11) | collective-permute-done | bytes 2097184 | tf_op jit(solution)/shard_map/ppermute | solution.py:106
  308.7 4.5 fusion.54
  314.5 5.1 collective-permute-start.8
  319.7 39.2 %collective-permute-done.12 = bf16[256,4096]{1,0:T(8,128)(2,1)S(1)} collective-permute-done((bf16[256,4096]{1,0:T(8,128)(2,1)S(1)}, bf16[256,4096]{1,0:T(8,128)(2,1)S(1)}, u32[]{:S(2)}, u32[]{:S(2)}) %collective-permute-start.12) | collective-permute-done | bytes 2097184 | tf_op jit(solution)/shard_map/ppermute | solution.py:106
  360.0 6.2 %fusion.44 = (bf16[256,4096]{1,0:T(8,128)(2,1)}, bf16[256,4096]{1,0:T(8,128)(2,1)}) fusion(bf16[4,256,4096]{2,1,0:T(8,128)(2,1)} %bitcast.84, s32[]{:T(128)S(6)} %min.30, bf16[256,4096]{1,0:T(8,128)(2,1)S(1)} %collective-permute-done.12, pred[]{:T(512)S(6)} %and.21, s32[]{:T(128)S(6)} %min.29, bf16[256,4096]{1,0:T(8,128)(2,1)S(1)} %collective-permute-done.8), kind=kLoop, calls=%fused_computation.46 | loop fusion | flops 10485760 | bytes 12582921 | tf_op jit(solution)/shard_map/convert_element_type | solution.py:45
  366.2 5.7 collective-permute-start.9
  375.6 14.8 %fusion.8 = f32[1024,1024]{1,0:T(8,128)} fusion(bf16[1,4096,1024]{2,1,0:T(8,128)(2,1)} %param.6, bf16[256,4096]{1,0:T(8,128)(2,1)S(1)} %select_add_fusion, bf16[256,4096]{1,0:T(8,128)(2,1)S(1)} %get-tuple-element.40, bf16[256,4096]{1,0:T(8,128)(2,1)S(1)} %select_add_fusion.1, bf16[256,4096]{1,0:T(8,128)(2,1)} %multiply_convert_fusion), kind=kOutput, calls=%fused_computation.9 | convolution fusion | flops 8623489024 | bytes 20971520 | tf_op jit(solution)/shard_map/dot_general | solution.py:169
  390.4 20.1 %collective-permute-done.9 = bf16[256,4096]{1,0:T(8,128)(2,1)} collective-permute-done((bf16[256,4096]{1,0:T(8,128)(2,1)}, bf16[256,4096]{1,0:T(8,128)(2,1)}, u32[]{:S(2)}, u32[]{:S(2)}) %collective-permute-start.9) | collective-permute-done | bytes 2097184 | tf_op jit(solution)/shard_map/ppermute | solution.py:106
  410.5 2.3 select_convert_fusion.1
  412.8 3.1 collective-permute-done.13
  415.9 3.9 select_convert_fusion
  421.4 8.2 %fusion.42 = bf16[256,4096]{1,0:T(8,128)(2,1)} fusion(f32[256,4096]{1,0:T(8,128)} %select_convert_fusion, f32[256,4096]{1,0:T(8,128)} %select_convert_fusion.1, bf16[4,256,4096]{2,1,0:T(8,128)(2,1)} %bitcast.85, s32[]{:T(128)S(6)} %select_n.303, bf16[256,4096]{1,0:T(8,128)(2,1)S(1)} %copy-done.5, pred[]{:T(512)S(6)} %and.26, ...), kind=kLoop, calls=%fused_computation.38 | loop fusion | flops 20971520 | bytes 18874374 | tf_op jit(solution)/shard_map/convert_element_type | solution.py:180
  429.6 5.1 collective-permute-start.14
  436.0 8.1 %fusion.20 = f32[256,1024]{1,0:T(8,128)} fusion(bf16[256,4096]{1,0:T(8,128)(2,1)} %fusion.42, bf16[1,1024,4096]{2,1,0:T(8,128)(2,1)} %param.5), kind=kOutput, calls=%fused_computation.21 | convolution fusion | flops 2147483648 | bytes 11534336 | tf_op jit(solution)/shard_map/dot_general | solution.py:206
  444.1 26.8 %collective-permute-done.14 = bf16[256,4096]{1,0:T(8,128)(2,1)} collective-permute-done((bf16[256,4096]{1,0:T(8,128)(2,1)}, bf16[256,4096]{1,0:T(8,128)(2,1)}, u32[]{:S(2)}, u32[]{:S(2)}) %collective-permute-start.14) | collective-permute-done | bytes 2097184 | tf_op jit(solution)/shard_map/ppermute | solution.py:106
  479.8 7.7 %fusion.16 = f32[256,1024]{1,0:T(8,128)} fusion(bf16[256,4096]{1,0:T(8,128)(2,1)} %broadcast_select_fusion.1, bf16[1,1024,4096]{2,1,0:T(8,128)(2,1)} %param.5), kind=kOutput, calls=%fused_computation.17 | convolution fusion | flops 2147483648 | bytes 11534336 | tf_op jit(solution)/shard_map/dot_general | solution.py:206
  487.6 14.0 %convolution_convert_fusion = bf16[4096,1024]{1,0:T(8,128)(2,1)} fusion(s32[]{:T(128)S(6)} %select_n.327, bf16[1024,1024]{1,0:T(8,128)(2,1)} %all-gather.8.cloned.1.call-done, bf16[256,4096]{1,0:T(8,128)(2,1)S(1)} %copy-done.9, bf16[256,4096]{1,0:T(8,128)(2,1)} %copy-done.11, bf16[256,4096]{1,0:T(8,128)(2,1)} %copy-done.10, ...), kind=kOutput, calls=%fused_computation.30 | convolution fusion | flops 8631877632 | bytes 18874372 | tf_op jit(solution)/shard_map/dot_general | solution.py:170
  501.6 7.4 %fusion.18 = f32[256,1024]{1,0:T(8,128)} fusion(bf16[256,4096]{1,0:T(8,128)(2,1)} %broadcast_select_fusion.6, bf16[1,1024,4096]{2,1,0:T(8,128)(2,1)} %param.5), kind=kOutput, calls=%fused_computation.19 | convolution fusion | flops 2147483648 | bytes 11534336 | tf_op jit(solution)/shard_map/dot_general | solution.py:206
  509.3 15.5 %collective-permute-done.17 = bf16[256,4096]{1,0:T(8,128)(2,1)} collective-permute-done((bf16[256,4096]{1,0:T(8,128)(2,1)}, bf16[256,4096]{1,0:T(8,128)(2,1)}, u32[]{:S(2)}, u32[]{:S(2)}) %collective-permute-start.17) | collective-permute-done | bytes 2097184 | tf_op jit(solution)/shard_map/ppermute | solution.py:106
  524.7 3.1 broadcast_select_fusion.4
  531.3 2.4 add.237
  535.0 6.9 %fusion.14 = f32[256,1024]{1,0:T(8,128)} fusion(bf16[256,4096]{1,0:T(8,128)(2,1)S(1)} %add.237, bf16[1,1024,4096]{2,1,0:T(8,128)(2,1)} %param.5), kind=kOutput, calls=%fused_computation.15 | convolution fusion | flops 2147483648 | bytes 11534336 | tf_op jit(solution)/shard_map/dot_general | solution.py:206
  543.2 2.5 fusion.65
  545.7 20.9 %collective-permute-done.19 = bf16[256,4096]{1,0:T(8,128)(2,1)} collective-permute-done((bf16[256,4096]{1,0:T(8,128)(2,1)}, bf16[256,4096]{1,0:T(8,128)(2,1)}, u32[]{:S(2)}, u32[]{:S(2)}) %collective-permute-start.19) | collective-permute-done | bytes 2097184 | tf_op jit(solution)/shard_map/ppermute | solution.py:106
  566.7 7.4 %fusion.12 = f32[256,1024]{1,0:T(8,128)} fusion(bf16[1,1024,4096]{2,1,0:T(8,128)(2,1)} %param.5, bf16[256,4096]{1,0:T(8,128)(2,1)} %collective-permute-done.19, pred[]{:T(512)S(6)} %and.24, bf16[256,4096]{1,0:T(8,128)(2,1)} %collective-permute-done.18, pred[]{:T(512)S(6)} %and.27), kind=kOutput, calls=%fused_computation.13 | convolution fusion | flops 2150629376 | bytes 13631490 | tf_op jit(solution)/shard_map/dot_general | solution.py:206
  577.9 14.1 %convert_bitcast_fusion = bf16[1,1024,4096]{2,1,0:T(8,128)(2,1)} fusion(bf16[256,4096]{1,0:T(8,128)(2,1)S(1)} %fusion.61, bf16[256,4096]{1,0:T(8,128)(2,1)S(1)} %copy-done.7, bf16[256,4096]{1,0:T(8,128)(2,1)S(1)} %fusion.62, bf16[256,4096]{1,0:T(8,128)(2,1)} %fusion.42, s32[]{:T(128)S(6)} %select_n.327, bf16[1024,1024]{1,0:T(8,128)(2,1)} %all-gather.6.cloned.1.call-done), kind=kOutput, calls=%fused_computation.27 | convolution fusion | flops 8631877632 | bytes 18874372 | tf_op jit(solution)/shard_map/dot_general | solution.py:192
  592.1 8.9 %reduce-scatter.17.cloned.1.call-done = f32[256,256]{1,0:T(8,128)} async-done(((f32[256,1024]{1,0:T(8,128)}), f32[256,256]{1,0:T(8,128)}) %reduce-scatter.17.cloned.1.call-update) | async-done | bytes 262160 | tf_op jit(solution)/shard_map/reduce_scatter | solution.py:209
  (94 shorter events, 44.1 us)
Async XLA Ops:
  7.2 22.5 %all-gather.4.cloned.1.call-start = ((), (), s32[]{:S(2)}) async-start(), calls=%async_computation.6 | async-start | bytes 1310720 | tf_op jit(solution)/shard_map/all_gather | solution.py:144
  9.0 45.2 %all-gather.6.cloned.1.call-start = ((), (), s32[]{:S(2)}) async-start(), calls=%async_computation.7 | async-start | bytes 2621440 | tf_op jit(solution)/shard_map/all_gather | solution.py:124
  9.7 91.0 %all-gather.8.cloned.1.call-start = ((), (), s32[]{:S(2)}) async-start(), calls=%async_computation.8 | async-start | bytes 2621440 | tf_op jit(solution)/shard_map/all_gather | solution.py:126
  40.2 49.0 %collective-permute-start = (bf16[256,4096]{1,0:T(8,128)(2,1)}, bf16[256,4096]{1,0:T(8,128)(2,1)S(1)}, u32[]{:S(2)}, u32[]{:S(2)}) collective-permute-start(bf16[256,4096]{1,0:T(8,128)(2,1)} %get-tuple-element.42), channel_id=1, source_target_pairs={{0,4},{1,5},{2,6},{3,7},{16,20},{17,21},{18,22},{19,23}} | collective-permute-start | bytes 6291464 | tf_op jit(solution)/shard_map/ppermute | solution.py:106
  43.8 484.0 %reduce-scatter.7.cloned.1.call-start = ((), (), s32[]{:S(2)}) async-start(), calls=%async_computation.9 | async-start | bytes 5242880 | tf_op jit(solution)/shard_map/reduce_scatter | solution.py:178
  43.9 45.7 %collective-permute-start.1 = (bf16[256,4096]{1,0:T(8,128)(2,1)}, bf16[256,4096]{1,0:T(8,128)(2,1)}, u32[]{:S(2)}, u32[]{:S(2)}) collective-permute-start(bf16[256,4096]{1,0:T(8,128)(2,1)} %get-tuple-element.41), channel_id=1, source_target_pairs={{12,8},{13,9},{14,10},{15,11},{28,24},{29,25},{30,26},{31,27}} | collective-permute-start | bytes 6291464 | tf_op jit(solution)/shard_map/ppermute | solution.py:106
  66.9 22.9 %copy-start = (bf16[1024,4096]{1,0:T(8,128)(2,1)}, bf16[1024,4096]{1,0:T(8,128)(2,1)S(1)}, u32[]{:S(2)}) copy-start(bf16[1024,4096]{1,0:T(8,128)(2,1)S(1)} %fusion.26) | copy-start | bytes 25165828
  92.6 49.1 %collective-permute-start.2 = (bf16[256,4096]{1,0:T(8,128)(2,1)}, bf16[256,4096]{1,0:T(8,128)(2,1)}, u32[]{:S(2)}, u32[]{:S(2)}) collective-permute-start(bf16[256,4096]{1,0:T(8,128)(2,1)} %get-tuple-element.39), channel_id=1, source_target_pairs={{0,4},{4,8},{1,5},{5,9},{2,6},{6,10},{3,7},{7,11},{16,20},{20,24},... | collective-permute-start | bytes 6291464 | tf_op jit(solution)/shard_map/ppermute | solution.py:106
  98.2 43.7 %collective-permute-start.3 = (bf16[256,4096]{1,0:T(8,128)(2,1)S(1)}, bf16[256,4096]{1,0:T(8,128)(2,1)}, u32[]{:S(2)}, u32[]{:S(2)}) collective-permute-start(bf16[256,4096]{1,0:T(8,128)(2,1)S(1)} %get-tuple-element.38), channel_id=1, source_target_pairs={{8,4},{12,8},{9,5},{13,9},{10,6},{14,10},{11,7},{15,11},{24,20},{2... | collective-permute-start | bytes 6291464 | tf_op jit(solution)/shard_map/ppermute | solution.py:106
  141.6 3.4 copy-start.1
  148.5 52.3 %collective-permute-start.5 = (bf16[256,4096]{1,0:T(8,128)(2,1)}, bf16[256,4096]{1,0:T(8,128)(2,1)S(1)}, u32[]{:S(2)}, u32[]{:S(2)}) collective-permute-start(bf16[256,4096]{1,0:T(8,128)(2,1)} %get-tuple-element.37), channel_id=1, source_target_pairs={{4,0},{8,4},{12,8},{5,1},{9,5},{13,9},{6,2},{10,6},{14,10},{7,3},{... | collective-permute-start | bytes 6291464 | tf_op jit(solution)/shard_map/ppermute | solution.py:106
  149.8 52.3 %collective-permute-start.4 = (bf16[256,4096]{1,0:T(8,128)(2,1)}, bf16[256,4096]{1,0:T(8,128)(2,1)}, u32[]{:S(2)}, u32[]{:S(2)}) collective-permute-start(bf16[256,4096]{1,0:T(8,128)(2,1)} %get-tuple-element.36), channel_id=1, source_target_pairs={{0,4},{4,8},{8,12},{1,5},{5,9},{9,13},{2,6},{6,10},{10,14},{3,7},{... | collective-permute-start | bytes 6291464 | tf_op jit(solution)/shard_map/ppermute | solution.py:106
  200.8 1.4 copy-start.4
  206.1 47.9 %collective-permute-start.10 = (bf16[256,4096]{1,0:T(8,128)(2,1)}, bf16[256,4096]{1,0:T(8,128)(2,1)S(1)}, u32[]{:S(2)}, u32[]{:S(2)}) collective-permute-start(bf16[256,4096]{1,0:T(8,128)(2,1)} %multiply_convert_fusion), channel_id=1, source_target_pairs={{4,0},{8,4},{12,8},{5,1},{9,5},{13,9},{6,2},{10,6},{14,10},{7,3},{... | collective-permute-start | bytes 6291464 | tf_op jit(solution)/shard_map/ppermute | solution.py:106
  207.3 47.9 %collective-permute-start.6 = (bf16[256,4096]{1,0:T(8,128)(2,1)}, bf16[256,4096]{1,0:T(8,128)(2,1)}, u32[]{:S(2)}, u32[]{:S(2)}) collective-permute-start(bf16[256,4096]{1,0:T(8,128)(2,1)} %multiply_convert_fusion), channel_id=1, source_target_pairs={{0,4},{4,8},{8,12},{1,5},{5,9},{9,13},{2,6},{6,10},{10,14},{3,7},{... | collective-permute-start | bytes 6291464 | tf_op jit(solution)/shard_map/ppermute | solution.py:106
  260.0 47.5 %collective-permute-start.11 = (bf16[256,4096]{1,0:T(8,128)(2,1)}, bf16[256,4096]{1,0:T(8,128)(2,1)}, u32[]{:S(2)}, u32[]{:S(2)}) collective-permute-start(bf16[256,4096]{1,0:T(8,128)(2,1)} %get-tuple-element.34), channel_id=1, source_target_pairs={{4,0},{8,4},{12,8},{5,1},{9,5},{13,9},{6,2},{10,6},{14,10},{7,3},{... | collective-permute-start | bytes 6291464 | tf_op jit(solution)/shard_map/ppermute | solution.py:106
  261.3 47.4 %collective-permute-start.7 = (bf16[256,4096]{1,0:T(8,128)(2,1)}, bf16[256,4096]{1,0:T(8,128)(2,1)}, u32[]{:S(2)}, u32[]{:S(2)}) collective-permute-start(bf16[256,4096]{1,0:T(8,128)(2,1)} %get-tuple-element.35), channel_id=1, source_target_pairs={{4,8},{8,12},{0,4},{5,9},{9,13},{1,5},{6,10},{10,14},{2,6},{7,11},... | collective-permute-start | bytes 6291464 | tf_op jit(solution)/shard_map/ppermute | solution.py:106
  313.2 60.7 %copy-start.11 = (bf16[256,4096]{1,0:T(8,128)(2,1)}, bf16[256,4096]{1,0:T(8,128)(2,1)S(1)}, u32[]{:S(2)}) copy-start(bf16[256,4096]{1,0:T(8,128)(2,1)S(1)} %get-tuple-element.40) | copy-start | bytes 6291460
  313.2 45.6 %collective-permute-start.12 = (bf16[256,4096]{1,0:T(8,128)(2,1)S(1)}, bf16[256,4096]{1,0:T(8,128)(2,1)S(1)}, u32[]{:S(2)}, u32[]{:S(2)}) collective-permute-start(bf16[256,4096]{1,0:T(8,128)(2,1)S(1)} %get-tuple-element.32), channel_id=1, source_target_pairs={{4,0},{8,4},{12,8},{5,1},{9,5},{13,9},{6,2},{10,6},{14,10},{7,3},{... | collective-permute-start | bytes 6291464 | tf_op jit(solution)/shard_map/ppermute | solution.py:106
  314.5 45.5 %collective-permute-start.8 = (bf16[256,4096]{1,0:T(8,128)(2,1)S(1)}, bf16[256,4096]{1,0:T(8,128)(2,1)S(1)}, u32[]{:S(2)}, u32[]{:S(2)}) collective-permute-start(bf16[256,4096]{1,0:T(8,128)(2,1)S(1)} %get-tuple-element.33), channel_id=1, source_target_pairs={{8,12},{0,4},{4,8},{9,13},{1,5},{5,9},{10,14},{2,6},{6,10},{11,15}... | collective-permute-start | bytes 6291464 | tf_op jit(solution)/shard_map/ppermute | solution.py:106
  366.2 44.3 %collective-permute-start.9 = (bf16[256,4096]{1,0:T(8,128)(2,1)}, bf16[256,4096]{1,0:T(8,128)(2,1)}, u32[]{:S(2)}, u32[]{:S(2)}) collective-permute-start(bf16[256,4096]{1,0:T(8,128)(2,1)} %get-tuple-element.31), channel_id=1, source_target_pairs={{0,4},{4,8},{8,12},{1,5},{5,9},{9,13},{2,6},{6,10},{10,14},{3,7},{... | collective-permute-start | bytes 6291464 | tf_op jit(solution)/shard_map/ppermute | solution.py:106
  371.9 44.0 %collective-permute-start.13 = (bf16[256,4096]{1,0:T(8,128)(2,1)}, bf16[256,4096]{1,0:T(8,128)(2,1)}, u32[]{:S(2)}, u32[]{:S(2)}) collective-permute-start(bf16[256,4096]{1,0:T(8,128)(2,1)} %get-tuple-element.30), channel_id=1, source_target_pairs={{4,0},{8,4},{12,8},{5,1},{9,5},{13,9},{6,2},{10,6},{14,10},{7,3},{... | collective-permute-start | bytes 6291464 | tf_op jit(solution)/shard_map/ppermute | solution.py:106
  373.6 1.4 copy-start.8
  373.9 1.7 copy-start.10
  419.8 1.6 copy-start.5
  419.9 172.1 %reduce-scatter.9.cloned.1.call-start = ((), (), s32[]{:S(2)}) async-start(), calls=%async_computation.10 | async-start | bytes 1310720 | tf_op jit(solution)/shard_map/reduce_scatter | solution.py:209
  429.6 41.4 %collective-permute-start.14 = (bf16[256,4096]{1,0:T(8,128)(2,1)}, bf16[256,4096]{1,0:T(8,128)(2,1)}, u32[]{:S(2)}, u32[]{:S(2)}) collective-permute-start(bf16[256,4096]{1,0:T(8,128)(2,1)} %fusion.42), channel_id=1, source_target_pairs={{0,4},{4,8},{8,12},{1,5},{5,9},{9,13},{2,6},{6,10},{10,14},{3,7},{... | collective-permute-start | bytes 6291464 | tf_op jit(solution)/shard_map/ppermute | solution.py:106
  434.7 41.6 %collective-permute-start.16 = (bf16[256,4096]{1,0:T(8,128)(2,1)}, bf16[256,4096]{1,0:T(8,128)(2,1)S(1)}, u32[]{:S(2)}, u32[]{:S(2)}) collective-permute-start(bf16[256,4096]{1,0:T(8,128)(2,1)} %fusion.42), channel_id=1, source_target_pairs={{4,0},{8,4},{12,8},{5,1},{9,5},{13,9},{6,2},{10,6},{14,10},{7,3},{... | collective-permute-start | bytes 6291464 | tf_op jit(solution)/shard_map/ppermute | solution.py:106
  444.0 147.9 %reduce-scatter.13.cloned.1.call-start = ((), (), s32[]{:S(2)}) async-start(), calls=%async_computation.12 | async-start | bytes 1310720 | tf_op jit(solution)/shard_map/reduce_scatter | solution.py:209
  472.5 36.6 %collective-permute-start.15 = (bf16[256,4096]{1,0:T(8,128)(2,1)}, bf16[256,4096]{1,0:T(8,128)(2,1)}, u32[]{:S(2)}, u32[]{:S(2)}) collective-permute-start(bf16[256,4096]{1,0:T(8,128)(2,1)} %broadcast_select_fusion.6), channel_id=1, source_target_pairs={{4,8},{8,12},{5,9},{9,13},{6,10},{10,14},{7,11},{11,15},{20,24},{2... | collective-permute-start | bytes 6291464 | tf_op jit(solution)/shard_map/ppermute | solution.py:106
  476.3 2.0 copy-start.2
  478.3 46.4 %collective-permute-start.17 = (bf16[256,4096]{1,0:T(8,128)(2,1)}, bf16[256,4096]{1,0:T(8,128)(2,1)}, u32[]{:S(2)}, u32[]{:S(2)}) collective-permute-start(bf16[256,4096]{1,0:T(8,128)(2,1)} %broadcast_select_fusion.1), channel_id=1, source_target_pairs={{4,0},{8,4},{5,1},{9,5},{6,2},{10,6},{7,3},{11,7},{20,16},{24,20},... | collective-permute-start | bytes 6291464 | tf_op jit(solution)/shard_map/ppermute | solution.py:106
  479.8 7.8 %copy-start.9 = (bf16[256,4096]{1,0:T(8,128)(2,1)S(1)}, bf16[256,4096]{1,0:T(8,128)(2,1)}, u32[]{:S(2)}) copy-start(bf16[256,4096]{1,0:T(8,128)(2,1)} %copy-done.8) | copy-start | bytes 6291460
  487.6 104.5 %reduce-scatter.11.cloned.1.call-start = ((), (), s32[]{:S(2)}) async-start(), calls=%async_computation.11 | async-start | bytes 1310720 | tf_op jit(solution)/shard_map/reduce_scatter | solution.py:209
  509.0 83.0 %reduce-scatter.15.cloned.1.call-start = ((), (), s32[]{:S(2)}) async-start(), calls=%async_computation.13 | async-start | bytes 1310720 | tf_op jit(solution)/shard_map/reduce_scatter | solution.py:209
  527.8 38.9 %collective-permute-start.19 = (bf16[256,4096]{1,0:T(8,128)(2,1)}, bf16[256,4096]{1,0:T(8,128)(2,1)}, u32[]{:S(2)}, u32[]{:S(2)}) collective-permute-start(bf16[256,4096]{1,0:T(8,128)(2,1)} %broadcast_select_fusion.4), channel_id=1, source_target_pairs={{4,0},{5,1},{6,2},{7,3},{20,16},{21,17},{22,18},{23,19}} | collective-permute-start | bytes 6291464 | tf_op jit(solution)/shard_map/ppermute | solution.py:106
  529.1 37.6 %collective-permute-start.18 = (bf16[256,4096]{1,0:T(8,128)(2,1)S(1)}, bf16[256,4096]{1,0:T(8,128)(2,1)}, u32[]{:S(2)}, u32[]{:S(2)}) collective-permute-start(bf16[256,4096]{1,0:T(8,128)(2,1)S(1)} %broadcast_select_fusion.8), channel_id=1, source_target_pairs={{8,12},{9,13},{10,14},{11,15},{24,28},{25,29},{26,30},{27,31}} | collective-permute-start | bytes 6291464 | tf_op jit(solution)/shard_map/ppermute | solution.py:106
  533.7 1.3 copy-start.6
  542.0 59.0 %reduce-scatter.17.cloned.1.call-start = ((), (), s32[]{:S(2)}) async-start(), calls=%async_computation.14 | async-start | bytes 1310720 | tf_op jit(solution)/shard_map/reduce_scatter | solution.py:209
  574.1 2.2 copy-start.3
  576.3 1.6 copy-start.7
  592.0 10.5 %copy-start.12 = (f32[256,256]{1,0:T(8,128)S(1)}, f32[256,256]{1,0:T(8,128)}, u32[]{:S(2)}) copy-start(f32[256,256]{1,0:T(8,128)} %reduce-scatter.9.cloned.1.call-done) | copy-start | bytes 786436
  592.0 10.5 %copy-start.13 = (f32[256,256]{1,0:T(8,128)S(1)}, f32[256,256]{1,0:T(8,128)}, u32[]{:S(2)}) copy-start(f32[256,256]{1,0:T(8,128)} %reduce-scatter.13.cloned.1.call-done) | copy-start | bytes 786436
  592.0 10.5 %copy-start.14 = (f32[256,256]{1,0:T(8,128)S(1)}, f32[256,256]{1,0:T(8,128)}, u32[]{:S(2)}) copy-start(f32[256,256]{1,0:T(8,128)} %reduce-scatter.11.cloned.1.call-done) | copy-start | bytes 786436
  592.1 10.4 %copy-start.15 = (f32[256,256]{1,0:T(8,128)S(1)}, f32[256,256]{1,0:T(8,128)}, u32[]{:S(2)}) copy-start(f32[256,256]{1,0:T(8,128)} %reduce-scatter.15.cloned.1.call-done) | copy-start | bytes 786436
  601.0 1.5 copy-start.16
Sparse Core Ops, SparseCore 0:
  10.1 19.5 all-gather.3
  31.3 22.8 all-gather.5
  55.7 22.8 all-gather.7
  420.0 43.0 reduce-scatter.6
  465.6 24.8 reduce-scatter.8
  492.9 25.3 reduce-scatter.12
  521.0 24.8 reduce-scatter.10
  548.4 24.8 reduce-scatter.14
  576.0 24.8 reduce-scatter.16
